TPU v7x, 256 devices: a whole 4x4x8 slice. The times are simulated.
256 devices in a mesh: dp: 32 (over x, z_hi, y), owner: 8 (over z_lo, core).
Axes of the slice: x: 4, y: 4, z: 8 (z_hi: 2, z_lo: 4; z = z_hi * 4 + z_lo), core: 2. Of those that a mesh axis runs over, the one named last changes fastest.
Arguments:
- line_columns: bfloat16 [8, 131072, 512], P(None, ('dp', 'owner')), may hold values from -12 to 12
- line_widths: int32 [256, 4], P(('dp', 'owner')), may hold values from 1 to 128, as said below
- layer_owner: int32 [8], replicated, may hold values from 0 to 7, each once
Outputs:
- preconditioned: float32 [8, 1152, 128], replicated
Inputs may be any that keep to these rules, and one draw needn't show every extreme that they name: `line_widths`: row b holds the widths of the 4 lines of device b, laid end to end from its first position; in every draw the lines of some device all have width 128.
All inputs are finite; a program needn't handle non-finite values.
Results may differ from a plain program's by a relative error of at most 0.0003.
Values may be sent and summed in bfloat16 or wider, within the bound.
No kernel may reach another device: no remote copies, remote signals or barrier semaphores. Data moves between devices by JAX's collectives and lax.ppermute only.
A program may use at most 128 MiB of HBM per device.

v0:
```python
import jax
import jax.numpy as jnp
from jax import lax
from jax.sharding import PartitionSpec as P

damping = 0.1


def patch_columns(block, widths):
    positions = block.shape[-2]
    channels = block.shape[-1] // 4
    line_ends = jnp.cumsum(widths, axis=-1).astype(jnp.int32)
    line_starts = line_ends - widths
    place = jnp.arange(positions, dtype=jnp.int32)[:, None]
    opening = jnp.any(place == line_starts[..., None, :], axis=-1)[..., None]
    closing = jnp.any(place + 1 == line_ends[..., None, :], axis=-1)[..., None]
    inside = place < line_ends[..., None, -1:]
    features = block[..., : 3 * channels]
    gradients = block[..., 3 * channels :]
    padding = jnp.zeros_like(features[..., :1, :])
    before = jnp.concatenate([padding, features[..., :-1, :]], axis=-2)
    after = jnp.concatenate([features[..., 1:, :], padding], axis=-2)
    before = jnp.where(opening, jnp.zeros_like(before), before)
    after = jnp.where(closing, jnp.zeros_like(after), after)
    stacked = jnp.concatenate([before, features, after, gradients], axis=-1)
    return jnp.where(inside, stacked, jnp.zeros_like(stacked))


def precondition(factor, total_rows):
    full_width = factor.shape[0]
    patch_width = full_width // 10 * 9
    scaled = factor / total_rows
    act_factor = scaled[:patch_width, :patch_width] + damping * jnp.eye(
        patch_width, dtype=factor.dtype
    )
    grad_factor = scaled[patch_width:, patch_width:] + damping * jnp.eye(
        full_width - patch_width, dtype=factor.dtype
    )
    cross_term = scaled[:patch_width, patch_width:]
    act_cholesky = jnp.linalg.cholesky(act_factor)
    left_solved = jax.scipy.linalg.cho_solve((act_cholesky, True), cross_term)
    grad_cholesky = jnp.linalg.cholesky(grad_factor)
    return jax.scipy.linalg.cho_solve((grad_cholesky, True), left_solved.T).T


def body(line_columns, line_widths, layer_owner):
    layer_count, positions, packed_width = line_columns.shape
    channels = packed_width // 4
    full_width = 10 * channels
    n_replicas = lax.axis_size("dp")
    n_owners = lax.axis_size("owner")
    per_owner = layer_count // n_owners
    total_rows = n_replicas * n_owners * positions
    ordered = jnp.take(line_columns, layer_owner, axis=0)
    width_copies = jnp.broadcast_to(line_widths[None, :, :], (n_owners, 1, line_widths.shape[1]))
    received, source_widths = (
        lax.all_to_all(ordered, "owner", split_axis=0, concat_axis=1, tiled=True),
        lax.all_to_all(width_copies, "owner", split_axis=0, concat_axis=1, tiled=True),
    )
    blocks = received.reshape(per_owner, n_owners, positions, packed_width)
    columns = patch_columns(blocks, source_widths.reshape(n_owners, line_widths.shape[1]))
    columns = columns.reshape(per_owner, n_owners * positions, full_width)
    row_sums = lax.psum_scatter(
        jnp.einsum("lpr,lpb->rlb", columns, columns, preferred_element_type=jnp.float32),
        "dp",
        scatter_dimension=0,
        tiled=True,
    )
    gathered = lax.all_gather(row_sums, "dp", axis=0, tiled=True)
    factors = [gathered[:, 0, :]]
    results = jnp.stack([precondition(factor, total_rows) for factor in factors])
    return lax.all_gather(results, "owner", axis=0, tiled=True)


def solution(mesh):
    in_specs = (P(None, ("dp", "owner"), None), P(("dp", "owner"), None), P())
    out_specs = P()
    return jax.shard_map(body, mesh=mesh, in_specs=in_specs, out_specs=out_specs, check_vma=False)
```

profile of v0, /device:TPU:2, one launch (start us, length us, event | category | flops | bytes accessed | tf_op | source)
XLA Modules:
  0.0 1300.3 jit_solution(9094154907228109679)
XLA Ops:
  7.8 5.9 all-to-all-start
  15.0 5.0 gather_fusion
  20.0 4.7 broadcast_select_fusion
  24.7 5.1 all-to-all-start.1
  30.2 93.7 %all-to-all-done.1 = bf16[8,512,512]{2,1,0:T(8,128)(2,1)} async-done(((bf16[8,512,512]{2,1,0:T(8,128)(2,1)}), bf16[8,512,512]{2,1,0:T(8,128)(2,1)}, u32[]{:S(2)}, u32[]{:S(2)}) %all-to-all-start.1) | async-done | bytes 4194336 | tf_op jit(solution)/shard_map/all_to_all | solution.py:57
  123.9 3.9 fusion.136
  131.3 2.7 pad_select_fusion
  134.1 18.3 %fusion.8 = f32[1280,1,1280]{0,2,1:T(8,128)} fusion(bf16[4096,128]{1,0:T(8,128)(2,1)S(1)} %bitcast.185, bf16[4096,384]{1,0:T(8,128)(2,1)S(1)} %bitcast.183, bf16[4096,384]{1,0:T(8,128)(2,1)S(1)} %bitcast.182, bf16[4096,384]{1,0:T(8,128)(2,1)S(1)} %bitcast.184, pred[4096]{0:T(1024)(128)(4,1)S(1)} %bitcast.187), kind=kOutput, calls=%fused_computation.12 | convolution fusion | flops 13468958720 | bytes 17043456 | tf_op jit(solution)/shard_map/lpr,lpb->rlb/dot_general | solution.py:64
  152.4 14.2 %copy.112 = f32[1280,1,1280]{2,1,0:T(1,128)} copy(f32[1280,1,1280]{0,2,1:T(8,128)} %fusion.8) | data formatting | bytes 13107200 | tf_op jit(solution)/shard_map/lpr,lpb->rlb/transpose | solution.py:64
  168.5 462.1 %all-reduce.6.cloned.1.call-done = f32[1280,1,1280]{2,1,0:T(1,128)} async-done(((f32[1280,1,1280]{2,1,0:T(1,128)}), f32[1280,1,1280]{2,1,0:T(1,128)}) %all-reduce.6.cloned.1.call-update) | async-done | bytes 6553616
  632.4 152.1 %all-gather.4.cloned.1.call-done = f32[1280,1,1280]{2,1,0:T(1,128)} async-done(((f32[40,1,1280]{2,1,0:T(1,128)}), f32[1280,1,1280]{2,1,0:T(1,128)}) %all-gather.4.cloned.1.call-update) | async-done | bytes 6553616 | tf_op jit(solution)/shard_map/all_gather | solution.py:69
  784.4 14.2 %copy.113 = f32[1280,1,1280]{0,2,1:T(8,128)} copy(f32[1280,1,1280]{2,1,0:T(1,128)} %all-gather.4.cloned.1.call-done) | data formatting | bytes 13107200 | tf_op jit(solution)/shard_map/all_gather | solution.py:69
  798.7 3.3 multiply_bitcast_fusion
  802.0 2.7 copy-done
  804.7 2.7 slice_add_fusion
  807.4 6.9 copy.119
  814.3 4.6 fusion.9
  821.3 11.7 cholesky.228
  833.4 9.8 custom-call.85
  847.5 2.6 cholesky.254
  850.1 12.1 cholesky.247
  865.2 9.8 custom-call.86
  876.4 3.0 convolution_subtract_fusion.1
  879.4 11.7 cholesky.464
  892.6 9.8 custom-call.87
  903.8 3.7 convolution_subtract_fusion.2
  907.5 11.7 cholesky.483
  920.8 9.8 custom-call.88
  931.8 3.7 fusion.15
  935.5 11.9 cholesky.502
  949.0 9.8 custom-call.89
  960.0 3.8 fusion.21
  963.8 11.7 cholesky.522
  977.0 10.2 custom-call.90
  988.3 3.4 fusion.24
  991.8 11.7 cholesky.542
  1005.0 9.8 custom-call.91
  1015.8 3.0 convolution_subtract_fusion.3
  1018.8 11.9 cholesky.562
  1032.2 9.8 custom-call.92
  1045.2 11.7 cholesky.580
  1064.0 5.3 select_select_fusion
  1069.3 27.0 %while.1 = (s32[]{:T(128)}, f32[1152,1152]{0,1:T(8,128)}, s32[9,2]{0,1:T(2,128)S(1)}, f32[9,128,128]{2,1,0:T(8,128)S(1)}, s32[]{:T(128)}) while((s32[]{:T(128)}, f32[1152,1152]{0,1:T(8,128)}, s32[9,2]{0,1:T(2,128)S(1)}, f32[9,128,128]{2,1,0:T(8,128)S(1)}, s32[]{:T(128)}) %tuple.70), condition=%wide.while_cond, body=%wide.while_body.sunk | while | flops 2 | bytes 393321 | solution.py:41
  1096.3 88.6 %custom-call.93 = f32[9,128,128]{1,2,0:T(8,128)S(1)} custom-call(f32[9,128,128]{2,1,0:T(8,128)S(1)} %get-tuple-element.12), custom_call_target="InvertDiagBlocksLowerTriangular" | custom-call | tf_op jit(solution)/shard_map/jit(_cho_solve)/triangular_solve | solution.py:41
  1208.2 11.9 cholesky.219
  1221.8 9.8 custom-call.84
  1234.2 54.4 %all-gather.6.cloned.1.call-done = f32[9216,128]{1,0:T(8,128)} async-done(((f32[1152,128]{1,0:T(8,128)}), f32[9216,128]{1,0:T(8,128)}) %all-gather.6.cloned.1.call-update) | async-done | bytes 4718608 | tf_op jit(solution)/shard_map/all_gather | solution.py:72
  1288.7 4.9 copy.269
  (209 shorter events, 94.0 us)
Async XLA Ops:
  7.8 16.9 %all-to-all-start = ((s32[8,1,4]{2,1,0:T(1,128)}), s32[8,1,4]{2,1,0:T(1,128)S(1)}, u32[]{:S(2)}, u32[]{:S(2)}) async-start(s32[8,1,4]{2,1,0:T(1,128)} %broadcast_in_dim.57), calls=%async_computation | async-start | bytes 8192 | tf_op jit(solution)/shard_map/all_to_all | solution.py:58
  24.7 99.2 %all-to-all-start.1 = ((bf16[8,512,512]{2,1,0:T(8,128)(2,1)}), bf16[8,512,512]{2,1,0:T(8,128)(2,1)}, u32[]{:S(2)}, u32[]{:S(2)}) async-start(bf16[8,512,512]{2,1,0:T(8,128)(2,1)} %broadcast_select_fusion), calls=%async_computation.1 | async-start | bytes 8388608 | tf_op jit(solution)/shard_map/all_to_all | solution.py:57
  29.8 600.9 %all-reduce.6.cloned.1.call-start = ((), (), s32[]{:S(2)}) async-start(), calls=%async_computation.4 | async-start | bytes 13107200
  166.6 0.7 copy-start.3
  166.6 617.8 %all-gather.4.cloned.1.call-start = ((), (), s32[]{:S(2)}) async-start(), calls=%async_computation.2 | async-start | bytes 6758400 | tf_op jit(solution)/shard_map/all_gather | solution.py:69
  632.3 656.4 %all-gather.6.cloned.1.call-start = ((), (), s32[]{:S(2)}) async-start(), calls=%async_computation.3 | async-start | bytes 5308416 | tf_op jit(solution)/shard_map/all_gather | solution.py:72
  802.0 2.7 copy-start
  818.9 2.4 copy-start.2
  1184.9 10.2 copy-start.1
Sparse Core Ops, SparseCore 0:
  166.7 463.8 all-reduce.5
  634.2 150.2 all-gather.3
  1234.4 54.2 all-gather.5
where the time goes:
time: 1310 us; the launch traced here: 1300 us
  waiting for transfers between devices  762 us (58%)
  other arithmetic  335 us (26%)
  local copies, waits for them, and re-layouts  94.4 us (7%)
  matrix products  76.5 us (6%)
  between operations  20.7 us (2%)
    unnamed x4, waiting for transfers between devices  462 us
    another operation x35, other arithmetic, precondition(): act_cholesky = jnp.linalg.cholesky(act_factor)  196 us
    all_gather x1, waiting for transfers between devices, body(): gathered = lax.all_gather(row_sums, 'dp', axis=0, tiled=True)  152 us
    another operation x3, other arithmetic, precondition(): left_solved = jax.scipy.linalg.cho_solve((act_cholesky, True), cross_term)  93.9 us
    all_to_all x1, waiting for transfers between devices, body(): lax.all_to_all(ordered, 'owner', split_axis=0, concat_axis=1, tiled=True)  93.7 us
    all_gather x1, waiting for transfers between devices, body(): return lax.all_gather(results, 'owner', axis=0, tiled=True)  54.4 us
    another operation x16, matrix products, precondition(): act_cholesky = jnp.linalg.cholesky(act_factor)  34.1 us
    another operation x45, local copies, waits for them, and re-layouts  26.7 us
  transfers between devices with their start and end apart: 5, of which 4 were waited for; matrix products, arithmetic and copies ran while one was open for 1% of the time, Pallas kernels for 0%

commit v1 on v0

--- a/solution.py
+++ b/solution.py
@@ -1,3 +1,4 @@
+import numpy as np
 import jax
 import jax.numpy as jnp
 from jax import lax
@@ -43,6 +44,29 @@
     return jax.scipy.linalg.cho_solve((grad_cholesky, True), left_solved.T).T
 
 
+def _tri_pairs(nb):
+    return [(i, j) for i in range(nb) for j in range(i + 1)]
+
+
+def pack_lower(gram, block):
+    nb = gram.shape[0] // block
+    tiles = gram.reshape(nb, block, nb, block).transpose(0, 2, 1, 3)
+    pairs = _tri_pairs(nb)
+    rows = np.array([p[0] for p in pairs], dtype=np.int32)
+    cols = np.array([p[1] for p in pairs], dtype=np.int32)
+    return tiles[rows, cols]
+
+
+def unpack_lower(blocks, nb):
+    block = blocks.shape[-1]
+    index = {p: k for k, p in enumerate(_tri_pairs(nb))}
+    pick = np.array([[index[(max(i, j), min(i, j))] for j in range(nb)] for i in range(nb)], dtype=np.int32)
+    upper = np.array([[i < j for j in range(nb)] for i in range(nb)])
+    tiles = blocks[pick]
+    tiles = jnp.where(upper[:, :, None, None], jnp.swapaxes(tiles, -1, -2), tiles)
+    return tiles.transpose(0, 2, 1, 3).reshape(nb * block, nb * block)
+
+
 def body(line_columns, line_widths, layer_owner):
     layer_count, positions, packed_width = line_columns.shape
     channels = packed_width // 4
@@ -59,16 +83,23 @@
     )
     blocks = received.reshape(per_owner, n_owners, positions, packed_width)
     columns = patch_columns(blocks, source_widths.reshape(n_owners, line_widths.shape[1]))
-    columns = columns.reshape(per_owner, n_owners * positions, full_width)
-    row_sums = lax.psum_scatter(
-        jnp.einsum("lpr,lpb->rlb", columns, columns, preferred_element_type=jnp.float32),
-        "dp",
-        scatter_dimension=0,
-        tiled=True,
+    columns = columns.reshape(n_owners * positions, full_width)
+    gram = jnp.dot(columns.T, columns, preferred_element_type=jnp.float32)
+    block = 128
+    nb = full_width // block
+    packed = pack_lower(gram, block)
+    n_blocks = packed.shape[0]
+    padded = -(-n_blocks * block // (8 * n_replicas)) * 8 * n_replicas // block
+    packed = jnp.concatenate(
+        [packed, jnp.zeros((padded - n_blocks, block, block), packed.dtype)], axis=0
     )
-    gathered = lax.all_gather(row_sums, "dp", axis=0, tiled=True)
-    factors = [gathered[:, 0, :]]
-    results = jnp.stack([precondition(factor, total_rows) for factor in factors])
+    chunk = padded * block // n_replicas
+    packed = packed.reshape(n_replicas, chunk, block)
+    mine = lax.psum_scatter(packed, "dp", scatter_dimension=0, tiled=True)
+    gathered = lax.all_gather(mine, "dp", axis=0, tiled=True)
+    gathered = gathered.reshape(padded, block, block)[:n_blocks]
+    factor = unpack_lower(gathered, nb)
+    results = precondition(factor, total_rows)[None]
     return lax.all_gather(results, "owner", axis=0, tiled=True)
 
 

time: 1310 us -> 1090 us (0.83)
  waiting for transfers between devices: 762 us -> 486 us
  local copies, waits for them, and re-layouts: 94.4 us -> 138 us
    unnamed x4 -> x3, waiting for transfers between devices: 462 us -> 0.05 us
    reduce_scatter x0 -> x1, waiting for transfers between devices: none -> 217 us  [body(): mine = lax.psum_scatter(packed, 'dp', scatter_dimension=0, tiled=True)]
    all_gather x1, waiting for transfers between devices: 152 us -> 121 us  [body(): gathered = lax.all_gather(mine, 'dp', axis=0, tiled=True)]
    gather x0 -> x3, local copies, waits for them, and re-layouts: none -> 19.3 us  [the longest x2 13.9 us: unpack_lower(): tiles = blocks[pick]]
    dot_general x0 -> x1, local copies, waits for them, and re-layouts: none -> 14.3 us  [body(): gram = jnp.dot(columns.T, columns, preferred_element_type=jnp.float32)]
    all_gather x1 -> x0, local copies, waits for them, and re-layouts: 14.2 us -> none  [body(): gathered = lax.all_gather(row_sums, 'dp', axis=0, tiled=True)]
    transpose x1 -> x0, local copies, waits for them, and re-layouts: 14.2 us -> none  [body(): jnp.einsum('lpr,lpb->rlb', columns, columns, preferred_element_type=jnp.f...]
    another operation x47 -> x45, local copies, waits for them, and re-layouts: 26.9 us -> 26.7 us
where the time goes in v1:
time: 1090 us; the launch traced here: 1080 us
  waiting for transfers between devices  486 us (45%)
  other arithmetic  342 us (31%)
  local copies, waits for them, and re-layouts  138 us (13%)
  matrix products  81.1 us (7%)
  between operations  19.9 us (2%)
  starting transfers between devices  11.3 us (1%)
    reduce_scatter x1, waiting for transfers between devices, body(): mine = lax.psum_scatter(packed, 'dp', scatter_dimension=0, tiled=True)  217 us
    another operation x35, other arithmetic, precondition(): act_cholesky = jnp.linalg.cholesky(act_factor)  191 us
    all_gather x1, waiting for transfers between devices, body(): gathered = lax.all_gather(mine, 'dp', axis=0, tiled=True)  121 us
    another operation x3, other arithmetic, precondition(): left_solved = jax.scipy.linalg.cho_solve((act_cholesky, True), cross_term)  93.9 us
    all_to_all x1, waiting for transfers between devices, body(): lax.all_to_all(ordered, 'owner', split_axis=0, concat_axis=1, tiled=True)  93.7 us
    all_gather x1, waiting for transfers between devices, body(): return lax.all_gather(results, 'owner', axis=0, tiled=True)  54.7 us
    another operation x16, matrix products, precondition(): act_cholesky = jnp.linalg.cholesky(act_factor)  34.3 us
    another operation x45, local copies, waits for them, and re-layouts  26.7 us
  transfers between devices with their start and end apart: 5, of which 4 were waited for; matrix products, arithmetic and copies ran while one was open for 1% of the time, Pallas kernels for 0%

profile of v1, /device:TPU:2, one launch (start us, length us, event | category | flops | bytes accessed | tf_op | source)
XLA Modules:
  0.0 1079.3 jit_solution(5165541737103423756)
XLA Ops:
  7.8 5.9 all-to-all-start
  15.0 5.0 gather_fusion
  20.0 4.7 broadcast_select_fusion
  24.7 5.1 all-to-all-start.1
  30.2 93.7 %all-to-all-done.1 = bf16[8,512,512]{2,1,0:T(8,128)(2,1)} async-done(((bf16[8,512,512]{2,1,0:T(8,128)(2,1)}), bf16[8,512,512]{2,1,0:T(8,128)(2,1)}, u32[]{:S(2)}, u32[]{:S(2)}) %all-to-all-start.1) | async-done | bytes 4194336 | tf_op jit(solution)/shard_map/all_to_all | solution.py:81
  125.2 3.9 fusion.126
  133.5 6.0 fusion
  139.5 14.3 %copy.120 = bf16[1280,4096]{1,0:T(8,128)(2,1)} copy(bf16[1280,4096]{0,1:T(8,128)(2,1)} %fusion) | data formatting | bytes 20971520 | tf_op jit(solution)/shard_map/dot_general | solution.py:87
  153.8 22.7 %convolution_bitcast_fusion = f32[10,10,128,128]{3,2,1,0:T(8,128)} fusion(bf16[10,128,4096,1]{2,1,3,0:T(8,128)(2,1)} %bitcast.218, bf16[10,128,4096,1]{2,1,0,3:T(8,128)(2,1)} %bitcast.219), kind=kOutput, calls=%fused_computation.19 | convolution fusion | flops 13421772800 | bytes 27525120 | tf_op jit(solution)/shard_map/dot_general | solution.py:87
  176.5 5.5 gather_fusion.1
  182.0 4.3 concatenate.96
  186.4 216.8 %reduce-scatter.2.cloned.1.call-done = f32[1,224,128]{2,1,0:T(8,128)} async-done(((f32[32,224,128]{2,1,0:T(8,128)}), f32[1,224,128]{2,1,0:T(8,128)}) %reduce-scatter.2.cloned.1.call-update) | async-done | bytes 114704 | tf_op jit(solution)/shard_map/reduce_scatter | solution.py:98
  403.6 121.2 %all-gather.4.cloned.1.call-done = f32[32,224,128]{2,1,0:T(8,128)} async-done(((f32[1,224,128]{2,1,0:T(8,128)}), f32[32,224,128]{2,1,0:T(8,128)}) %all-gather.4.cloned.1.call-update) | async-done | bytes 3670032 | tf_op jit(solution)/shard_map/all_gather | solution.py:99
  524.8 4.2 slice.440
  529.0 5.7 gather_fusion.2
  534.7 8.1 copy.121
  542.9 8.1 fusion.1
  551.0 11.5 %copy.122 = f32[10,128,10,128]{3,2,1,0:T(8,128)} copy(f32[10,128,10,128]{1,3,2,0:T(8,128)} %fusion.1) | data formatting | bytes 13107200 | tf_op jit(solution)/shard_map/div | solution.py:33
  562.5 7.2 copy.157
  575.1 6.9 copy.153
  581.9 5.2 select_add_fusion
  587.1 7.2 copy.125
  594.4 4.6 fusion.2
  601.4 11.7 %cholesky.228 = f32[128,128]{1,0:T(8,128)S(1)} custom-call(f32[128,128]{1,0:T(8,128)S(1)} %cholesky.596), custom_call_target="Cholesky" | custom-call | tf_op jit(solution)/shard_map/jit(cholesky)/cholesky | solution.py:41
  613.3 9.8 custom-call.85
  626.6 11.7 %cholesky.247 = f32[128,128]{1,0:T(8,128)S(1)} custom-call(f32[128,128]{1,0:T(8,128)S(1)} %cholesky.600), custom_call_target="Cholesky" | custom-call | tf_op jit(solution)/shard_map/jit(cholesky)/cholesky | solution.py:41
  641.2 9.8 custom-call.86
  656.9 11.7 %cholesky.464 = f32[128,128]{1,0:T(8,128)S(1)} custom-call(f32[128,128]{1,0:T(8,128)S(1)} %cholesky.605), custom_call_target="Cholesky" | custom-call | tf_op jit(solution)/shard_map/jit(cholesky)/cholesky | solution.py:41
  669.4 9.8 custom-call.87
  684.3 11.7 %cholesky.483 = f32[128,128]{1,0:T(8,128)S(1)} custom-call(f32[128,128]{1,0:T(8,128)S(1)} %cholesky.610), custom_call_target="Cholesky" | custom-call | tf_op jit(solution)/shard_map/jit(cholesky)/cholesky | solution.py:41
  696.8 9.8 custom-call.88
  711.5 12.1 %cholesky.502 = f32[128,128]{1,0:T(8,128)S(1)} custom-call(f32[128,128]{1,0:T(8,128)S(1)} %cholesky.615), custom_call_target="Cholesky" | custom-call | tf_op jit(solution)/shard_map/jit(cholesky)/cholesky | solution.py:41
  724.4 9.8 custom-call.89
  735.4 3.8 fusion.13
  739.2 11.7 %cholesky.522 = f32[128,128]{1,0:T(8,128)S(1)} custom-call(f32[128,128]{1,0:T(8,128)S(1)} %cholesky.620), custom_call_target="Cholesky" | custom-call | tf_op jit(solution)/shard_map/jit(cholesky)/cholesky | solution.py:41
  751.7 9.8 custom-call.90
  766.2 11.7 %cholesky.542 = f32[128,128]{1,0:T(8,128)S(1)} custom-call(f32[128,128]{1,0:T(8,128)S(1)} %cholesky.625), custom_call_target="Cholesky" | custom-call | tf_op jit(solution)/shard_map/jit(cholesky)/cholesky | solution.py:41
  778.7 9.8 custom-call.91
  792.5 12.1 %cholesky.562 = f32[128,128]{1,0:T(8,128)S(1)} custom-call(f32[128,128]{1,0:T(8,128)S(1)} %cholesky.630), custom_call_target="Cholesky" | custom-call | tf_op jit(solution)/shard_map/jit(cholesky)/cholesky | solution.py:41
  805.4 9.8 custom-call.92
  818.4 11.7 %cholesky.580 = f32[128,128]{1,0:T(8,128)S(1)} custom-call(f32[128,128]{1,0:T(8,128)S(1)} %convolution_subtract_fusion.16), custom_call_target="Cholesky" | custom-call | tf_op jit(solution)/shard_map/jit(cholesky)/cholesky | solution.py:41
  843.3 5.3 select_select_fusion
  848.6 27.0 %while.1 = (s32[]{:T(128)}, f32[1152,1152]{0,1:T(8,128)}, s32[9,2]{0,1:T(2,128)S(1)}, f32[9,128,128]{2,1,0:T(8,128)S(1)}, s32[]{:T(128)}) while((s32[]{:T(128)}, f32[1152,1152]{0,1:T(8,128)}, s32[9,2]{0,1:T(2,128)S(1)}, f32[9,128,128]{2,1,0:T(8,128)S(1)}, s32[]{:T(128)}) %tuple.63), condition=%wide.while_cond, body=%wide.while_body.sunk | while | flops 2 | bytes 393329 | solution.py:42
  875.6 88.6 %custom-call.93 = f32[9,128,128]{1,2,0:T(8,128)S(1)} custom-call(f32[9,128,128]{2,1,0:T(8,128)S(1)} %get-tuple-element.12), custom_call_target="InvertDiagBlocksLowerTriangular" | custom-call | tf_op jit(solution)/shard_map/jit(_cho_solve)/triangular_solve | solution.py:42
  987.3 11.9 %cholesky.219 = f32[128,128]{1,0:T(8,128)S(1)} custom-call(f32[128,128]{1,0:T(8,128)S(1)} %fusion.99), custom_call_target="Cholesky" | custom-call | tf_op jit(solution)/shard_map/jit(cholesky)/cholesky | solution.py:43
  1000.6 9.8 custom-call.84
  1013.1 54.7 %all-gather.6.cloned.1.call-done = f32[9216,128]{1,0:T(8,128)} async-done(((f32[1152,128]{1,0:T(8,128)}), f32[9216,128]{1,0:T(8,128)}) %all-gather.6.cloned.1.call-update) | async-done | bytes 4718608 | tf_op jit(solution)/shard_map/all_gather | solution.py:103
  1067.7 4.9 copy.238
  (218 shorter events, 117.7 us)
Async XLA Ops:
  7.8 16.9 %all-to-all-start = ((s32[8,1,4]{2,1,0:T(1,128)}), s32[8,1,4]{2,1,0:T(1,128)S(1)}, u32[]{:S(2)}, u32[]{:S(2)}) async-start(s32[8,1,4]{2,1,0:T(1,128)} %broadcast_in_dim.82), calls=%async_computation | async-start | bytes 8192 | tf_op jit(solution)/shard_map/all_to_all | solution.py:82
  24.7 99.2 %all-to-all-start.1 = ((bf16[8,512,512]{2,1,0:T(8,128)(2,1)}), bf16[8,512,512]{2,1,0:T(8,128)(2,1)}, u32[]{:S(2)}, u32[]{:S(2)}) async-start(bf16[8,512,512]{2,1,0:T(8,128)(2,1)} %broadcast_select_fusion), calls=%async_computation.1 | async-start | bytes 8388608 | tf_op jit(solution)/shard_map/all_to_all | solution.py:81
  29.8 373.4 %reduce-scatter.2.cloned.1.call-start = ((), (), s32[]{:S(2)}) async-start(), calls=%async_computation.3 | async-start | bytes 3784704 | tf_op jit(solution)/shard_map/reduce_scatter | solution.py:98
  153.8 22.7 %copy-start.3 = (s32[55]{0:T(128)S(1)}, s32[55]{0:T(128)}, u32[]{:S(2)}) copy-start(s32[55]{0:T(128)} %constant.467) | copy-start | bytes 664
  182.0 221.6 %copy-start.5 = (s32[100]{0:T(128)S(1)}, s32[100]{0:T(128)}, u32[]{:S(2)}) copy-start(s32[100]{0:T(128)} %constant.468) | copy-start | bytes 1204
  186.3 338.4 %all-gather.4.cloned.1.call-start = ((), (), s32[]{:S(2)}) async-start(), calls=%async_computation.4 | async-start | bytes 3784704 | tf_op jit(solution)/shard_map/all_gather | solution.py:99
  403.3 664.5 %all-gather.6.cloned.1.call-start = ((), (), s32[]{:S(2)}) async-start(), calls=%async_computation.5 | async-start | bytes 5308416 | tf_op jit(solution)/shard_map/all_gather | solution.py:103
  534.7 8.1 copy-start.4
  569.7 2.7 copy-start
  599.0 2.4 copy-start.2
  964.2 10.2 copy-start.1
Sparse Core Ops, SparseCore 0:
  186.4 216.7 reduce-scatter.1
  407.2 117.5 all-gather.3
  1013.2 54.4 all-gather.5

commit v2 on v1

--- a/solution.py
+++ b/solution.py
@@ -71,7 +71,9 @@
     layer_count, positions, packed_width = line_columns.shape
     channels = packed_width // 4
     full_width = 10 * channels
-    n_replicas = lax.axis_size("dp")
+    n_replicas = 1
+    for axis in DP_AXES:
+        n_replicas = n_replicas * lax.axis_size(axis)
     n_owners = lax.axis_size("owner")
     per_owner = layer_count // n_owners
     total_rows = n_replicas * n_owners * positions
@@ -95,15 +97,26 @@
     )
     chunk = padded * block // n_replicas
     packed = packed.reshape(n_replicas, chunk, block)
-    mine = lax.psum_scatter(packed, "dp", scatter_dimension=0, tiled=True)
-    gathered = lax.all_gather(mine, "dp", axis=0, tiled=True)
+    mine = packed.reshape(padded * block, block)
+    for axis in DP_AXES[::-1]:
+        mine = lax.psum_scatter(mine, axis, scatter_dimension=0, tiled=True)
+    gathered = mine
+    for axis in DP_AXES:
+        gathered = lax.all_gather(gathered, axis, axis=0, tiled=True)
     gathered = gathered.reshape(padded, block, block)[:n_blocks]
     factor = unpack_lower(gathered, nb)
     results = precondition(factor, total_rows)[None]
     return lax.all_gather(results, "owner", axis=0, tiled=True)
 
 
+DP_AXES = ("dp_x", "dp_z", "dp_y")
+
+
 def solution(mesh):
-    in_specs = (P(None, ("dp", "owner"), None), P(("dp", "owner"), None), P())
+    dp_shape = (4, 2, mesh.shape["dp"] // 8)
+    devices = mesh.devices.reshape(dp_shape + (mesh.shape["owner"],))
+    fine = jax.sharding.Mesh(devices, DP_AXES + ("owner",))
+    rows = DP_AXES + ("owner",)
+    in_specs = (P(None, rows, None), P(rows, None), P())
     out_specs = P()
-    return jax.shard_map(body, mesh=mesh, in_specs=in_specs, out_specs=out_specs, check_vma=False)
+    return jax.shard_map(body, mesh=fine, in_specs=in_specs, out_specs=out_specs, check_vma=False)

time: 1090 us -> 946 us (0.87)
  waiting for transfers between devices: 486 us -> 310 us
  blocking collectives: 0 us -> 34.6 us
    reduce_scatter x1 -> x3, waiting for transfers between devices: 217 us -> 106 us  [body(): mine = lax.psum_scatter(mine, axis, scatter_dimension=0, tiled=True)]
    all_gather x1, waiting for transfers between devices: 121 us -> 49.7 us  [body(): gathered = lax.all_gather(gathered, axis, axis=0, tiled=True)]
    all_gather x0 -> x2, blocking collectives: none -> 34.6 us  [body(): gathered = lax.all_gather(gathered, axis, axis=0, tiled=True)]
  transfers between devices with their start and end apart: 5 -> 7, of which waited for: 4 -> 6; matrix products, arithmetic and copies ran while one was open for 1% -> 1% of each run, Pallas kernels for 0% -> 0%
where the time goes in v2:
time: 946 us; the launch traced here: 937 us
  other arithmetic  342 us (36%)
  waiting for transfers between devices  310 us (33%)
  local copies, waits for them, and re-layouts  138 us (15%)
  matrix products  81.1 us (9%)
  blocking collectives  34.6 us (4%)
  between operations  19.9 us (2%)
  starting transfers between devices  11.4 us (1%)
    another operation x35, other arithmetic, precondition(): act_cholesky = jnp.linalg.cholesky(act_factor)  191 us
    reduce_scatter x3, waiting for transfers between devices, body(): mine = lax.psum_scatter(mine, axis, scatter_dimension=0, tiled=True)  106 us
    another operation x3, other arithmetic, precondition(): left_solved = jax.scipy.linalg.cho_solve((act_cholesky, True), cross_term)  93.9 us
    all_to_all x1, waiting for transfers between devices, body(): lax.all_to_all(ordered, 'owner', split_axis=0, concat_axis=1, tiled=True)  93.7 us
    all_gather x1, waiting for transfers between devices, body(): return lax.all_gather(results, 'owner', axis=0, tiled=True)  60.1 us
    all_gather x1, waiting for transfers between devices, body(): gathered = lax.all_gather(gathered, axis, axis=0, tiled=True)  49.7 us
    all_gather x2, blocking collectives, body(): gathered = lax.all_gather(gathered, axis, axis=0, tiled=True)  34.6 us
    another operation x16, matrix products, precondition(): act_cholesky = jnp.linalg.cholesky(act_factor)  34.3 us
  transfers between devices with their start and end apart: 7, of which 6 were waited for; matrix products, arithmetic and copies ran while one was open for 1% of the time, Pallas kernels for 0%

profile of v2, /device:TPU:2, one launch (start us, length us, event | category | flops | bytes accessed | tf_op | source)
XLA Modules:
  0.0 937.3 jit_solution(9149687033109921557)
XLA Ops:
  7.8 5.9 all-to-all-start
  15.0 5.0 gather_fusion
  20.0 4.7 broadcast_select_fusion
  24.7 5.1 all-to-all-start.1
  30.2 93.7 %all-to-all-done.1 = bf16[8,512,512]{2,1,0:T(8,128)(2,1)} async-done(((bf16[8,512,512]{2,1,0:T(8,128)(2,1)}), bf16[8,512,512]{2,1,0:T(8,128)(2,1)}, u32[]{:S(2)}, u32[]{:S(2)}) %all-to-all-start.1) | async-done | bytes 4194336 | tf_op jit(solution)/shard_map/all_to_all | solution.py:83
  133.5 6.0 fusion
  139.5 14.3 %copy.120 = bf16[1280,4096]{1,0:T(8,128)(2,1)} copy(bf16[1280,4096]{0,1:T(8,128)(2,1)} %fusion) | data formatting | bytes 20971520 | tf_op jit(solution)/shard_map/dot_general | solution.py:89
  153.8 22.7 %convolution_bitcast_fusion = f32[10,10,128,128]{3,2,1,0:T(8,128)} fusion(bf16[10,128,4096,1]{2,1,3,0:T(8,128)(2,1)} %bitcast.219, bf16[10,128,4096,1]{2,1,0,3:T(8,128)(2,1)} %bitcast.220), kind=kOutput, calls=%fused_computation.19 | convolution fusion | flops 13421772800 | bytes 27525120 | tf_op jit(solution)/shard_map/dot_general | solution.py:89
  176.5 5.5 gather_fusion.1
  186.4 45.5 %reduce-scatter.4.cloned.1.call-done = f32[1792,128]{1,0:T(8,128)} async-done(((f32[7168,128]{1,0:T(8,128)}), f32[1792,128]{1,0:T(8,128)}) %reduce-scatter.4.cloned.1.call-update) | async-done | bytes 917520 | tf_op jit(solution)/shard_map/reduce_scatter | solution.py:102
  232.0 40.3 %reduce-scatter.6.cloned.1.call-done = f32[896,128]{1,0:T(8,128)} async-done(((f32[1792,128]{1,0:T(8,128)}), f32[896,128]{1,0:T(8,128)}) %reduce-scatter.6.cloned.1.call-update) | async-done | bytes 458768 | tf_op jit(solution)/shard_map/reduce_scatter | solution.py:102
  272.4 20.5 %reduce-scatter.8.cloned.1.call-done = f32[224,128]{1,0:T(8,128)} async-done(((f32[896,128]{1,0:T(8,128)}), f32[224,128]{1,0:T(8,128)}) %reduce-scatter.8.cloned.1.call-update) | async-done | bytes 114704 | tf_op jit(solution)/shard_map/reduce_scatter | solution.py:102
  292.9 13.4 %all_gather.12 = f32[896,128]{1,0:T(8,128)S(1)} all-gather(f32[224,128]{1,0:T(8,128)} %reduce-scatter.8.cloned.1.call-done), channel_id=1, replica_groups=mesh['dp_x'=4,'dp_z'=2,'dp_y'=4,'owner'=8] {'dp_x'}, dimensions={0}, use_global_device_ids=true | all-gather | bytes 573440 | tf_op jit(solution)/shard_map/all_gather | solution.py:105
  306.3 21.1 %all_gather.13 = f32[1792,128]{1,0:T(8,128)} all-gather(f32[896,128]{1,0:T(8,128)S(1)} %all_gather.12), channel_id=1, replica_groups=mesh['dp_x'=4,'dp_z'=2,'dp_y'=4,'owner'=8] {'dp_z'}, dimensions={0}, use_global_device_ids=true | all-gather | bytes 1376256 | tf_op jit(solution)/shard_map/all_gather | solution.py:105
  327.8 49.7 %all-gather.4.cloned.1.call-done = f32[7168,128]{1,0:T(8,128)} async-done(((f32[1792,128]{1,0:T(8,128)}), f32[7168,128]{1,0:T(8,128)}) %all-gather.4.cloned.1.call-update) | async-done | bytes 3670032 | tf_op jit(solution)/shard_map/all_gather | solution.py:105
  381.6 5.7 gather_fusion.2
  387.3 8.1 copy.121
  395.4 8.1 fusion.1
  403.5 11.5 %copy.122 = f32[10,128,10,128]{3,2,1,0:T(8,128)} copy(f32[10,128,10,128]{1,3,2,0:T(8,128)} %fusion.1) | data formatting | bytes 13107200 | tf_op jit(solution)/shard_map/div | solution.py:33
  415.0 7.2 copy.157
  427.6 6.9 copy.153
  434.5 5.2 select_add_fusion
  439.7 7.2 copy.125
  446.9 4.6 fusion.2
  454.0 11.7 %cholesky.228 = f32[128,128]{1,0:T(8,128)S(1)} custom-call(f32[128,128]{1,0:T(8,128)S(1)} %cholesky.596), custom_call_target="Cholesky" | custom-call | tf_op jit(solution)/shard_map/jit(cholesky)/cholesky | solution.py:41
  465.8 9.8 %custom-call.85 = f32[1,128,128]{1,2,0:T(8,128)S(1)} custom-call(f32[1,128,128]{2,1,0:T(8,128)S(1)} %get-tuple-element.81), custom_call_target="InvertDiagBlocksLowerTriangular" | custom-call | tf_op jit(solution)/shard_map/jit(cholesky)/cholesky | solution.py:41
  479.1 11.7 %cholesky.247 = f32[128,128]{1,0:T(8,128)S(1)} custom-call(f32[128,128]{1,0:T(8,128)S(1)} %cholesky.600), custom_call_target="Cholesky" | custom-call | tf_op jit(solution)/shard_map/jit(cholesky)/cholesky | solution.py:41
  493.8 9.8 %custom-call.86 = f32[1,128,128]{1,2,0:T(8,128)S(1)} custom-call(f32[1,128,128]{2,1,0:T(8,128)S(1)} %get-tuple-element.79), custom_call_target="InvertDiagBlocksLowerTriangular" | custom-call | tf_op jit(solution)/shard_map/jit(cholesky)/cholesky | solution.py:41
  509.5 11.7 %cholesky.464 = f32[128,128]{1,0:T(8,128)S(1)} custom-call(f32[128,128]{1,0:T(8,128)S(1)} %cholesky.605), custom_call_target="Cholesky" | custom-call | tf_op jit(solution)/shard_map/jit(cholesky)/cholesky | solution.py:41
  522.0 9.8 %custom-call.87 = f32[1,128,128]{1,2,0:T(8,128)S(1)} custom-call(f32[1,128,128]{2,1,0:T(8,128)S(1)} %get-tuple-element.77), custom_call_target="InvertDiagBlocksLowerTriangular" | custom-call | tf_op jit(solution)/shard_map/jit(cholesky)/cholesky | solution.py:41
  536.8 11.7 %cholesky.483 = f32[128,128]{1,0:T(8,128)S(1)} custom-call(f32[128,128]{1,0:T(8,128)S(1)} %cholesky.610), custom_call_target="Cholesky" | custom-call | tf_op jit(solution)/shard_map/jit(cholesky)/cholesky | solution.py:41
  549.4 9.8 %custom-call.88 = f32[1,128,128]{1,2,0:T(8,128)S(1)} custom-call(f32[1,128,128]{2,1,0:T(8,128)S(1)} %get-tuple-element.75), custom_call_target="InvertDiagBlocksLowerTriangular" | custom-call | tf_op jit(solution)/shard_map/jit(cholesky)/cholesky | solution.py:41
  564.1 12.1 %cholesky.502 = f32[128,128]{1,0:T(8,128)S(1)} custom-call(f32[128,128]{1,0:T(8,128)S(1)} %cholesky.615), custom_call_target="Cholesky" | custom-call | tf_op jit(solution)/shard_map/jit(cholesky)/cholesky | solution.py:41
  577.0 9.8 %custom-call.89 = f32[1,128,128]{1,2,0:T(8,128)S(1)} custom-call(f32[1,128,128]{2,1,0:T(8,128)S(1)} %get-tuple-element.73), custom_call_target="InvertDiagBlocksLowerTriangular" | custom-call | tf_op jit(solution)/shard_map/jit(cholesky)/cholesky | solution.py:41
  591.7 11.7 %cholesky.522 = f32[128,128]{1,0:T(8,128)S(1)} custom-call(f32[128,128]{1,0:T(8,128)S(1)} %cholesky.620), custom_call_target="Cholesky" | custom-call | tf_op jit(solution)/shard_map/jit(cholesky)/cholesky | solution.py:41
  604.2 9.8 %custom-call.90 = f32[1,128,128]{1,2,0:T(8,128)S(1)} custom-call(f32[1,128,128]{2,1,0:T(8,128)S(1)} %get-tuple-element.71), custom_call_target="InvertDiagBlocksLowerTriangular" | custom-call | tf_op jit(solution)/shard_map/jit(cholesky)/cholesky | solution.py:41
  618.8 11.7 %cholesky.542 = f32[128,128]{1,0:T(8,128)S(1)} custom-call(f32[128,128]{1,0:T(8,128)S(1)} %cholesky.625), custom_call_target="Cholesky" | custom-call | tf_op jit(solution)/shard_map/jit(cholesky)/cholesky | solution.py:41
  631.3 9.8 %custom-call.91 = f32[1,128,128]{1,2,0:T(8,128)S(1)} custom-call(f32[1,128,128]{2,1,0:T(8,128)S(1)} %get-tuple-element.69), custom_call_target="InvertDiagBlocksLowerTriangular" | custom-call | tf_op jit(solution)/shard_map/jit(cholesky)/cholesky | solution.py:41
  645.1 12.1 %cholesky.562 = f32[128,128]{1,0:T(8,128)S(1)} custom-call(f32[128,128]{1,0:T(8,128)S(1)} %cholesky.630), custom_call_target="Cholesky" | custom-call | tf_op jit(solution)/shard_map/jit(cholesky)/cholesky | solution.py:41
  658.0 9.8 %custom-call.92 = f32[1,128,128]{1,2,0:T(8,128)S(1)} custom-call(f32[1,128,128]{2,1,0:T(8,128)S(1)} %get-tuple-element.67), custom_call_target="InvertDiagBlocksLowerTriangular" | custom-call | tf_op jit(solution)/shard_map/jit(cholesky)/cholesky | solution.py:41
  671.0 11.7 %cholesky.580 = f32[128,128]{1,0:T(8,128)S(1)} custom-call(f32[128,128]{1,0:T(8,128)S(1)} %convolution_subtract_fusion.16), custom_call_target="Cholesky" | custom-call | tf_op jit(solution)/shard_map/jit(cholesky)/cholesky | solution.py:41
  695.9 5.3 select_select_fusion
  701.1 27.0 %while.1 = (s32[]{:T(128)}, f32[1152,1152]{0,1:T(8,128)}, s32[9,2]{0,1:T(2,128)S(1)}, f32[9,128,128]{2,1,0:T(8,128)S(1)}, s32[]{:T(128)}) while((s32[]{:T(128)}, f32[1152,1152]{0,1:T(8,128)}, s32[9,2]{0,1:T(2,128)S(1)}, f32[9,128,128]{2,1,0:T(8,128)S(1)}, s32[]{:T(128)}) %tuple.63), condition=%wide.while_cond, body=%wide.while_body.sunk | while | flops 2 | bytes 393329 | solution.py:42
  728.1 88.6 %custom-call.93 = f32[9,128,128]{1,2,0:T(8,128)S(1)} custom-call(f32[9,128,128]{2,1,0:T(8,128)S(1)} %get-tuple-element.12), custom_call_target="InvertDiagBlocksLowerTriangular" | custom-call | tf_op jit(solution)/shard_map/jit(_cho_solve)/triangular_solve | solution.py:42
  839.9 11.9 %cholesky.219 = f32[128,128]{1,0:T(8,128)S(1)} custom-call(f32[128,128]{1,0:T(8,128)S(1)} %fusion.99), custom_call_target="Cholesky" | custom-call | tf_op jit(solution)/shard_map/jit(cholesky)/cholesky | solution.py:43
  853.1 9.8 %custom-call.84 = f32[1,128,128]{1,2,0:T(8,128)S(1)} custom-call(f32[1,128,128]{2,1,0:T(8,128)S(1)} %fusion.80), custom_call_target="InvertDiagBlocksLowerTriangular" | custom-call | tf_op jit(solution)/shard_map/jit(_cho_solve)/triangular_solve | solution.py:44
  865.6 60.1 %all-gather.6.cloned.1.call-done = f32[9216,128]{1,0:T(8,128)} async-done(((f32[1152,128]{1,0:T(8,128)}), f32[9216,128]{1,0:T(8,128)}) %all-gather.6.cloned.1.call-update) | async-done | bytes 4718608 | tf_op jit(solution)/shard_map/all_gather | solution.py:109
  925.7 4.9 copy.238
  (226 shorter events, 133.9 us)
Async XLA Ops:
  7.8 16.9 %all-to-all-start = ((s32[8,1,4]{2,1,0:T(1,128)}), s32[8,1,4]{2,1,0:T(1,128)S(1)}, u32[]{:S(2)}, u32[]{:S(2)}) async-start(s32[8,1,4]{2,1,0:T(1,128)} %broadcast_in_dim.82), calls=%async_computation | async-start | bytes 8192 | tf_op jit(solution)/shard_map/all_to_all | solution.py:84
  24.7 99.2 %all-to-all-start.1 = ((bf16[8,512,512]{2,1,0:T(8,128)(2,1)}), bf16[8,512,512]{2,1,0:T(8,128)(2,1)}, u32[]{:S(2)}, u32[]{:S(2)}) async-start(bf16[8,512,512]{2,1,0:T(8,128)(2,1)} %broadcast_select_fusion), calls=%async_computation.1 | async-start | bytes 8388608 | tf_op jit(solution)/shard_map/all_to_all | solution.py:83
  29.8 202.1 %reduce-scatter.4.cloned.1.call-start = ((), (), s32[]{:S(2)}) async-start(), calls=%async_computation.5 | async-start | bytes 4587520 | tf_op jit(solution)/shard_map/reduce_scatter | solution.py:102
  153.8 22.7 %copy-start.3 = (s32[55]{0:T(128)S(1)}, s32[55]{0:T(128)}, u32[]{:S(2)}) copy-start(s32[55]{0:T(128)} %constant.467) | copy-start | bytes 664
  186.3 141.4 %copy-start.5 = (s32[100]{0:T(128)S(1)}, s32[100]{0:T(128)}, u32[]{:S(2)}) copy-start(s32[100]{0:T(128)} %constant.468) | copy-start | bytes 1204
  186.3 86.0 %reduce-scatter.6.cloned.1.call-start = ((), (), s32[]{:S(2)}) async-start(), calls=%async_computation.6 | async-start | bytes 1376256 | tf_op jit(solution)/shard_map/reduce_scatter | solution.py:102
  231.9 60.9 %reduce-scatter.8.cloned.1.call-start = ((), (), s32[]{:S(2)}) async-start(), calls=%async_computation.7 | async-start | bytes 573440 | tf_op jit(solution)/shard_map/reduce_scatter | solution.py:102
  272.3 105.2 %all-gather.4.cloned.1.call-start = ((), (), s32[]{:S(2)}) async-start(), calls=%async_computation.8 | async-start | bytes 4587520 | tf_op jit(solution)/shard_map/all_gather | solution.py:105
  327.5 598.2 %all-gather.6.cloned.1.call-start = ((), (), s32[]{:S(2)}) async-start(), calls=%async_computation.9 | async-start | bytes 5308416 | tf_op jit(solution)/shard_map/all_gather | solution.py:109
  387.3 8.1 copy-start.4
  422.3 2.7 copy-start
  451.6 2.4 copy-start.2
  816.7 10.2 %copy-start.1 = (f32[1152,1152]{0,1:T(8,128)S(1)}, f32[1152,1152]{0,1:T(8,128)}, u32[]{:S(2)}) copy-start(f32[1152,1152]{0,1:T(8,128)} %get-tuple-element.150) | copy-start | bytes 15925252
Sparse Core Ops, SparseCore 0:
  186.4 45.4 reduce-scatter.3
  234.4 37.8 reduce-scatter.5
  275.0 17.7 reduce-scatter.7
  327.6 49.8 all-gather.3
  865.7 59.8 all-gather.5

commit v3 on v2

--- a/solution.py
+++ b/solution.py
@@ -67,6 +67,70 @@
     return tiles.transpose(0, 2, 1, 3).reshape(nb * block, nb * block)
 
 
+HIGH = lax.Precision.HIGHEST
+
+
+def _mm(a, b):
+    return jnp.dot(a, b, precision=HIGH, preferred_element_type=jnp.float32)
+
+
+def _mm_t(a, b):
+    return lax.dot_general(a, b, (((0,), (0,)), ((), ())), precision=HIGH,
+                           preferred_element_type=jnp.float32)
+
+
+def _mm_nt(a, b):
+    return lax.dot_general(a, b, (((1,), (1,)), ((), ())), precision=HIGH,
+                           preferred_element_type=jnp.float32)
+
+
+def _chol_inv(block):
+    lower = jnp.linalg.cholesky(block, symmetrize_input=False)
+    eye = jnp.eye(block.shape[0], dtype=block.dtype)
+    inverse = lax.linalg.triangular_solve(lower, eye, left_side=True, lower=True)
+    return lower, inverse
+
+
+def precondition_blocks(blocks, nb, total_rows):
+    block = blocks.shape[-1]
+    na = nb - 1
+    index = {p: k for k, p in enumerate(_tri_pairs(nb))}
+    zero = len(index)
+    pick = np.array([[index[(i, j)] if i >= j else zero for j in range(na)] for i in range(nb)],
+                    dtype=np.int32)
+    scale = 1.0 / total_rows
+    tiles = blocks[pick] * scale
+    work = tiles.transpose(0, 2, 1, 3).reshape(nb * block, na * block)
+    eye = jnp.eye(block, dtype=blocks.dtype)
+    grad_factor = blocks[index[(na, na)]] * scale + damping * eye
+    inverses = []
+    for k in range(na):
+        lo = k * block
+        hi = lo + block
+        diag = work[lo:hi, lo:hi] + damping * eye
+        lower, inverse = _chol_inv(diag)
+        inverses.append(inverse)
+        panel = _mm_nt(work[hi:, lo:hi], inverse)
+        work = work.at[lo:hi, lo:hi].set(lower)
+        work = work.at[hi:, lo:hi].set(panel)
+        if k + 1 < na:
+            update = _mm_nt(panel, panel[: (na - k - 1) * block])
+            work = work.at[hi:, hi:].add(-update)
+    solved_t = work[na * block:, :]
+    pieces = [None] * na
+    for k in reversed(range(na)):
+        lo = k * block
+        hi = lo + block
+        rhs = solved_t[:, lo:hi].T
+        if k + 1 < na:
+            below = jnp.concatenate(pieces[k + 1:], axis=0)
+            rhs = rhs - _mm_t(work[hi:na * block, lo:hi], below)
+        pieces[k] = _mm_t(inverses[k], rhs)
+    left_solved = jnp.concatenate(pieces, axis=0)
+    _, grad_inverse = _chol_inv(grad_factor)
+    return _mm(_mm_nt(left_solved, grad_inverse), grad_inverse)
+
+
 def body(line_columns, line_widths, layer_owner):
     layer_count, positions, packed_width = line_columns.shape
     channels = packed_width // 4
@@ -103,9 +167,8 @@
     gathered = mine
     for axis in DP_AXES:
         gathered = lax.all_gather(gathered, axis, axis=0, tiled=True)
-    gathered = gathered.reshape(padded, block, block)[:n_blocks]
-    factor = unpack_lower(gathered, nb)
-    results = precondition(factor, total_rows)[None]
+    gathered = gathered.reshape(padded, block, block)
+    results = precondition_blocks(gathered, nb, total_rows)[None]
     return lax.all_gather(results, "owner", axis=0, tiled=True)
 
 

time: 946 us -> 802 us (0.85)
  other arithmetic: 342 us -> 256 us
  local copies, waits for them, and re-layouts: 138 us -> 81.5 us
    another operation x43 -> x45, other arithmetic: 308 us -> 227 us  [the longest x30 125 us: _chol_inv(): lower = jnp.linalg.cholesky(block, symmetrize_input=False)]
    dot_general x0 -> x36, matrix products: none -> 60 us  [the longest x18 44.6 us: _mm_nt(): lax.dot_general(a, b, (((1,), (1,)), ((), ())), precision=HIGH, preferred...]
    another operation x52 -> x10, matrix products: 58.4 us -> 2.85 us  [_chol_inv(): lax.linalg.triangular_solve(lower, eye, left_side=True, lower=True)]
    another operation x79 -> x0, local copies, waits for them, and re-layouts: 36.7 us -> none
    div x3 -> x0, other arithmetic: 13.6 us -> none  [the longest x1 8.14 us: precondition(): scaled = factor / total_rows]
    div x1 -> x0, local copies, waits for them, and re-layouts: 11.5 us -> none  [precondition(): scaled = factor / total_rows]
    mul x0 -> x1, local copies, waits for them, and re-layouts: none -> 9.84 us  [precondition_blocks(): tiles = blocks[pick] * scale]
    unnamed x41 -> x36, local copies, waits for them, and re-layouts: 24.3 us -> 18.3 us
where the time goes in v3:
time: 802 us; the launch traced here: 794 us
  waiting for transfers between devices  310 us (39%)
  other arithmetic  256 us (32%)
  matrix products  85.5 us (11%)
  local copies, waits for them, and re-layouts  81.5 us (10%)
  blocking collectives  34.5 us (4%)
  between operations  14.3 us (2%)
  starting transfers between devices  11.2 us (1%)
    another operation x30, other arithmetic, _chol_inv(): lower = jnp.linalg.cholesky(block, symmetrize_input=False)  125 us
    reduce_scatter x3, waiting for transfers between devices, body(): mine = lax.psum_scatter(mine, axis, scatter_dimension=0, tiled=True)  106 us
    another operation x15, other arithmetic, _chol_inv(): lax.linalg.triangular_solve(lower, eye, left_side=True, lower=True)  103 us
    all_to_all x1, waiting for transfers between devices, body(): lax.all_to_all(ordered, 'owner', split_axis=0, concat_axis=1, tiled=True)  93.7 us
    all_gather x1, waiting for transfers between devices, body(): return lax.all_gather(results, 'owner', axis=0, tiled=True)  60 us
    all_gather x1, waiting for transfers between devices, body(): gathered = lax.all_gather(gathered, axis, axis=0, tiled=True)  50.1 us
    dot_general x18, matrix products, _mm_nt(): lax.dot_general(a, b, (((1,), (1,)), ((), ())), precision=HIGH, preferred...  44.6 us
    all_gather x2, blocking collectives, body(): gathered = lax.all_gather(gathered, axis, axis=0, tiled=True)  34.5 us
  transfers between devices with their start and end apart: 7, of which 6 were waited for; matrix products, arithmetic and copies ran while one was open for 1% of the time, Pallas kernels for 0%

profile of v3, /device:TPU:2, one launch (start us, length us, event | category | flops | bytes accessed | tf_op | source)
XLA Modules:
  0.0 793.7 jit_solution(1356625987688774728)
XLA Ops:
  7.8 5.9 all-to-all-start
  15.0 5.0 gather_fusion
  20.0 4.7 broadcast_select_fusion
  24.7 5.1 all-to-all-start.1
  30.2 93.7 %all-to-all-done.1 = bf16[8,512,512]{2,1,0:T(8,128)(2,1)} async-done(((bf16[8,512,512]{2,1,0:T(8,128)(2,1)}), bf16[8,512,512]{2,1,0:T(8,128)(2,1)}, u32[]{:S(2)}, u32[]{:S(2)}) %all-to-all-start.1) | async-done | bytes 4194336 | tf_op jit(solution)/shard_map/all_to_all | solution.py:147
  127.5 3.9 fusion.101
  133.6 6.0 fusion
  139.5 14.3 %copy.37 = bf16[1280,4096]{1,0:T(8,128)(2,1)} copy(bf16[1280,4096]{0,1:T(8,128)(2,1)} %fusion) | data formatting | bytes 20971520 | tf_op jit(solution)/shard_map/dot_general | solution.py:153
  153.9 22.7 %convolution_bitcast_fusion = f32[10,10,128,128]{3,2,1,0:T(8,128)} fusion(bf16[10,128,4096,1]{2,1,3,0:T(8,128)(2,1)} %bitcast.176, bf16[10,128,4096,1]{2,1,0,3:T(8,128)(2,1)} %bitcast.177), kind=kOutput, calls=%fused_computation.13 | convolution fusion | flops 13421772800 | bytes 27525120 | tf_op jit(solution)/shard_map/dot_general | solution.py:153
  176.6 5.5 gather_fusion.1
  182.0 4.3 concatenate.110
  186.4 45.5 %reduce-scatter.4.cloned.1.call-done = f32[1792,128]{1,0:T(8,128)} async-done(((f32[7168,128]{1,0:T(8,128)}), f32[1792,128]{1,0:T(8,128)}) %reduce-scatter.4.cloned.1.call-update) | async-done | bytes 917520 | tf_op jit(solution)/shard_map/reduce_scatter | solution.py:166
  232.1 40.3 %reduce-scatter.6.cloned.1.call-done = f32[896,128]{1,0:T(8,128)} async-done(((f32[1792,128]{1,0:T(8,128)}), f32[896,128]{1,0:T(8,128)}) %reduce-scatter.6.cloned.1.call-update) | async-done | bytes 458768 | tf_op jit(solution)/shard_map/reduce_scatter | solution.py:166
  272.4 20.5 %reduce-scatter.8.cloned.1.call-done = f32[224,128]{1,0:T(8,128)} async-done(((f32[896,128]{1,0:T(8,128)}), f32[224,128]{1,0:T(8,128)}) %reduce-scatter.8.cloned.1.call-update) | async-done | bytes 114704 | tf_op jit(solution)/shard_map/reduce_scatter | solution.py:166
  292.9 13.4 %all_gather.12 = f32[896,128]{1,0:T(8,128)S(1)} all-gather(f32[224,128]{1,0:T(8,128)} %reduce-scatter.8.cloned.1.call-done), channel_id=1, replica_groups=mesh['dp_x'=4,'dp_z'=2,'dp_y'=4,'owner'=8] {'dp_x'}, dimensions={0}, use_global_device_ids=true | all-gather | bytes 573440 | tf_op jit(solution)/shard_map/all_gather | solution.py:169
  306.4 21.1 %all_gather.13 = f32[1792,128]{1,0:T(8,128)} all-gather(f32[896,128]{1,0:T(8,128)S(1)} %all_gather.12), channel_id=1, replica_groups=mesh['dp_x'=4,'dp_z'=2,'dp_y'=4,'owner'=8] {'dp_z'}, dimensions={0}, use_global_device_ids=true | all-gather | bytes 1376256 | tf_op jit(solution)/shard_map/all_gather | solution.py:169
  327.6 50.1 %all-gather.4.cloned.1.call-done = f32[7168,128]{1,0:T(8,128)} async-done(((f32[1792,128]{1,0:T(8,128)}), f32[7168,128]{1,0:T(8,128)}) %all-gather.4.cloned.1.call-update) | async-done | bytes 3670032 | tf_op jit(solution)/shard_map/all_gather | solution.py:169
  377.7 5.5 gather_fusion.2
  383.2 6.3 broadcast_multiply_fusion
  389.5 9.8 %copy.38 = f32[10,128,9,128]{1,0,3,2:T(8,128)} copy(f32[10,128,9,128]{3,1,2,0:T(8,128)} %bitcast.171) | data formatting | bytes 11796480 | tf_op jit(solution)/shard_map/mul | solution.py:102
  399.4 9.2 %copy.61 = f32[144,8,10,128]{3,1,2,0:T(8,128)} copy(f32[144,8,10,128]{3,2,1,0:T(8,128)} %bitcast.168) | data formatting | bytes 11796480
  408.5 7.7 copy.39
  417.1 11.7 %cholesky.165 = f32[128,128]{1,0:T(8,128)S(1)} custom-call(f32[128,128]{1,0:T(8,128)S(1)} %select_add_fusion.9), custom_call_target="Cholesky" | custom-call | tf_op jit(solution)/shard_map/jit(cholesky)/cholesky | solution.py:88
  430.7 9.8 %custom-call.16 = f32[1,128,128]{1,2,0:T(8,128)S(1)} custom-call(f32[1,128,128]{2,1,0:T(8,128)S(1)} %get-tuple-element.334), custom_call_target="InvertDiagBlocksLowerTriangular" | custom-call | tf_op jit(solution)/shard_map/triangular_solve/custom-call.0 | solution.py:90
  443.9 7.7 constant_dynamic-update-slice_fusion.45
  453.8 11.7 %cholesky.176 = f32[128,128]{1,0:T(8,128)S(1)} custom-call(f32[128,128]{1,0:T(8,128)S(1)} %select_add_fusion.8), custom_call_target="Cholesky" | custom-call | tf_op jit(solution)/shard_map/jit(cholesky)/cholesky | solution.py:88
  467.6 9.8 %custom-call.17 = f32[1,128,128]{1,2,0:T(8,128)S(1)} custom-call(f32[1,128,128]{2,1,0:T(8,128)S(1)} %get-tuple-element.332), custom_call_target="InvertDiagBlocksLowerTriangular" | custom-call | tf_op jit(solution)/shard_map/triangular_solve/custom-call.0 | solution.py:90
  480.2 6.2 constant_dynamic-update-slice_fusion.43
  488.3 11.7 %cholesky.187 = f32[128,128]{1,0:T(8,128)S(1)} custom-call(f32[128,128]{1,0:T(8,128)S(1)} %select_add_fusion.7), custom_call_target="Cholesky" | custom-call | tf_op jit(solution)/shard_map/jit(cholesky)/cholesky | solution.py:88
  502.1 9.8 %custom-call.18 = f32[1,128,128]{1,2,0:T(8,128)S(1)} custom-call(f32[1,128,128]{2,1,0:T(8,128)S(1)} %get-tuple-element.330), custom_call_target="InvertDiagBlocksLowerTriangular" | custom-call | tf_op jit(solution)/shard_map/triangular_solve/custom-call.0 | solution.py:90
  514.6 5.7 constant_dynamic-update-slice_fusion.41
  520.3 11.9 %cholesky.198 = f32[128,128]{1,0:T(8,128)S(1)} custom-call(f32[128,128]{1,0:T(8,128)S(1)} %select_add_fusion.6), custom_call_target="Cholesky" | custom-call | tf_op jit(solution)/shard_map/jit(cholesky)/cholesky | solution.py:88
  534.2 9.8 %custom-call.19 = f32[1,128,128]{1,2,0:T(8,128)S(1)} custom-call(f32[1,128,128]{2,1,0:T(8,128)S(1)} %get-tuple-element.328), custom_call_target="InvertDiagBlocksLowerTriangular" | custom-call | tf_op jit(solution)/shard_map/triangular_solve/custom-call.0 | solution.py:90
  545.6 4.6 constant_dynamic-update-slice_fusion.39
  550.2 11.7 %cholesky.209 = f32[128,128]{1,0:T(8,128)S(1)} custom-call(f32[128,128]{1,0:T(8,128)S(1)} %select_add_fusion.5), custom_call_target="Cholesky" | custom-call | tf_op jit(solution)/shard_map/jit(cholesky)/cholesky | solution.py:88
  563.9 9.8 %custom-call.20 = f32[1,128,128]{1,2,0:T(8,128)S(1)} custom-call(f32[1,128,128]{2,1,0:T(8,128)S(1)} %get-tuple-element.326), custom_call_target="InvertDiagBlocksLowerTriangular" | custom-call | tf_op jit(solution)/shard_map/triangular_solve/custom-call.0 | solution.py:90
  579.5 11.7 %cholesky.220 = f32[128,128]{1,0:T(8,128)S(1)} custom-call(f32[128,128]{1,0:T(8,128)S(1)} %select_add_fusion.4), custom_call_target="Cholesky" | custom-call | tf_op jit(solution)/shard_map/jit(cholesky)/cholesky | solution.py:88
  593.1 9.8 %custom-call.21 = f32[1,128,128]{1,2,0:T(8,128)S(1)} custom-call(f32[1,128,128]{2,1,0:T(8,128)S(1)} %get-tuple-element.323), custom_call_target="InvertDiagBlocksLowerTriangular" | custom-call | tf_op jit(solution)/shard_map/triangular_solve/custom-call.0 | solution.py:90
  608.2 11.9 %cholesky.264 = f32[128,128]{1,0:T(8,128)S(1)} custom-call(f32[128,128]{1,0:T(8,128)S(1)} %select_add_fusion), custom_call_target="Cholesky" | custom-call | tf_op jit(solution)/shard_map/jit(cholesky)/cholesky | solution.py:88
  621.4 9.8 %custom-call.25 = f32[1,128,128]{1,2,0:T(8,128)S(1)} custom-call(f32[1,128,128]{2,1,0:T(8,128)S(1)} %fusion.72), custom_call_target="InvertDiagBlocksLowerTriangular" | custom-call | tf_op jit(solution)/shard_map/triangular_solve/custom-call.0 | solution.py:90
  631.5 11.7 %cholesky.231 = f32[128,128]{1,0:T(8,128)S(1)} custom-call(f32[128,128]{1,0:T(8,128)S(1)} %select_add_fusion.3), custom_call_target="Cholesky" | custom-call | tf_op jit(solution)/shard_map/jit(cholesky)/cholesky | solution.py:88
  645.2 9.8 %custom-call.22 = f32[1,128,128]{1,2,0:T(8,128)S(1)} custom-call(f32[1,128,128]{2,1,0:T(8,128)S(1)} %get-tuple-element.321), custom_call_target="InvertDiagBlocksLowerTriangular" | custom-call | tf_op jit(solution)/shard_map/triangular_solve/custom-call.0 | solution.py:90
  657.8 11.9 %cholesky.242 = f32[128,128]{1,0:T(8,128)S(1)} custom-call(f32[128,128]{1,0:T(8,128)S(1)} %select_add_fusion.2), custom_call_target="Cholesky" | custom-call | tf_op jit(solution)/shard_map/jit(cholesky)/cholesky | solution.py:88
  671.1 9.8 %custom-call.23 = f32[1,128,128]{1,2,0:T(8,128)S(1)} custom-call(f32[1,128,128]{2,1,0:T(8,128)S(1)} %fusion.70), custom_call_target="InvertDiagBlocksLowerTriangular" | custom-call | tf_op jit(solution)/shard_map/triangular_solve/custom-call.0 | solution.py:90
  681.8 11.7 %cholesky.253 = f32[128,128]{1,0:T(8,128)S(1)} custom-call(f32[128,128]{1,0:T(8,128)S(1)} %select_add_fusion.1), custom_call_target="Cholesky" | custom-call | tf_op jit(solution)/shard_map/jit(cholesky)/cholesky | solution.py:88
  694.8 9.8 %custom-call.24 = f32[1,128,128]{1,2,0:T(8,128)S(1)} custom-call(f32[1,128,128]{2,1,0:T(8,128)S(1)} %fusion.71), custom_call_target="InvertDiagBlocksLowerTriangular" | custom-call | tf_op jit(solution)/shard_map/triangular_solve/custom-call.0 | solution.py:90
  721.8 60.0 %all-gather.6.cloned.1.call-done = f32[9216,128]{1,0:T(8,128)} async-done(((f32[1152,128]{1,0:T(8,128)}), f32[9216,128]{1,0:T(8,128)}) %all-gather.6.cloned.1.call-update) | async-done | bytes 4718608 | tf_op jit(solution)/shard_map/all_gather | solution.py:172
  781.8 4.9 copy.113
  (150 shorter events, 73.9 us)
Async XLA Ops:
  7.8 16.9 %all-to-all-start = ((s32[8,1,4]{2,1,0:T(1,128)}), s32[8,1,4]{2,1,0:T(1,128)S(1)}, u32[]{:S(2)}, u32[]{:S(2)}) async-start(s32[8,1,4]{2,1,0:T(1,128)} %broadcast_in_dim.67), calls=%async_computation | async-start | bytes 8192 | tf_op jit(solution)/shard_map/all_to_all | solution.py:148
  24.7 99.2 %all-to-all-start.1 = ((bf16[8,512,512]{2,1,0:T(8,128)(2,1)}), bf16[8,512,512]{2,1,0:T(8,128)(2,1)}, u32[]{:S(2)}, u32[]{:S(2)}) async-start(bf16[8,512,512]{2,1,0:T(8,128)(2,1)} %broadcast_select_fusion), calls=%async_computation.1 | async-start | bytes 8388608 | tf_op jit(solution)/shard_map/all_to_all | solution.py:147
  29.8 202.2 %reduce-scatter.4.cloned.1.call-start = ((), (), s32[]{:S(2)}) async-start(), calls=%async_computation.5 | async-start | bytes 4587520 | tf_op jit(solution)/shard_map/reduce_scatter | solution.py:166
  153.9 22.7 %copy-start.2 = (s32[55]{0:T(128)S(1)}, s32[55]{0:T(128)}, u32[]{:S(2)}) copy-start(s32[55]{0:T(128)} %constant.760) | copy-start | bytes 664
  182.0 145.5 %copy-start.3 = (s32[90]{0:T(128)S(1)}, s32[90]{0:T(128)}, u32[]{:S(2)}) copy-start(s32[90]{0:T(128)} %constant.761) | copy-start | bytes 1084
  186.4 86.0 %reduce-scatter.6.cloned.1.call-start = ((), (), s32[]{:S(2)}) async-start(), calls=%async_computation.6 | async-start | bytes 1376256 | tf_op jit(solution)/shard_map/reduce_scatter | solution.py:166
  232.0 60.9 %reduce-scatter.8.cloned.1.call-start = ((), (), s32[]{:S(2)}) async-start(), calls=%async_computation.7 | async-start | bytes 573440 | tf_op jit(solution)/shard_map/reduce_scatter | solution.py:166
  272.4 105.3 %all-gather.4.cloned.1.call-start = ((), (), s32[]{:S(2)}) async-start(), calls=%async_computation.8 | async-start | bytes 4587520 | tf_op jit(solution)/shard_map/all_gather | solution.py:169
  327.5 454.3 %all-gather.6.cloned.1.call-start = ((), (), s32[]{:S(2)}) async-start(), calls=%async_computation.9 | async-start | bytes 5308416 | tf_op jit(solution)/shard_map/all_gather | solution.py:172
  451.6 2.2 copy-start
  486.4 1.8 copy-start.1
Sparse Core Ops, SparseCore 0:
  186.5 45.4 reduce-scatter.3
  234.5 37.8 reduce-scatter.5
  275.1 17.8 reduce-scatter.7
  327.6 49.9 all-gather.3
  721.9 59.8 all-gather.5

commit v4 on v3

--- a/solution.py
+++ b/solution.py
@@ -162,10 +162,10 @@
     chunk = padded * block // n_replicas
     packed = packed.reshape(n_replicas, chunk, block)
     mine = packed.reshape(padded * block, block)
-    for axis in DP_AXES[::-1]:
+    for axis in SCATTER_ORDER:
         mine = lax.psum_scatter(mine, axis, scatter_dimension=0, tiled=True)
     gathered = mine
-    for axis in DP_AXES:
+    for axis in SCATTER_ORDER[::-1]:
         gathered = lax.all_gather(gathered, axis, axis=0, tiled=True)
     gathered = gathered.reshape(padded, block, block)
     results = precondition_blocks(gathered, nb, total_rows)[None]
@@ -173,6 +173,7 @@
 
 
 DP_AXES = ("dp_x", "dp_z", "dp_y")
+SCATTER_ORDER = ("dp_y", "dp_x", "dp_z")
 
 
 def solution(mesh):

time: 802 us -> 780 us (0.973)
  waiting for transfers between devices: 310 us -> 295 us
    all_gather x2, blocking collectives: 34.5 us -> 26.5 us  [body(): gathered = lax.all_gather(gathered, axis, axis=0, tiled=True)]
where the time goes in v4:
time: 780 us; the launch traced here: 771 us
  waiting for transfers between devices  295 us (38%)
  other arithmetic  256 us (33%)
  matrix products  85.5 us (11%)
  local copies, waits for them, and re-layouts  81.5 us (10%)
  blocking collectives  26.5 us (3%)
  between operations  14.3 us (2%)
  starting transfers between devices  11.2 us (1%)
    another operation x30, other arithmetic, _chol_inv(): lower = jnp.linalg.cholesky(block, symmetrize_input=False)  125 us
    another operation x15, other arithmetic, _chol_inv(): lax.linalg.triangular_solve(lower, eye, left_side=True, lower=True)  103 us
    reduce_scatter x3, waiting for transfers between devices, body(): mine = lax.psum_scatter(mine, axis, scatter_dimension=0, tiled=True)  98.6 us
    all_to_all x1, waiting for transfers between devices, body(): lax.all_to_all(ordered, 'owner', split_axis=0, concat_axis=1, tiled=True)  93.7 us
    all_gather x1, waiting for transfers between devices, body(): return lax.all_gather(results, 'owner', axis=0, tiled=True)  60 us
    dot_general x18, matrix products, _mm_nt(): lax.dot_general(a, b, (((1,), (1,)), ((), ())), precision=HIGH, preferred...  44.6 us
    all_gather x1, waiting for transfers between devices, body(): gathered = lax.all_gather(gathered, axis, axis=0, tiled=True)  43 us
    all_gather x2, blocking collectives, body(): gathered = lax.all_gather(gathered, axis, axis=0, tiled=True)  26.5 us
  transfers between devices with their start and end apart: 7, of which 6 were waited for; matrix products, arithmetic and copies ran while one was open for 1% of the time, Pallas kernels for 0%

profile of v4, /device:TPU:2, one launch (start us, length us, event | category | flops | bytes accessed | tf_op | source)
XLA Modules:
  0.0 770.8 jit_solution(15448216205919539234)
XLA Ops:
  7.8 5.9 all-to-all-start
  15.0 5.0 gather_fusion
  20.0 4.7 broadcast_select_fusion
  24.7 5.1 all-to-all-start.1
  30.2 93.7 %all-to-all-done.1 = bf16[8,512,512]{2,1,0:T(8,128)(2,1)} async-done(((bf16[8,512,512]{2,1,0:T(8,128)(2,1)}), bf16[8,512,512]{2,1,0:T(8,128)(2,1)}, u32[]{:S(2)}, u32[]{:S(2)}) %all-to-all-start.1) | async-done | bytes 4194336 | tf_op jit(solution)/shard_map/all_to_all | solution.py:147
  127.5 3.9 fusion.101
  133.6 6.0 fusion
  139.5 14.3 %copy.37 = bf16[1280,4096]{1,0:T(8,128)(2,1)} copy(bf16[1280,4096]{0,1:T(8,128)(2,1)} %fusion) | data formatting | bytes 20971520 | tf_op jit(solution)/shard_map/dot_general | solution.py:153
  153.9 22.7 %convolution_bitcast_fusion = f32[10,10,128,128]{3,2,1,0:T(8,128)} fusion(bf16[10,128,4096,1]{2,1,3,0:T(8,128)(2,1)} %bitcast.176, bf16[10,128,4096,1]{2,1,0,3:T(8,128)(2,1)} %bitcast.177), kind=kOutput, calls=%fused_computation.13 | convolution fusion | flops 13421772800 | bytes 27525120 | tf_op jit(solution)/shard_map/dot_general | solution.py:153
  176.6 5.5 gather_fusion.1
  182.0 4.3 concatenate.110
  186.4 45.5 %reduce-scatter.4.cloned.1.call-done = f32[1792,128]{1,0:T(8,128)} async-done(((f32[7168,128]{1,0:T(8,128)}), f32[1792,128]{1,0:T(8,128)}) %reduce-scatter.4.cloned.1.call-update) | async-done | bytes 917520 | tf_op jit(solution)/shard_map/reduce_scatter | solution.py:166
  232.1 25.5 %reduce-scatter.6.cloned.1.call-done = f32[448,128]{1,0:T(8,128)} async-done(((f32[1792,128]{1,0:T(8,128)}), f32[448,128]{1,0:T(8,128)}) %reduce-scatter.6.cloned.1.call-update) | async-done | bytes 229392 | tf_op jit(solution)/shard_map/reduce_scatter | solution.py:166
  257.6 27.6 %reduce-scatter.8.cloned.1.call-done = f32[224,128]{1,0:T(8,128)} async-done(((f32[448,128]{1,0:T(8,128)}), f32[224,128]{1,0:T(8,128)}) %reduce-scatter.8.cloned.1.call-update) | async-done | bytes 114704 | tf_op jit(solution)/shard_map/reduce_scatter | solution.py:166
  285.2 12.2 %all_gather.12 = f32[448,128]{1,0:T(8,128)S(1)} all-gather(f32[224,128]{1,0:T(8,128)} %reduce-scatter.8.cloned.1.call-done), channel_id=1, replica_groups=mesh['dp_x'=4,'dp_z'=2,'dp_y'=4,'owner'=8] {'dp_z'}, dimensions={0}, use_global_device_ids=true | all-gather | bytes 344064 | tf_op jit(solution)/shard_map/all_gather | solution.py:169
  297.4 14.3 %all_gather.13 = f32[1792,128]{1,0:T(8,128)} all-gather(f32[448,128]{1,0:T(8,128)S(1)} %all_gather.12), channel_id=1, replica_groups=mesh['dp_x'=4,'dp_z'=2,'dp_y'=4,'owner'=8] {'dp_x'}, dimensions={0}, use_global_device_ids=true | all-gather | bytes 1146880 | tf_op jit(solution)/shard_map/all_gather | solution.py:169
  311.8 43.0 %all-gather.4.cloned.1.call-done = f32[7168,128]{1,0:T(8,128)} async-done(((f32[1792,128]{1,0:T(8,128)}), f32[7168,128]{1,0:T(8,128)}) %all-gather.4.cloned.1.call-update) | async-done | bytes 3670032 | tf_op jit(solution)/shard_map/all_gather | solution.py:169
  354.8 5.5 gather_fusion.2
  360.3 6.3 broadcast_multiply_fusion
  366.6 9.8 %copy.38 = f32[10,128,9,128]{1,0,3,2:T(8,128)} copy(f32[10,128,9,128]{3,1,2,0:T(8,128)} %bitcast.171) | data formatting | bytes 11796480 | tf_op jit(solution)/shard_map/mul | solution.py:102
  376.5 9.2 %copy.61 = f32[144,8,10,128]{3,1,2,0:T(8,128)} copy(f32[144,8,10,128]{3,2,1,0:T(8,128)} %bitcast.168) | data formatting | bytes 11796480
  385.6 7.7 copy.39
  394.2 11.7 %cholesky.165 = f32[128,128]{1,0:T(8,128)S(1)} custom-call(f32[128,128]{1,0:T(8,128)S(1)} %select_add_fusion.9), custom_call_target="Cholesky" | custom-call | tf_op jit(solution)/shard_map/jit(cholesky)/cholesky | solution.py:88
  407.9 9.8 %custom-call.16 = f32[1,128,128]{1,2,0:T(8,128)S(1)} custom-call(f32[1,128,128]{2,1,0:T(8,128)S(1)} %get-tuple-element.334), custom_call_target="InvertDiagBlocksLowerTriangular" | custom-call | tf_op jit(solution)/shard_map/triangular_solve/custom-call.0 | solution.py:90
  421.0 7.7 %constant_dynamic-update-slice_fusion.45 = (f32[1280,1152]{1,0:T(8,128)}, f32[1152,1024]{1,0:T(8,128)S(1)}) fusion(f32[1280,1152]{1,0:T(8,128)} %get-tuple-element.335, f32[1152,128]{1,0:T(8,128)S(1)} %get-tuple-element.336), kind=kOutput, calls=%fused_computation.236 | convolution fusion | flops 1814298624 | bytes 15269888 | tf_op jit(solution)/shard_map/dot_general | solution.py:83
  430.9 11.7 %cholesky.176 = f32[128,128]{1,0:T(8,128)S(1)} custom-call(f32[128,128]{1,0:T(8,128)S(1)} %select_add_fusion.8), custom_call_target="Cholesky" | custom-call | tf_op jit(solution)/shard_map/jit(cholesky)/cholesky | solution.py:88
  444.7 9.8 %custom-call.17 = f32[1,128,128]{1,2,0:T(8,128)S(1)} custom-call(f32[1,128,128]{2,1,0:T(8,128)S(1)} %get-tuple-element.332), custom_call_target="InvertDiagBlocksLowerTriangular" | custom-call | tf_op jit(solution)/shard_map/triangular_solve/custom-call.0 | solution.py:90
  457.3 6.2 constant_dynamic-update-slice_fusion.43
  465.4 11.7 %cholesky.187 = f32[128,128]{1,0:T(8,128)S(1)} custom-call(f32[128,128]{1,0:T(8,128)S(1)} %select_add_fusion.7), custom_call_target="Cholesky" | custom-call | tf_op jit(solution)/shard_map/jit(cholesky)/cholesky | solution.py:88
  479.2 9.8 %custom-call.18 = f32[1,128,128]{1,2,0:T(8,128)S(1)} custom-call(f32[1,128,128]{2,1,0:T(8,128)S(1)} %get-tuple-element.330), custom_call_target="InvertDiagBlocksLowerTriangular" | custom-call | tf_op jit(solution)/shard_map/triangular_solve/custom-call.0 | solution.py:90
  491.7 5.7 constant_dynamic-update-slice_fusion.41
  497.5 11.9 %cholesky.198 = f32[128,128]{1,0:T(8,128)S(1)} custom-call(f32[128,128]{1,0:T(8,128)S(1)} %select_add_fusion.6), custom_call_target="Cholesky" | custom-call | tf_op jit(solution)/shard_map/jit(cholesky)/cholesky | solution.py:88
  511.3 9.8 %custom-call.19 = f32[1,128,128]{1,2,0:T(8,128)S(1)} custom-call(f32[1,128,128]{2,1,0:T(8,128)S(1)} %get-tuple-element.328), custom_call_target="InvertDiagBlocksLowerTriangular" | custom-call | tf_op jit(solution)/shard_map/triangular_solve/custom-call.0 | solution.py:90
  522.7 4.6 constant_dynamic-update-slice_fusion.39
  527.4 11.7 %cholesky.209 = f32[128,128]{1,0:T(8,128)S(1)} custom-call(f32[128,128]{1,0:T(8,128)S(1)} %select_add_fusion.5), custom_call_target="Cholesky" | custom-call | tf_op jit(solution)/shard_map/jit(cholesky)/cholesky | solution.py:88
  541.1 9.8 %custom-call.20 = f32[1,128,128]{1,2,0:T(8,128)S(1)} custom-call(f32[1,128,128]{2,1,0:T(8,128)S(1)} %get-tuple-element.326), custom_call_target="InvertDiagBlocksLowerTriangular" | custom-call | tf_op jit(solution)/shard_map/triangular_solve/custom-call.0 | solution.py:90
  556.6 11.7 %cholesky.220 = f32[128,128]{1,0:T(8,128)S(1)} custom-call(f32[128,128]{1,0:T(8,128)S(1)} %select_add_fusion.4), custom_call_target="Cholesky" | custom-call | tf_op jit(solution)/shard_map/jit(cholesky)/cholesky | solution.py:88
  570.2 9.8 %custom-call.21 = f32[1,128,128]{1,2,0:T(8,128)S(1)} custom-call(f32[1,128,128]{2,1,0:T(8,128)S(1)} %get-tuple-element.323), custom_call_target="InvertDiagBlocksLowerTriangular" | custom-call | tf_op jit(solution)/shard_map/triangular_solve/custom-call.0 | solution.py:90
  585.3 11.9 %cholesky.264 = f32[128,128]{1,0:T(8,128)S(1)} custom-call(f32[128,128]{1,0:T(8,128)S(1)} %select_add_fusion), custom_call_target="Cholesky" | custom-call | tf_op jit(solution)/shard_map/jit(cholesky)/cholesky | solution.py:88
  598.5 9.8 %custom-call.25 = f32[1,128,128]{1,2,0:T(8,128)S(1)} custom-call(f32[1,128,128]{2,1,0:T(8,128)S(1)} %fusion.72), custom_call_target="InvertDiagBlocksLowerTriangular" | custom-call | tf_op jit(solution)/shard_map/triangular_solve/custom-call.0 | solution.py:90
  608.6 11.7 %cholesky.231 = f32[128,128]{1,0:T(8,128)S(1)} custom-call(f32[128,128]{1,0:T(8,128)S(1)} %select_add_fusion.3), custom_call_target="Cholesky" | custom-call | tf_op jit(solution)/shard_map/jit(cholesky)/cholesky | solution.py:88
  622.3 9.8 %custom-call.22 = f32[1,128,128]{1,2,0:T(8,128)S(1)} custom-call(f32[1,128,128]{2,1,0:T(8,128)S(1)} %get-tuple-element.321), custom_call_target="InvertDiagBlocksLowerTriangular" | custom-call | tf_op jit(solution)/shard_map/triangular_solve/custom-call.0 | solution.py:90
  634.9 11.9 %cholesky.242 = f32[128,128]{1,0:T(8,128)S(1)} custom-call(f32[128,128]{1,0:T(8,128)S(1)} %select_add_fusion.2), custom_call_target="Cholesky" | custom-call | tf_op jit(solution)/shard_map/jit(cholesky)/cholesky | solution.py:88
  648.2 9.8 %custom-call.23 = f32[1,128,128]{1,2,0:T(8,128)S(1)} custom-call(f32[1,128,128]{2,1,0:T(8,128)S(1)} %fusion.70), custom_call_target="InvertDiagBlocksLowerTriangular" | custom-call | tf_op jit(solution)/shard_map/triangular_solve/custom-call.0 | solution.py:90
  658.9 11.7 %cholesky.253 = f32[128,128]{1,0:T(8,128)S(1)} custom-call(f32[128,128]{1,0:T(8,128)S(1)} %select_add_fusion.1), custom_call_target="Cholesky" | custom-call | tf_op jit(solution)/shard_map/jit(cholesky)/cholesky | solution.py:88
  671.9 9.8 %custom-call.24 = f32[1,128,128]{1,2,0:T(8,128)S(1)} custom-call(f32[1,128,128]{2,1,0:T(8,128)S(1)} %fusion.71), custom_call_target="InvertDiagBlocksLowerTriangular" | custom-call | tf_op jit(solution)/shard_map/triangular_solve/custom-call.0 | solution.py:90
  698.9 60.0 %all-gather.6.cloned.1.call-done = f32[9216,128]{1,0:T(8,128)} async-done(((f32[1152,128]{1,0:T(8,128)}), f32[9216,128]{1,0:T(8,128)}) %all-gather.6.cloned.1.call-update) | async-done | bytes 4718608 | tf_op jit(solution)/shard_map/all_gather | solution.py:172
  758.9 4.9 copy.113
  (150 shorter events, 73.9 us)
Async XLA Ops:
  7.8 16.9 %all-to-all-start = ((s32[8,1,4]{2,1,0:T(1,128)}), s32[8,1,4]{2,1,0:T(1,128)S(1)}, u32[]{:S(2)}, u32[]{:S(2)}) async-start(s32[8,1,4]{2,1,0:T(1,128)} %broadcast_in_dim.67), calls=%async_computation | async-start | bytes 8192 | tf_op jit(solution)/shard_map/all_to_all | solution.py:148
  24.7 99.2 %all-to-all-start.1 = ((bf16[8,512,512]{2,1,0:T(8,128)(2,1)}), bf16[8,512,512]{2,1,0:T(8,128)(2,1)}, u32[]{:S(2)}, u32[]{:S(2)}) async-start(bf16[8,512,512]{2,1,0:T(8,128)(2,1)} %broadcast_select_fusion), calls=%async_computation.1 | async-start | bytes 8388608 | tf_op jit(solution)/shard_map/all_to_all | solution.py:147
  29.8 202.2 %reduce-scatter.4.cloned.1.call-start = ((), (), s32[]{:S(2)}) async-start(), calls=%async_computation.5 | async-start | bytes 4587520 | tf_op jit(solution)/shard_map/reduce_scatter | solution.py:166
  153.9 22.7 %copy-start.2 = (s32[55]{0:T(128)S(1)}, s32[55]{0:T(128)}, u32[]{:S(2)}) copy-start(s32[55]{0:T(128)} %constant.760) | copy-start | bytes 664
  182.0 129.7 %copy-start.3 = (s32[90]{0:T(128)S(1)}, s32[90]{0:T(128)}, u32[]{:S(2)}) copy-start(s32[90]{0:T(128)} %constant.761) | copy-start | bytes 1084
  186.4 71.1 %reduce-scatter.6.cloned.1.call-start = ((), (), s32[]{:S(2)}) async-start(), calls=%async_computation.6 | async-start | bytes 1146880 | tf_op jit(solution)/shard_map/reduce_scatter | solution.py:166
  232.0 53.2 %reduce-scatter.8.cloned.1.call-start = ((), (), s32[]{:S(2)}) async-start(), calls=%async_computation.7 | async-start | bytes 344064 | tf_op jit(solution)/shard_map/reduce_scatter | solution.py:166
  257.5 97.3 %all-gather.4.cloned.1.call-start = ((), (), s32[]{:S(2)}) async-start(), calls=%async_computation.8 | async-start | bytes 4587520 | tf_op jit(solution)/shard_map/all_gather | solution.py:169
  311.7 447.2 %all-gather.6.cloned.1.call-start = ((), (), s32[]{:S(2)}) async-start(), calls=%async_computation.9 | async-start | bytes 5308416 | tf_op jit(solution)/shard_map/all_gather | solution.py:172
  428.7 2.2 copy-start
  463.5 1.8 copy-start.1
Sparse Core Ops, SparseCore 0:
  186.5 45.4 reduce-scatter.3
  234.6 22.9 reduce-scatter.5
  260.0 25.1 reduce-scatter.7
  311.8 42.9 all-gather.3
  699.0 59.8 all-gather.5

commit v5 on v4

--- a/solution.py
+++ b/solution.py
@@ -2,6 +2,8 @@
 import jax
 import jax.numpy as jnp
 from jax import lax
+from jax.experimental import pallas as pl
+from jax.experimental.pallas import tpu as pltpu
 from jax.sharding import PartitionSpec as P
 
 damping = 0.1
@@ -91,6 +93,45 @@
     return lower, inverse
 
 
+def _leaf_kernel(a_ref, w_ref, s_ref):
+    n = a_ref.shape[0]
+    s_ref[...] = a_ref[...]
+    sub = lax.broadcasted_iota(jnp.int32, (n, n), 0)
+    lane = lax.broadcasted_iota(jnp.int32, (n, n), 1)
+    w_ref[...] = jnp.where(sub == lane, 1.0, 0.0).astype(jnp.float32)
+    lane_row = lax.broadcasted_iota(jnp.int32, (1, n), 1)
+    sub_col = lax.broadcasted_iota(jnp.int32, (n, 1), 0)
+
+    def step(j, carry):
+        a = s_ref[...]
+        row = s_ref[pl.ds(j, 1), :]
+        pivot = jnp.sum(jnp.where(lane_row == j, row, 0.0), axis=1, keepdims=True)
+        inv_root = 1.0 / jnp.sqrt(pivot)
+        col = jnp.sum(jnp.where(lane == j, a, 0.0), axis=1, keepdims=True)
+        lcol = jnp.where(sub_col > j, col * inv_root, 0.0)
+        lrow = jnp.where(lane_row >= j, row * inv_root, 0.0)
+        s_ref[...] = a - lcol * lrow
+        wrow = w_ref[pl.ds(j, 1), :] * inv_root
+        w_ref[...] = w_ref[...] - lcol * wrow
+        w_ref[pl.ds(j, 1), :] = wrow
+        return carry
+
+    lax.fori_loop(0, n, step, 0)
+
+
+def _chol_inverse(block):
+    n = block.shape[0]
+    return pl.pallas_call(
+        _leaf_kernel,
+        out_shape=jax.ShapeDtypeStruct((n, n), jnp.float32),
+        in_specs=[pl.BlockSpec(memory_space=pltpu.VMEM)],
+        out_specs=pl.BlockSpec(memory_space=pltpu.VMEM),
+        scratch_shapes=[pltpu.VMEM((n, n), jnp.float32)],
+        cost_estimate=pl.CostEstimate(flops=6 * n * n * n, bytes_accessed=8 * n * n,
+                                      transcendentals=n),
+    )(block)
+
+
 def precondition_blocks(blocks, nb, total_rows):
     block = blocks.shape[-1]
     na = nb - 1
@@ -108,10 +149,9 @@
         lo = k * block
         hi = lo + block
         diag = work[lo:hi, lo:hi] + damping * eye
-        lower, inverse = _chol_inv(diag)
+        inverse = _chol_inverse(diag)
         inverses.append(inverse)
         panel = _mm_nt(work[hi:, lo:hi], inverse)
-        work = work.at[lo:hi, lo:hi].set(lower)
         work = work.at[hi:, lo:hi].set(panel)
         if k + 1 < na:
             update = _mm_nt(panel, panel[: (na - k - 1) * block])
@@ -127,7 +167,7 @@
             rhs = rhs - _mm_t(work[hi:na * block, lo:hi], below)
         pieces[k] = _mm_t(inverses[k], rhs)
     left_solved = jnp.concatenate(pieces, axis=0)
-    _, grad_inverse = _chol_inv(grad_factor)
+    grad_inverse = _chol_inverse(grad_factor)
     return _mm(_mm_nt(left_solved, grad_inverse), grad_inverse)
 
 

time: 780 us -> 712 us (0.913)
  other arithmetic: 256 us -> 28.9 us
  Pallas kernels: 0 us -> 157 us
    another operation x45 -> x0, other arithmetic: 227 us -> none  [the longest x30 125 us: _chol_inv(): lower = jnp.linalg.cholesky(block, symmetrize_input=False)]
    pallas_call x0 -> x10, Pallas kernels: none -> 157 us  [_chol_inverse(): pl.pallas_call(_leaf_kernel, out_shape=jax.ShapeDtypeStruct((n, n), jnp.f...]
    unnamed x36 -> x50, local copies, waits for them, and re-layouts: 18.3 us -> 18.3 us
  transfers between devices with their start and end apart: 7 -> 7, of which waited for: 6 -> 6; matrix products, arithmetic and copies ran while one was open for 1% -> 2% of each run, Pallas kernels for 0% -> 0%
where the time goes in v5:
time: 712 us; the launch traced here: 703 us
  waiting for transfers between devices  295 us (41%)
  Pallas kernels  157 us (22%)
  matrix products  89 us (12%)
  local copies, waits for them, and re-layouts  81.2 us (11%)
  other arithmetic  28.9 us (4%)
  blocking collectives  26.5 us (4%)
  between operations  14.2 us (2%)
  starting transfers between devices  11.4 us (2%)
    pallas_call x10, Pallas kernels, _chol_inverse(): pl.pallas_call(_leaf_kernel, out_shape=jax.ShapeDtypeStruct((n, n), jnp.f...  157 us
    reduce_scatter x3, waiting for transfers between devices, body(): mine = lax.psum_scatter(mine, axis, scatter_dimension=0, tiled=True)  98.7 us
    all_to_all x1, waiting for transfers between devices, body(): lax.all_to_all(ordered, 'owner', split_axis=0, concat_axis=1, tiled=True)  93.7 us
    all_gather x1, waiting for transfers between devices, body(): return lax.all_gather(results, 'owner', axis=0, tiled=True)  60 us
    dot_general x18, matrix products, _mm_nt(): lax.dot_general(a, b, (((1,), (1,)), ((), ())), precision=HIGH, preferred...  48.6 us
    all_gather x1, waiting for transfers between devices, body(): gathered = lax.all_gather(gathered, axis, axis=0, tiled=True)  42.9 us
    all_gather x2, blocking collectives, body(): gathered = lax.all_gather(gathered, axis, axis=0, tiled=True)  26.5 us
    dot_general x1, matrix products, body(): gram = jnp.dot(columns.T, columns, preferred_element_type=jnp.float32)  22.7 us
  transfers between devices with their start and end apart: 7, of which 6 were waited for; matrix products, arithmetic and copies ran while one was open for 2% of the time, Pallas kernels for 0%

profile of v5, /device:TPU:2, one launch (start us, length us, event | category | flops | bytes accessed | tf_op | source)
XLA Modules:
  0.0 702.9 jit_solution(5964608055906689408)
XLA Ops:
  7.8 5.9 all-to-all-start
  15.0 5.0 gather_fusion
  20.0 4.7 broadcast_select_fusion
  24.7 5.1 all-to-all-start.1
  30.2 93.7 %all-to-all-done.1 = bf16[8,512,512]{2,1,0:T(8,128)(2,1)} async-done(((bf16[8,512,512]{2,1,0:T(8,128)(2,1)}), bf16[8,512,512]{2,1,0:T(8,128)(2,1)}, u32[]{:S(2)}, u32[]{:S(2)}) %all-to-all-start.1) | async-done | bytes 4194336 | tf_op jit(solution)/shard_map/all_to_all | solution.py:187
  125.2 2.3 slice.627
  127.5 3.9 fusion.60
  131.3 2.2 pad_select_fusion
  133.6 6.0 fusion
  139.6 14.2 %copy.37 = bf16[1280,4096]{1,0:T(8,128)(2,1)} copy(bf16[1280,4096]{0,1:T(8,128)(2,1)} %fusion) | data formatting | bytes 20971520 | tf_op jit(solution)/shard_map/dot_general | solution.py:193
  153.9 22.7 %convolution_bitcast_fusion = f32[10,10,128,128]{3,2,1,0:T(8,128)} fusion(bf16[10,128,4096,1]{2,1,3,0:T(8,128)(2,1)} %bitcast.126, bf16[10,128,4096,1]{2,1,0,3:T(8,128)(2,1)} %bitcast.127), kind=kOutput, calls=%fused_computation.13 | convolution fusion | flops 13421772800 | bytes 27525120 | tf_op jit(solution)/shard_map/dot_general | solution.py:193
  176.6 5.5 gather_fusion.1
  182.1 4.3 concatenate.92
  186.5 45.5 %reduce-scatter.4.cloned.1.call-done = f32[1792,128]{1,0:T(8,128)} async-done(((f32[7168,128]{1,0:T(8,128)}), f32[1792,128]{1,0:T(8,128)}) %reduce-scatter.4.cloned.1.call-update) | async-done | bytes 917520 | tf_op jit(solution)/shard_map/reduce_scatter | solution.py:206
  232.0 25.5 %reduce-scatter.6.cloned.1.call-done = f32[448,128]{1,0:T(8,128)} async-done(((f32[1792,128]{1,0:T(8,128)}), f32[448,128]{1,0:T(8,128)}) %reduce-scatter.6.cloned.1.call-update) | async-done | bytes 229392 | tf_op jit(solution)/shard_map/reduce_scatter | solution.py:206
  257.6 27.7 %reduce-scatter.8.cloned.1.call-done = f32[224,128]{1,0:T(8,128)} async-done(((f32[448,128]{1,0:T(8,128)}), f32[224,128]{1,0:T(8,128)}) %reduce-scatter.8.cloned.1.call-update) | async-done | bytes 114704 | tf_op jit(solution)/shard_map/reduce_scatter | solution.py:206
  285.3 12.1 %all_gather.12 = f32[448,128]{1,0:T(8,128)S(1)} all-gather(f32[224,128]{1,0:T(8,128)} %reduce-scatter.8.cloned.1.call-done), channel_id=1, replica_groups=mesh['dp_x'=4,'dp_z'=2,'dp_y'=4,'owner'=8] {'dp_z'}, dimensions={0}, use_global_device_ids=true | all-gather | bytes 344064 | tf_op jit(solution)/shard_map/all_gather | solution.py:209
  297.4 14.3 %all_gather.13 = f32[1792,128]{1,0:T(8,128)} all-gather(f32[448,128]{1,0:T(8,128)S(1)} %all_gather.12), channel_id=1, replica_groups=mesh['dp_x'=4,'dp_z'=2,'dp_y'=4,'owner'=8] {'dp_x'}, dimensions={0}, use_global_device_ids=true | all-gather | bytes 1146880 | tf_op jit(solution)/shard_map/all_gather | solution.py:209
  312.0 42.9 %all-gather.4.cloned.1.call-done = f32[7168,128]{1,0:T(8,128)} async-done(((f32[1792,128]{1,0:T(8,128)}), f32[7168,128]{1,0:T(8,128)}) %all-gather.4.cloned.1.call-update) | async-done | bytes 3670032 | tf_op jit(solution)/shard_map/all_gather | solution.py:209
  354.9 5.5 gather_fusion.2
  360.4 6.3 broadcast_multiply_fusion
  366.7 9.6 %copy.38 = f32[10,128,9,128]{1,0,3,2:T(8,128)} copy(f32[10,128,9,128]{3,1,2,0:T(8,128)} %bitcast.121) | data formatting | bytes 11796480 | tf_op jit(solution)/shard_map/mul | solution.py:143
  376.3 9.1 %copy.61 = f32[144,8,10,128]{3,1,2,0:T(8,128)} copy(f32[144,8,10,128]{3,2,1,0:T(8,128)} %bitcast.118) | data formatting | bytes 11796480
  385.5 7.7 %copy.39 = f32[1280,1152]{1,0:T(8,128)} copy(f32[1280,1152]{0,1:T(8,128)} %bitcast.119) | data formatting | bytes 11796480 | tf_op jit(solution)/shard_map/reshape | solution.py:144
  394.6 15.7 %shard_map.91 = f32[128,128]{1,0:T(8,128)} custom-call(f32[128,128]{1,0:T(8,128)} %select_add_fusion.9.a_ref), custom_call_target="tpu_custom_call" | custom-call | flops 12582912 | bytes 131072 | tf_op jit(solution)/shard_map/pallas_call | solution.py:124
  410.3 3.0 constant_dynamic-update-slice_fusion.46
  413.3 7.3 %constant_dynamic-update-slice_fusion.45 = (f32[1280,1152]{1,0:T(8,128)}, f32[1152,1024]{1,0:T(8,128)S(1)}) fusion(f32[1280,1152]{1,0:T(8,128)} %get-tuple-element.211, f32[1152,128]{1,0:T(8,128)S(1)} %get-tuple-element.212), kind=kOutput, calls=%fused_computation.158 | convolution fusion | flops 1814298624 | bytes 15269888 | tf_op jit(solution)/shard_map/dot_general | solution.py:85
  420.6 2.2 copy-done
  423.5 15.7 %shard_map.92 = f32[128,128]{1,0:T(8,128)} custom-call(f32[128,128]{1,0:T(8,128)} %select_add_fusion.8.a_ref), custom_call_target="tpu_custom_call" | custom-call | flops 12582912 | bytes 131072 | tf_op jit(solution)/shard_map/pallas_call | solution.py:124
  439.1 2.4 constant_dynamic-update-slice_fusion.44
  441.6 6.0 constant_dynamic-update-slice_fusion.43
  450.0 15.7 %shard_map.93 = f32[128,128]{1,0:T(8,128)} custom-call(f32[128,128]{1,0:T(8,128)} %select_add_fusion.7.a_ref), custom_call_target="tpu_custom_call" | custom-call | flops 12582912 | bytes 131072 | tf_op jit(solution)/shard_map/pallas_call | solution.py:124
  465.7 2.3 constant_dynamic-update-slice_fusion.42
  468.0 5.8 constant_dynamic-update-slice_fusion.41
  474.4 15.7 %shard_map.94 = f32[128,128]{1,0:T(8,128)} custom-call(f32[128,128]{1,0:T(8,128)} %select_add_fusion.6.a_ref), custom_call_target="tpu_custom_call" | custom-call | flops 12582912 | bytes 131072 | tf_op jit(solution)/shard_map/pallas_call | solution.py:124
  490.0 2.1 constant_dynamic-update-slice_fusion.40
  492.2 4.6 constant_dynamic-update-slice_fusion.39
  497.4 15.7 %shard_map.95 = f32[128,128]{1,0:T(8,128)} custom-call(f32[128,128]{1,0:T(8,128)} %select_add_fusion.5.a_ref), custom_call_target="tpu_custom_call" | custom-call | flops 12582912 | bytes 131072 | tf_op jit(solution)/shard_map/pallas_call | solution.py:124
  513.1 2.0 constant_dynamic-update-slice_fusion.38
  515.1 2.5 fusion.1
  519.5 15.7 %shard_map.96 = f32[128,128]{1,0:T(8,128)} custom-call(f32[128,128]{1,0:T(8,128)} %select_add_fusion.4.a_ref), custom_call_target="tpu_custom_call" | custom-call | flops 12582912 | bytes 131072 | tf_op jit(solution)/shard_map/pallas_call | solution.py:124
  542.3 15.7 %shard_map.100 = f32[128,128]{1,0:T(8,128)} custom-call(f32[128,128]{1,0:T(8,128)} %select_add_fusion.a_ref), custom_call_target="tpu_custom_call" | custom-call | flops 12582912 | bytes 131072 | tf_op jit(solution)/shard_map/pallas_call | solution.py:124
  557.9 15.7 %shard_map.97 = f32[128,128]{1,0:T(8,128)} custom-call(f32[128,128]{1,0:T(8,128)} %select_add_fusion.3.a_ref), custom_call_target="tpu_custom_call" | custom-call | flops 12582912 | bytes 131072 | tf_op jit(solution)/shard_map/pallas_call | solution.py:124
  577.6 15.7 %shard_map.98 = f32[128,128]{1,0:T(8,128)} custom-call(f32[128,128]{1,0:T(8,128)} %select_add_fusion.2.a_ref), custom_call_target="tpu_custom_call" | custom-call | flops 12582912 | bytes 131072 | tf_op jit(solution)/shard_map/pallas_call | solution.py:124
  595.3 15.7 %shard_map.99 = f32[128,128]{1,0:T(8,128)} custom-call(f32[128,128]{1,0:T(8,128)} %select_add_fusion.1.a_ref), custom_call_target="tpu_custom_call" | custom-call | flops 12582912 | bytes 131072 | tf_op jit(solution)/shard_map/pallas_call | solution.py:124
  626.4 2.1 convolution_subtract_fusion
  631.1 60.0 %all-gather.6.cloned.1.call-done = f32[9216,128]{1,0:T(8,128)} async-done(((f32[1152,128]{1,0:T(8,128)}), f32[9216,128]{1,0:T(8,128)}) %all-gather.6.cloned.1.call-update) | async-done | bytes 4718608 | tf_op jit(solution)/shard_map/all_gather | solution.py:212
  691.1 4.9 copy.106
  (114 shorter events, 43.1 us)
Async XLA Ops:
  7.8 16.9 %all-to-all-start = ((s32[8,1,4]{2,1,0:T(1,128)}), s32[8,1,4]{2,1,0:T(1,128)S(1)}, u32[]{:S(2)}, u32[]{:S(2)}) async-start(s32[8,1,4]{2,1,0:T(1,128)} %broadcast_in_dim.66), calls=%async_computation | async-start | bytes 8192 | tf_op jit(solution)/shard_map/all_to_all | solution.py:188
  24.7 99.2 %all-to-all-start.1 = ((bf16[8,512,512]{2,1,0:T(8,128)(2,1)}), bf16[8,512,512]{2,1,0:T(8,128)(2,1)}, u32[]{:S(2)}, u32[]{:S(2)}) async-start(bf16[8,512,512]{2,1,0:T(8,128)(2,1)} %broadcast_select_fusion), calls=%async_computation.1 | async-start | bytes 8388608 | tf_op jit(solution)/shard_map/all_to_all | solution.py:187
  29.8 202.2 %reduce-scatter.4.cloned.1.call-start = ((), (), s32[]{:S(2)}) async-start(), calls=%async_computation.5 | async-start | bytes 4587520 | tf_op jit(solution)/shard_map/reduce_scatter | solution.py:206
  153.9 22.7 %copy-start.2 = (s32[55]{0:T(128)S(1)}, s32[55]{0:T(128)}, u32[]{:S(2)}) copy-start(s32[55]{0:T(128)} %constant.541) | copy-start | bytes 664
  182.1 129.9 %copy-start.10 = (s32[90]{0:T(128)S(1)}, s32[90]{0:T(128)}, u32[]{:S(2)}) copy-start(s32[90]{0:T(128)} %constant.542) | copy-start | bytes 1084
  186.4 71.1 %reduce-scatter.6.cloned.1.call-start = ((), (), s32[]{:S(2)}) async-start(), calls=%async_computation.6 | async-start | bytes 1146880 | tf_op jit(solution)/shard_map/reduce_scatter | solution.py:206
  232.0 53.3 %reduce-scatter.8.cloned.1.call-start = ((), (), s32[]{:S(2)}) async-start(), calls=%async_computation.7 | async-start | bytes 344064 | tf_op jit(solution)/shard_map/reduce_scatter | solution.py:206
  257.5 97.4 %all-gather.4.cloned.1.call-start = ((), (), s32[]{:S(2)}) async-start(), calls=%async_computation.8 | async-start | bytes 4587520 | tf_op jit(solution)/shard_map/all_gather | solution.py:209
  311.8 379.3 %all-gather.6.cloned.1.call-start = ((), (), s32[]{:S(2)}) async-start(), calls=%async_computation.9 | async-start | bytes 5308416 | tf_op jit(solution)/shard_map/all_gather | solution.py:212
  420.6 2.2 copy-start
  447.5 1.8 copy-start.1
  518.9 100.6 %copy-start.8 = (f32[128,128]{1,0:T(8,128)S(1)}, f32[128,128]{1,0:T(8,128)}, u32[]{:S(2)}) copy-start(f32[128,128]{1,0:T(8,128)} %shard_map.95) | copy-start | bytes 196612
  535.2 82.4 %copy-start.9 = (f32[128,128]{1,0:T(8,128)S(1)}, f32[128,128]{1,0:T(8,128)}, u32[]{:S(2)}) copy-start(f32[128,128]{1,0:T(8,128)} %shard_map.96) | copy-start | bytes 196612
  535.2 86.3 %copy-start.7 = (f32[128,128]{1,0:T(8,128)S(1)}, f32[128,128]{1,0:T(8,128)}, u32[]{:S(2)}) copy-start(f32[128,128]{1,0:T(8,128)} %shard_map.94) | copy-start | bytes 196612
  539.1 84.5 %copy-start.6 = (f32[128,128]{1,0:T(8,128)S(1)}, f32[128,128]{1,0:T(8,128)}, u32[]{:S(2)}) copy-start(f32[128,128]{1,0:T(8,128)} %shard_map.93) | copy-start | bytes 196612
  540.1 85.9 %copy-start.5 = (f32[128,128]{1,0:T(8,128)S(1)}, f32[128,128]{1,0:T(8,128)}, u32[]{:S(2)}) copy-start(f32[128,128]{1,0:T(8,128)} %shard_map.92) | copy-start | bytes 196612
  576.9 51.6 %copy-start.3 = (f32[128,128]{1,0:T(8,128)S(1)}, f32[128,128]{1,0:T(8,128)}, u32[]{:S(2)}) copy-start(f32[128,128]{1,0:T(8,128)} %shard_map.91) | copy-start | bytes 196612
  594.7 34.3 %copy-start.4 = (f32[128,128]{1,0:T(8,128)S(1)}, f32[128,128]{1,0:T(8,128)}, u32[]{:S(2)}) copy-start(f32[128,128]{1,0:T(8,128)} %shard_map.100) | copy-start | bytes 196612
Sparse Core Ops, SparseCore 0:
  186.6 45.3 reduce-scatter.3
  234.5 22.9 reduce-scatter.5
  260.0 25.2 reduce-scatter.7
  311.9 42.9 all-gather.3
  631.2 59.8 all-gather.5

commit v6 on v5

--- a/solution.py
+++ b/solution.py
@@ -47,7 +47,7 @@
 
 
 def _tri_pairs(nb):
-    return [(i, j) for i in range(nb) for j in range(i + 1)]
+    return [(i, j) for j in range(nb) for i in range(j, nb)]
 
 
 def pack_lower(gram, block):
@@ -136,12 +136,14 @@
     block = blocks.shape[-1]
     na = nb - 1
     index = {p: k for k, p in enumerate(_tri_pairs(nb))}
-    zero = len(index)
-    pick = np.array([[index[(i, j)] if i >= j else zero for j in range(na)] for i in range(nb)],
-                    dtype=np.int32)
     scale = 1.0 / total_rows
-    tiles = blocks[pick] * scale
-    work = tiles.transpose(0, 2, 1, 3).reshape(nb * block, na * block)
+    flat = blocks.reshape(-1, block)
+    panels = []
+    for j in range(na):
+        start = index[(j, j)] * block
+        panel = flat[start:start + (nb - j) * block]
+        panels.append(jnp.pad(panel, ((j * block, 0), (0, 0))))
+    work = jnp.concatenate(panels, axis=1) * scale
     eye = jnp.eye(block, dtype=blocks.dtype)
     grad_factor = blocks[index[(na, na)]] * scale + damping * eye
     inverses = []

time: 712 us -> 672 us (0.944); the launches traced: 703 us -> 670 us
  local copies, waits for them, and re-layouts: 81.2 us -> 56.5 us
    mul x1 -> x0, local copies, waits for them, and re-layouts: 9.64 us -> none  [precondition_blocks(): tiles = blocks[pick] * scale]
    reshape x1 -> x0, local copies, waits for them, and re-layouts: 7.68 us -> none  [precondition_blocks(): work = tiles.transpose(0, 2, 1, 3).reshape(nb * block, na * block)]
    unnamed x50 -> x57, local copies, waits for them, and re-layouts: 18.3 us -> 13.1 us
where the time goes in v6:
time: 672 us; the launch traced here: 670 us
  waiting for transfers between devices  295 us (44%)
  Pallas kernels  157 us (23%)
  matrix products  87.9 us (13%)
  local copies, waits for them, and re-layouts  56.5 us (8%)
  blocking collectives  26.5 us (4%)
  other arithmetic  22.2 us (3%)
  between operations  13.9 us (2%)
  starting transfers between devices  11.4 us (2%)
    pallas_call x10, Pallas kernels, _chol_inverse(): pl.pallas_call(_leaf_kernel, out_shape=jax.ShapeDtypeStruct((n, n), jnp.f...  157 us
    reduce_scatter x3, waiting for transfers between devices, body(): mine = lax.psum_scatter(mine, axis, scatter_dimension=0, tiled=True)  98.6 us
    all_to_all x1, waiting for transfers between devices, body(): lax.all_to_all(ordered, 'owner', split_axis=0, concat_axis=1, tiled=True)  93.7 us
    all_gather x1, waiting for transfers between devices, body(): return lax.all_gather(results, 'owner', axis=0, tiled=True)  60 us
    dot_general x18, matrix products, _mm_nt(): lax.dot_general(a, b, (((1,), (1,)), ((), ())), precision=HIGH, preferred...  47.4 us
    all_gather x1, waiting for transfers between devices, body(): gathered = lax.all_gather(gathered, axis, axis=0, tiled=True)  42.9 us
    all_gather x2, blocking collectives, body(): gathered = lax.all_gather(gathered, axis, axis=0, tiled=True)  26.5 us
    dot_general x1, matrix products, body(): gram = jnp.dot(columns.T, columns, preferred_element_type=jnp.float32)  22.8 us
  transfers between devices with their start and end apart: 7, of which 6 were waited for; matrix products, arithmetic and copies ran while one was open for 2% of the time, Pallas kernels for 0%

profile of v6, /device:TPU:2, one launch (start us, length us, event | category | flops | bytes accessed | tf_op | source)
XLA Modules:
  0.0 670.1 jit_solution(17553453209508025513)
XLA Ops:
  7.8 5.9 all-to-all-start
  15.0 5.0 gather_fusion
  20.0 4.7 broadcast_select_fusion
  24.7 5.1 all-to-all-start.1
  30.2 93.7 %all-to-all-done.1 = bf16[8,512,512]{2,1,0:T(8,128)(2,1)} async-done(((bf16[8,512,512]{2,1,0:T(8,128)(2,1)}), bf16[8,512,512]{2,1,0:T(8,128)(2,1)}, u32[]{:S(2)}, u32[]{:S(2)}) %all-to-all-start.1) | async-done | bytes 4194336 | tf_op jit(solution)/shard_map/all_to_all | solution.py:189
  125.2 2.3 slice.661
  127.5 3.9 fusion.60
  131.3 2.2 pad_select_fusion
  133.6 6.1 fusion
  139.6 14.3 %copy.18 = bf16[1280,4096]{1,0:T(8,128)(2,1)} copy(bf16[1280,4096]{0,1:T(8,128)(2,1)} %fusion) | data formatting | bytes 20971520 | tf_op jit(solution)/shard_map/dot_general | solution.py:195
  153.9 22.8 %convolution_bitcast_fusion = f32[10,10,128,128]{3,2,1,0:T(8,128)} fusion(bf16[10,128,4096,1]{2,1,3,0:T(8,128)(2,1)} %bitcast.111, bf16[10,128,4096,1]{2,1,0,3:T(8,128)(2,1)} %bitcast.112), kind=kOutput, calls=%fused_computation.11 | convolution fusion | flops 13421772800 | bytes 27525120 | tf_op jit(solution)/shard_map/dot_general | solution.py:195
  176.8 5.5 gather_fusion.1
  182.2 4.3 concatenate.95
  186.6 45.5 %reduce-scatter.4.cloned.1.call-done = f32[1792,128]{1,0:T(8,128)} async-done(((f32[7168,128]{1,0:T(8,128)}), f32[1792,128]{1,0:T(8,128)}) %reduce-scatter.4.cloned.1.call-update) | async-done | bytes 917520 | tf_op jit(solution)/shard_map/reduce_scatter | solution.py:208
  232.2 25.5 %reduce-scatter.6.cloned.1.call-done = f32[448,128]{1,0:T(8,128)} async-done(((f32[1792,128]{1,0:T(8,128)}), f32[448,128]{1,0:T(8,128)}) %reduce-scatter.6.cloned.1.call-update) | async-done | bytes 229392 | tf_op jit(solution)/shard_map/reduce_scatter | solution.py:208
  257.7 27.7 %reduce-scatter.8.cloned.1.call-done = f32[224,128]{1,0:T(8,128)} async-done(((f32[448,128]{1,0:T(8,128)}), f32[224,128]{1,0:T(8,128)}) %reduce-scatter.8.cloned.1.call-update) | async-done | bytes 114704 | tf_op jit(solution)/shard_map/reduce_scatter | solution.py:208
  285.4 12.1 %all_gather.12 = f32[448,128]{1,0:T(8,128)S(1)} all-gather(f32[224,128]{1,0:T(8,128)} %reduce-scatter.8.cloned.1.call-done), channel_id=1, replica_groups=mesh['dp_x'=4,'dp_z'=2,'dp_y'=4,'owner'=8] {'dp_z'}, dimensions={0}, use_global_device_ids=true | all-gather | bytes 344064 | tf_op jit(solution)/shard_map/all_gather | solution.py:211
  297.5 14.3 %all_gather.13 = f32[1792,128]{1,0:T(8,128)} all-gather(f32[448,128]{1,0:T(8,128)S(1)} %all_gather.12), channel_id=1, replica_groups=mesh['dp_x'=4,'dp_z'=2,'dp_y'=4,'owner'=8] {'dp_x'}, dimensions={0}, use_global_device_ids=true | all-gather | bytes 1146880 | tf_op jit(solution)/shard_map/all_gather | solution.py:211
  312.1 42.9 %all-gather.4.cloned.1.call-done = f32[7168,128]{1,0:T(8,128)} async-done(((f32[1792,128]{1,0:T(8,128)}), f32[7168,128]{1,0:T(8,128)}) %all-gather.4.cloned.1.call-update) | async-done | bytes 3670032 | tf_op jit(solution)/shard_map/all_gather | solution.py:211
  359.4 2.5 copy-done
  362.5 15.7 %shard_map.73 = f32[128,128]{1,0:T(8,128)} custom-call(f32[128,128]{1,0:T(8,128)} %select_add_fusion.9.a_ref), custom_call_target="tpu_custom_call" | custom-call | flops 12582912 | bytes 131072 | tf_op jit(solution)/shard_map/pallas_call | solution.py:124
  380.8 7.3 %constant_dynamic-update-slice_fusion.45 = (f32[1280,1152]{1,0:T(8,128)}, f32[1152,1024]{1,0:T(8,128)S(1)}) fusion(f32[1280,1152]{1,0:T(8,128)} %constant_dynamic-update-slice_fusion.46, f32[1152,128]{1,0:T(8,128)S(1)} %fusion.5), kind=kOutput, calls=%fused_computation.164 | convolution fusion | flops 1814298624 | bytes 15269888 | tf_op jit(solution)/shard_map/dot_general | solution.py:85
  388.1 2.2 copy-done.1
  391.0 15.7 %shard_map.74 = f32[128,128]{1,0:T(8,128)} custom-call(f32[128,128]{1,0:T(8,128)} %select_add_fusion.8.a_ref), custom_call_target="tpu_custom_call" | custom-call | flops 12582912 | bytes 131072 | tf_op jit(solution)/shard_map/pallas_call | solution.py:124
  406.6 2.5 constant_dynamic-update-slice_fusion.44
  409.1 6.0 constant_dynamic-update-slice_fusion.43
  415.1 1.8 copy-done.2
  417.6 15.7 %shard_map.75 = f32[128,128]{1,0:T(8,128)} custom-call(f32[128,128]{1,0:T(8,128)} %select_add_fusion.7.a_ref), custom_call_target="tpu_custom_call" | custom-call | flops 12582912 | bytes 131072 | tf_op jit(solution)/shard_map/pallas_call | solution.py:124
  433.2 2.3 constant_dynamic-update-slice_fusion.42
  435.6 5.8 constant_dynamic-update-slice_fusion.41
  442.0 15.7 %shard_map.76 = f32[128,128]{1,0:T(8,128)} custom-call(f32[128,128]{1,0:T(8,128)} %select_add_fusion.6.a_ref), custom_call_target="tpu_custom_call" | custom-call | flops 12582912 | bytes 131072 | tf_op jit(solution)/shard_map/pallas_call | solution.py:124
  457.6 2.1 constant_dynamic-update-slice_fusion.40
  459.7 4.7 constant_dynamic-update-slice_fusion.39
  465.0 15.7 %shard_map.77 = f32[128,128]{1,0:T(8,128)} custom-call(f32[128,128]{1,0:T(8,128)} %select_add_fusion.5.a_ref), custom_call_target="tpu_custom_call" | custom-call | flops 12582912 | bytes 131072 | tf_op jit(solution)/shard_map/pallas_call | solution.py:124
  480.7 2.1 constant_dynamic-update-slice_fusion.38
  482.8 2.5 fusion.1
  487.1 15.7 %shard_map.78 = f32[128,128]{1,0:T(8,128)} custom-call(f32[128,128]{1,0:T(8,128)} %select_add_fusion.4.a_ref), custom_call_target="tpu_custom_call" | custom-call | flops 12582912 | bytes 131072 | tf_op jit(solution)/shard_map/pallas_call | solution.py:124
  502.8 2.0 constant_dynamic-update-slice_fusion.36
  504.8 1.9 fusion.2
  509.9 15.7 %shard_map.82 = f32[128,128]{1,0:T(8,128)} custom-call(f32[128,128]{1,0:T(8,128)} %select_add_fusion.a_ref), custom_call_target="tpu_custom_call" | custom-call | flops 12582912 | bytes 131072 | tf_op jit(solution)/shard_map/pallas_call | solution.py:124
  525.5 15.7 %shard_map.79 = f32[128,128]{1,0:T(8,128)} custom-call(f32[128,128]{1,0:T(8,128)} %select_add_fusion.3.a_ref), custom_call_target="tpu_custom_call" | custom-call | flops 12582912 | bytes 131072 | tf_op jit(solution)/shard_map/pallas_call | solution.py:124
  541.2 1.9 constant_dynamic-update-slice_fusion.34
  545.2 15.7 %shard_map.80 = f32[128,128]{1,0:T(8,128)} custom-call(f32[128,128]{1,0:T(8,128)} %select_add_fusion.2.a_ref), custom_call_target="tpu_custom_call" | custom-call | flops 12582912 | bytes 131072 | tf_op jit(solution)/shard_map/pallas_call | solution.py:124
  562.9 15.7 %shard_map.81 = f32[128,128]{1,0:T(8,128)} custom-call(f32[128,128]{1,0:T(8,128)} %select_add_fusion.1.a_ref), custom_call_target="tpu_custom_call" | custom-call | flops 12582912 | bytes 131072 | tf_op jit(solution)/shard_map/pallas_call | solution.py:124
  591.7 1.9 convolution_subtract_fusion.1
  594.0 2.1 convolution_subtract_fusion
  598.7 60.0 %all-gather.6.cloned.1.call-done = f32[9216,128]{1,0:T(8,128)} async-done(((f32[1152,128]{1,0:T(8,128)}), f32[9216,128]{1,0:T(8,128)}) %all-gather.6.cloned.1.call-update) | async-done | bytes 4718608 | tf_op jit(solution)/shard_map/all_gather | solution.py:214
  658.7 4.9 copy.89
  (133 shorter events, 39.4 us)
Async XLA Ops:
  7.8 16.9 %all-to-all-start = ((s32[8,1,4]{2,1,0:T(1,128)}), s32[8,1,4]{2,1,0:T(1,128)S(1)}, u32[]{:S(2)}, u32[]{:S(2)}) async-start(s32[8,1,4]{2,1,0:T(1,128)} %broadcast_in_dim.63), calls=%async_computation | async-start | bytes 8192 | tf_op jit(solution)/shard_map/all_to_all | solution.py:190
  24.7 99.2 %all-to-all-start.1 = ((bf16[8,512,512]{2,1,0:T(8,128)(2,1)}), bf16[8,512,512]{2,1,0:T(8,128)(2,1)}, u32[]{:S(2)}, u32[]{:S(2)}) async-start(bf16[8,512,512]{2,1,0:T(8,128)(2,1)} %broadcast_select_fusion), calls=%async_computation.1 | async-start | bytes 8388608 | tf_op jit(solution)/shard_map/all_to_all | solution.py:189
  29.8 202.3 %reduce-scatter.4.cloned.1.call-start = ((), (), s32[]{:S(2)}) async-start(), calls=%async_computation.5 | async-start | bytes 4587520 | tf_op jit(solution)/shard_map/reduce_scatter | solution.py:208
  153.9 22.8 %copy-start.3 = (s32[55]{0:T(128)S(1)}, s32[55]{0:T(128)}, u32[]{:S(2)}) copy-start(s32[55]{0:T(128)} %constant.551) | copy-start | bytes 664
  186.6 71.1 %reduce-scatter.6.cloned.1.call-start = ((), (), s32[]{:S(2)}) async-start(), calls=%async_computation.6 | async-start | bytes 1146880 | tf_op jit(solution)/shard_map/reduce_scatter | solution.py:208
  232.1 53.2 %reduce-scatter.8.cloned.1.call-start = ((), (), s32[]{:S(2)}) async-start(), calls=%async_computation.7 | async-start | bytes 344064 | tf_op jit(solution)/shard_map/reduce_scatter | solution.py:208
  257.7 97.3 %all-gather.4.cloned.1.call-start = ((), (), s32[]{:S(2)}) async-start(), calls=%async_computation.8 | async-start | bytes 4587520 | tf_op jit(solution)/shard_map/all_gather | solution.py:211
  311.9 346.8 %all-gather.6.cloned.1.call-start = ((), (), s32[]{:S(2)}) async-start(), calls=%async_computation.9 | async-start | bytes 5308416 | tf_op jit(solution)/shard_map/all_gather | solution.py:214
  355.0 3.6 slice-start
  355.0 3.7 slice-start.1
  355.0 3.7 slice-start.2
  355.0 3.8 slice-start.3
  356.2 2.6 slice-start.4
  357.4 1.5 slice-start.5
  359.4 2.5 copy-start
  388.1 2.2 copy-start.1
  415.1 1.8 copy-start.2
  486.5 100.6 %copy-start.9 = (f32[128,128]{1,0:T(8,128)S(1)}, f32[128,128]{1,0:T(8,128)}, u32[]{:S(2)}) copy-start(f32[128,128]{1,0:T(8,128)} %shard_map.77) | copy-start | bytes 196612
  502.8 82.4 %copy-start.10 = (f32[128,128]{1,0:T(8,128)S(1)}, f32[128,128]{1,0:T(8,128)}, u32[]{:S(2)}) copy-start(f32[128,128]{1,0:T(8,128)} %shard_map.78) | copy-start | bytes 196612
  502.8 86.3 %copy-start.8 = (f32[128,128]{1,0:T(8,128)S(1)}, f32[128,128]{1,0:T(8,128)}, u32[]{:S(2)}) copy-start(f32[128,128]{1,0:T(8,128)} %shard_map.76) | copy-start | bytes 196612
  506.7 84.6 %copy-start.7 = (f32[128,128]{1,0:T(8,128)S(1)}, f32[128,128]{1,0:T(8,128)}, u32[]{:S(2)}) copy-start(f32[128,128]{1,0:T(8,128)} %shard_map.75) | copy-start | bytes 196612
  507.7 85.9 %copy-start.6 = (f32[128,128]{1,0:T(8,128)S(1)}, f32[128,128]{1,0:T(8,128)}, u32[]{:S(2)}) copy-start(f32[128,128]{1,0:T(8,128)} %shard_map.74) | copy-start | bytes 196612
  544.5 51.6 %copy-start.4 = (f32[128,128]{1,0:T(8,128)S(1)}, f32[128,128]{1,0:T(8,128)}, u32[]{:S(2)}) copy-start(f32[128,128]{1,0:T(8,128)} %shard_map.73) | copy-start | bytes 196612
  562.3 34.3 %copy-start.5 = (f32[128,128]{1,0:T(8,128)S(1)}, f32[128,128]{1,0:T(8,128)}, u32[]{:S(2)}) copy-start(f32[128,128]{1,0:T(8,128)} %shard_map.82) | copy-start | bytes 196612
Sparse Core Ops, SparseCore 0:
  186.7 45.3 reduce-scatter.3
  234.7 22.9 reduce-scatter.5
  260.1 25.1 reduce-scatter.7
  312.0 42.9 all-gather.3
  598.8 59.8 all-gather.5

commit v7 on v6

--- a/solution.py
+++ b/solution.py
@@ -180,30 +180,29 @@
     n_replicas = 1
     for axis in DP_AXES:
         n_replicas = n_replicas * lax.axis_size(axis)
-    n_owners = lax.axis_size("owner")
+    n_owners = lax.axis_size(OWNER_AXES[0]) * lax.axis_size(OWNER_AXES[1])
     per_owner = layer_count // n_owners
     total_rows = n_replicas * n_owners * positions
     ordered = jnp.take(line_columns, layer_owner, axis=0)
     width_copies = jnp.broadcast_to(line_widths[None, :, :], (n_owners, 1, line_widths.shape[1]))
     received, source_widths = (
-        lax.all_to_all(ordered, "owner", split_axis=0, concat_axis=1, tiled=True),
-        lax.all_to_all(width_copies, "owner", split_axis=0, concat_axis=1, tiled=True),
+        lax.all_to_all(ordered, OWNER_AXES, split_axis=0, concat_axis=1, tiled=True),
+        lax.all_to_all(width_copies, OWNER_AXES, split_axis=0, concat_axis=1, tiled=True),
     )
     blocks = received.reshape(per_owner, n_owners, positions, packed_width)
     columns = patch_columns(blocks, source_widths.reshape(n_owners, line_widths.shape[1]))
     columns = columns.reshape(n_owners * positions, full_width)
-    gram = jnp.dot(columns.T, columns, preferred_element_type=jnp.float32)
     block = 128
     nb = full_width // block
-    packed = pack_lower(gram, block)
-    n_blocks = packed.shape[0]
+    n_blocks = nb * (nb + 1) // 2
     padded = -(-n_blocks * block // (8 * n_replicas)) * 8 * n_replicas // block
-    packed = jnp.concatenate(
-        [packed, jnp.zeros((padded - n_blocks, block, block), packed.dtype)], axis=0
-    )
-    chunk = padded * block // n_replicas
-    packed = packed.reshape(n_replicas, chunk, block)
-    mine = packed.reshape(padded * block, block)
+    panels = [
+        lax.dot_general(columns[:, j * block:], columns[:, j * block:(j + 1) * block],
+                        (((0,), (0,)), ((), ())), preferred_element_type=jnp.float32)
+        for j in range(nb)
+    ]
+    panels.append(jnp.zeros(((padded - n_blocks) * block, block), jnp.float32))
+    mine = jnp.concatenate(panels, axis=0)
     for axis in SCATTER_ORDER:
         mine = lax.psum_scatter(mine, axis, scatter_dimension=0, tiled=True)
     gathered = mine
@@ -211,18 +210,24 @@
         gathered = lax.all_gather(gathered, axis, axis=0, tiled=True)
     gathered = gathered.reshape(padded, block, block)
     results = precondition_blocks(gathered, nb, total_rows)[None]
-    return lax.all_gather(results, "owner", axis=0, tiled=True)
+    results = lax.all_gather(results, OWNER_AXES[0], axis=0, tiled=True)
+    results = lax.all_gather(results, OWNER_AXES[1], axis=1, tiled=False)
+    return results.reshape((n_owners,) + results.shape[2:])
 
 
 DP_AXES = ("dp_x", "dp_z", "dp_y")
 SCATTER_ORDER = ("dp_y", "dp_x", "dp_z")
 
 
+OWNER_AXES = ("owner_z", "owner_c")
+
+
 def solution(mesh):
     dp_shape = (4, 2, mesh.shape["dp"] // 8)
-    devices = mesh.devices.reshape(dp_shape + (mesh.shape["owner"],))
-    fine = jax.sharding.Mesh(devices, DP_AXES + ("owner",))
-    rows = DP_AXES + ("owner",)
+    owner_shape = (mesh.shape["owner"] // 2, 2)
+    devices = mesh.devices.reshape(dp_shape + owner_shape)
+    fine = jax.sharding.Mesh(devices, DP_AXES + OWNER_AXES)
+    rows = DP_AXES + OWNER_AXES
     in_specs = (P(None, rows, None), P(rows, None), P())
     out_specs = P()
     return jax.shard_map(body, mesh=fine, in_specs=in_specs, out_specs=out_specs, check_vma=False)

time: 672 us -> 671 us (level)
  local copies, waits for them, and re-layouts: 56.5 us -> 33.1 us
  waiting for transfers between devices: 295 us -> 311 us
    all_gather x1 -> x2, waiting for transfers between devices: 60 us -> 75.9 us  [the longest x1 54.9 us: body(): results = lax.all_gather(results, OWNER_AXES[0], axis=0, tiled=True)]
    dot_general x1 -> x0, local copies, waits for them, and re-layouts: 14.3 us -> none  [body(): gram = jnp.dot(columns.T, columns, preferred_element_type=jnp.float32)]
    dot_general x1 -> x10, matrix products: 22.8 us -> 24.7 us  [body(): lax.dot_general(columns[:, j * block:], columns[:, j * block:(j + 1) * bl...]
  transfers between devices with their start and end apart: 7 -> 8, of which waited for: 6 -> 7; matrix products, arithmetic and copies ran while one was open for 2% -> 2% of each run, Pallas kernels for 0% -> 0%
where the time goes in v7:
time: 671 us; the launch traced here: 664 us
  waiting for transfers between devices  311 us (46%)
  Pallas kernels  157 us (23%)
  matrix products  89.9 us (13%)
  local copies, waits for them, and re-layouts  33.1 us (5%)
  blocking collectives  26.5 us (4%)
  other arithmetic  20.8 us (3%)
  between operations  14.4 us (2%)
  starting transfers between devices  11.2 us (2%)
    pallas_call x10, Pallas kernels, _chol_inverse(): pl.pallas_call(_leaf_kernel, out_shape=jax.ShapeDtypeStruct((n, n), jnp.f...  157 us
    reduce_scatter x3, waiting for transfers between devices, body(): mine = lax.psum_scatter(mine, axis, scatter_dimension=0, tiled=True)  98.6 us
    all_to_all x1, waiting for transfers between devices, body(): lax.all_to_all(ordered, OWNER_AXES, split_axis=0, concat_axis=1, tiled=True)  93.7 us
    all_gather x1, waiting for transfers between devices, body(): results = lax.all_gather(results, OWNER_AXES[0], axis=0, tiled=True)  54.9 us
    dot_general x18, matrix products, _mm_nt(): lax.dot_general(a, b, (((1,), (1,)), ((), ())), precision=HIGH, preferred...  47.5 us
    all_gather x1, waiting for transfers between devices, body(): gathered = lax.all_gather(gathered, axis, axis=0, tiled=True)  43 us
    all_gather x2, blocking collectives, body(): gathered = lax.all_gather(gathered, axis, axis=0, tiled=True)  26.5 us
    dot_general x10, matrix products, body(): lax.dot_general(columns[:, j * block:], columns[:, j * block:(j + 1) * bl...  24.7 us
  transfers between devices with their start and end apart: 8, of which 7 were waited for; matrix products, arithmetic and copies ran while one was open for 2% of the time, Pallas kernels for 0%

profile of v7, /device:TPU:2, one launch (start us, length us, event | category | flops | bytes accessed | tf_op | source)
XLA Modules:
  0.0 663.9 jit_solution(8685346360083662865)
XLA Ops:
  7.8 5.9 all-to-all-start
  15.0 5.0 gather_fusion
  20.0 4.7 broadcast_select_fusion
  24.7 5.1 all-to-all-start.1
  30.2 93.7 %all-to-all-done.1 = bf16[8,512,512]{2,1,0:T(8,128)(2,1)} async-done(((bf16[8,512,512]{2,1,0:T(8,128)(2,1)}), bf16[8,512,512]{2,1,0:T(8,128)(2,1)}, u32[]{:S(2)}, u32[]{:S(2)}) %all-to-all-start.1) | async-done | bytes 4194336 | tf_op jit(solution)/shard_map/all_to_all | solution.py:189
  125.2 2.3 slice.732
  127.5 3.9 fusion.109
  131.3 2.2 pad_select_fusion
  133.6 4.7 maximum_select_fusion
  138.3 3.8 convolution_dynamic-update-slice_fusion
  142.1 3.5 fusion.14
  145.5 3.2 fusion.21
  148.7 2.9 fusion.24
  151.5 2.6 fusion.27
  154.1 2.7 fusion.30
  156.8 2.0 fusion.34
  163.7 45.5 %reduce-scatter.4.cloned.1.call-done = f32[1792,128]{1,0:T(8,128)} async-done(((f32[7168,128]{1,0:T(8,128)}), f32[1792,128]{1,0:T(8,128)}) %reduce-scatter.4.cloned.1.call-update) | async-done | bytes 917520 | tf_op jit(solution)/shard_map/reduce_scatter | solution.py:207
  209.2 25.5 %reduce-scatter.6.cloned.1.call-done = f32[448,128]{1,0:T(8,128)} async-done(((f32[1792,128]{1,0:T(8,128)}), f32[448,128]{1,0:T(8,128)}) %reduce-scatter.6.cloned.1.call-update) | async-done | bytes 229392 | tf_op jit(solution)/shard_map/reduce_scatter | solution.py:207
  234.8 27.7 %reduce-scatter.8.cloned.1.call-done = f32[224,128]{1,0:T(8,128)} async-done(((f32[448,128]{1,0:T(8,128)}), f32[224,128]{1,0:T(8,128)}) %reduce-scatter.8.cloned.1.call-update) | async-done | bytes 114704 | tf_op jit(solution)/shard_map/reduce_scatter | solution.py:207
  262.4 12.1 %all_gather.18 = f32[448,128]{1,0:T(8,128)S(1)} all-gather(f32[224,128]{1,0:T(8,128)} %reduce-scatter.8.cloned.1.call-done), channel_id=1, replica_groups=mesh['dp_x'=4,'dp_z'=2,'dp_y'=4,'owner_z'=4,'owner_c'=2] {'dp_z'}, dimensions={0}, use_global_device_ids=true | all-gather | bytes 344064 | tf_op jit(solution)/shard_map/all_gather | solution.py:210
  274.6 14.3 %all_gather.19 = f32[1792,128]{1,0:T(8,128)} all-gather(f32[448,128]{1,0:T(8,128)S(1)} %all_gather.18), channel_id=1, replica_groups=mesh['dp_x'=4,'dp_z'=2,'dp_y'=4,'owner_z'=4,'owner_c'=2] {'dp_x'}, dimensions={0}, use_global_device_ids=true | all-gather | bytes 1146880 | tf_op jit(solution)/shard_map/all_gather | solution.py:210
  289.0 43.0 %all-gather.6.cloned.1.call-done = f32[7168,128]{1,0:T(8,128)} async-done(((f32[1792,128]{1,0:T(8,128)}), f32[7168,128]{1,0:T(8,128)}) %all-gather.6.cloned.1.call-update) | async-done | bytes 3670032 | tf_op jit(solution)/shard_map/all_gather | solution.py:210
  336.4 2.5 copy-done
  339.6 15.7 %shard_map.37 = f32[128,128]{1,0:T(8,128)} custom-call(f32[128,128]{1,0:T(8,128)} %select_add_fusion.9.a_ref), custom_call_target="tpu_custom_call" | custom-call | flops 12582912 | bytes 131072 | tf_op jit(solution)/shard_map/pallas_call | solution.py:124
  357.9 7.3 %constant_dynamic-update-slice_fusion.46 = (f32[1280,1152]{1,0:T(8,128)}, f32[1152,1024]{1,0:T(8,128)S(1)}) fusion(f32[1280,1152]{1,0:T(8,128)} %constant_dynamic-update-slice_fusion.47, f32[1152,128]{1,0:T(8,128)S(1)} %fusion.54), kind=kOutput, calls=%fused_computation.198 | convolution fusion | flops 1814298624 | bytes 15269888 | tf_op jit(solution)/shard_map/dot_general | solution.py:85
  365.2 2.2 copy-done.1
  368.1 15.7 %shard_map.38 = f32[128,128]{1,0:T(8,128)} custom-call(f32[128,128]{1,0:T(8,128)} %select_add_fusion.8.a_ref), custom_call_target="tpu_custom_call" | custom-call | flops 12582912 | bytes 131072 | tf_op jit(solution)/shard_map/pallas_call | solution.py:124
  383.7 2.5 constant_dynamic-update-slice_fusion.45
  386.2 6.1 constant_dynamic-update-slice_fusion.44
  394.7 15.7 %shard_map.39 = f32[128,128]{1,0:T(8,128)} custom-call(f32[128,128]{1,0:T(8,128)} %select_add_fusion.7.a_ref), custom_call_target="tpu_custom_call" | custom-call | flops 12582912 | bytes 131072 | tf_op jit(solution)/shard_map/pallas_call | solution.py:124
  410.4 2.4 constant_dynamic-update-slice_fusion.43
  412.8 5.8 constant_dynamic-update-slice_fusion.42
  419.2 15.7 %shard_map.40 = f32[128,128]{1,0:T(8,128)} custom-call(f32[128,128]{1,0:T(8,128)} %select_add_fusion.6.a_ref), custom_call_target="tpu_custom_call" | custom-call | flops 12582912 | bytes 131072 | tf_op jit(solution)/shard_map/pallas_call | solution.py:124
  434.9 2.1 constant_dynamic-update-slice_fusion.41
  437.0 4.7 constant_dynamic-update-slice_fusion.40
  442.3 15.7 %shard_map.41 = f32[128,128]{1,0:T(8,128)} custom-call(f32[128,128]{1,0:T(8,128)} %select_add_fusion.5.a_ref), custom_call_target="tpu_custom_call" | custom-call | flops 12582912 | bytes 131072 | tf_op jit(solution)/shard_map/pallas_call | solution.py:124
  458.0 2.0 constant_dynamic-update-slice_fusion.39
  460.0 2.5 fusion.19
  464.4 15.7 %shard_map.42 = f32[128,128]{1,0:T(8,128)} custom-call(f32[128,128]{1,0:T(8,128)} %select_add_fusion.4.a_ref), custom_call_target="tpu_custom_call" | custom-call | flops 12582912 | bytes 131072 | tf_op jit(solution)/shard_map/pallas_call | solution.py:124
  480.1 2.0 constant_dynamic-update-slice_fusion.37
  487.2 15.7 %shard_map.46 = f32[128,128]{1,0:T(8,128)} custom-call(f32[128,128]{1,0:T(8,128)} %select_add_fusion.a_ref), custom_call_target="tpu_custom_call" | custom-call | flops 12582912 | bytes 131072 | tf_op jit(solution)/shard_map/pallas_call | solution.py:124
  502.9 15.7 %shard_map.43 = f32[128,128]{1,0:T(8,128)} custom-call(f32[128,128]{1,0:T(8,128)} %select_add_fusion.3.a_ref), custom_call_target="tpu_custom_call" | custom-call | flops 12582912 | bytes 131072 | tf_op jit(solution)/shard_map/pallas_call | solution.py:124
  522.5 15.7 %shard_map.44 = f32[128,128]{1,0:T(8,128)} custom-call(f32[128,128]{1,0:T(8,128)} %select_add_fusion.2.a_ref), custom_call_target="tpu_custom_call" | custom-call | flops 12582912 | bytes 131072 | tf_op jit(solution)/shard_map/pallas_call | solution.py:124
  540.3 15.6 %shard_map.45 = f32[128,128]{1,0:T(8,128)} custom-call(f32[128,128]{1,0:T(8,128)} %select_add_fusion.1.a_ref), custom_call_target="tpu_custom_call" | custom-call | flops 12582912 | bytes 131072 | tf_op jit(solution)/shard_map/pallas_call | solution.py:124
  571.4 2.1 convolution_subtract_fusion
  576.0 54.9 %all-gather.8.cloned.1.call-done = f32[4608,128]{1,0:T(8,128)} async-done(((f32[1152,128]{1,0:T(8,128)}), f32[4608,128]{1,0:T(8,128)}) %all-gather.8.cloned.1.call-update) | async-done | bytes 2359312 | tf_op jit(solution)/shard_map/all_gather | solution.py:213
  630.9 21.1 %all-gather.10.cloned.1.call-done = f32[4,2304,128]{2,1,0:T(8,128)} async-done(((f32[4,1152,128]{2,1,0:T(8,128)}), f32[4,2304,128]{2,1,0:T(8,128)}) %all-gather.10.cloned.1.call-update) | async-done | bytes 4718608 | tf_op jit(solution)/shard_map/all_gather | solution.py:214
  652.0 4.9 copy.91
  (141 shorter events, 51.9 us)
Async XLA Ops:
  7.8 16.9 %all-to-all-start = ((s32[8,1,4]{2,1,0:T(1,128)}), s32[8,1,4]{2,1,0:T(1,128)S(1)}, u32[]{:S(2)}, u32[]{:S(2)}) async-start(s32[8,1,4]{2,1,0:T(1,128)} %broadcast_in_dim.59), calls=%async_computation | async-start | bytes 8192 | tf_op jit(solution)/shard_map/all_to_all | solution.py:190
  24.7 99.2 %all-to-all-start.1 = ((bf16[8,512,512]{2,1,0:T(8,128)(2,1)}), bf16[8,512,512]{2,1,0:T(8,128)(2,1)}, u32[]{:S(2)}, u32[]{:S(2)}) async-start(bf16[8,512,512]{2,1,0:T(8,128)(2,1)} %broadcast_select_fusion), calls=%async_computation.1 | async-start | bytes 8388608 | tf_op jit(solution)/shard_map/all_to_all | solution.py:189
  29.8 179.4 %reduce-scatter.4.cloned.1.call-start = ((), (), s32[]{:S(2)}) async-start(), calls=%async_computation.5 | async-start | bytes 4587520 | tf_op jit(solution)/shard_map/reduce_scatter | solution.py:207
  163.7 71.0 %reduce-scatter.6.cloned.1.call-start = ((), (), s32[]{:S(2)}) async-start(), calls=%async_computation.6 | async-start | bytes 1146880 | tf_op jit(solution)/shard_map/reduce_scatter | solution.py:207
  209.2 53.2 %reduce-scatter.8.cloned.1.call-start = ((), (), s32[]{:S(2)}) async-start(), calls=%async_computation.7 | async-start | bytes 344064 | tf_op jit(solution)/shard_map/reduce_scatter | solution.py:207
  234.7 97.3 %all-gather.6.cloned.1.call-start = ((), (), s32[]{:S(2)}) async-start(), calls=%async_computation.8 | async-start | bytes 4587520 | tf_op jit(solution)/shard_map/all_gather | solution.py:210
  288.9 342.0 %all-gather.8.cloned.1.call-start = ((), (), s32[]{:S(2)}) async-start(), calls=%async_computation.9 | async-start | bytes 2949120 | tf_op jit(solution)/shard_map/all_gather | solution.py:213
  332.0 3.6 slice-start
  332.0 3.7 slice-start.1
  332.0 3.7 slice-start.2
  332.0 3.8 slice-start.3
  333.3 2.6 slice-start.4
  334.4 1.5 slice-start.5
  336.4 2.5 copy-start
  365.2 2.2 copy-start.1
  392.2 1.8 copy-start.2
  463.8 100.6 %copy-start.8 = (f32[128,128]{1,0:T(8,128)S(1)}, f32[128,128]{1,0:T(8,128)}, u32[]{:S(2)}) copy-start(f32[128,128]{1,0:T(8,128)} %shard_map.41) | copy-start | bytes 196612
  480.1 82.4 %copy-start.9 = (f32[128,128]{1,0:T(8,128)S(1)}, f32[128,128]{1,0:T(8,128)}, u32[]{:S(2)}) copy-start(f32[128,128]{1,0:T(8,128)} %shard_map.42) | copy-start | bytes 196612
  480.1 86.3 %copy-start.7 = (f32[128,128]{1,0:T(8,128)S(1)}, f32[128,128]{1,0:T(8,128)}, u32[]{:S(2)}) copy-start(f32[128,128]{1,0:T(8,128)} %shard_map.40) | copy-start | bytes 196612
  484.1 84.6 %copy-start.6 = (f32[128,128]{1,0:T(8,128)S(1)}, f32[128,128]{1,0:T(8,128)}, u32[]{:S(2)}) copy-start(f32[128,128]{1,0:T(8,128)} %shard_map.39) | copy-start | bytes 196612
  485.1 85.9 %copy-start.5 = (f32[128,128]{1,0:T(8,128)S(1)}, f32[128,128]{1,0:T(8,128)}, u32[]{:S(2)}) copy-start(f32[128,128]{1,0:T(8,128)} %shard_map.38) | copy-start | bytes 196612
  521.9 51.6 %copy-start.3 = (f32[128,128]{1,0:T(8,128)S(1)}, f32[128,128]{1,0:T(8,128)}, u32[]{:S(2)}) copy-start(f32[128,128]{1,0:T(8,128)} %shard_map.37) | copy-start | bytes 196612
  539.6 34.3 %copy-start.4 = (f32[128,128]{1,0:T(8,128)S(1)}, f32[128,128]{1,0:T(8,128)}, u32[]{:S(2)}) copy-start(f32[128,128]{1,0:T(8,128)} %shard_map.46) | copy-start | bytes 196612
  576.0 76.0 %all-gather.10.cloned.1.call-start = ((), (), s32[]{:S(2)}) async-start(), calls=%async_computation.10 | async-start | bytes 7077888 | tf_op jit(solution)/shard_map/all_gather | solution.py:214
Sparse Core Ops, SparseCore 0:
  163.8 45.3 reduce-scatter.3
  211.7 22.9 reduce-scatter.5
  237.2 25.1 reduce-scatter.7
  289.1 42.9 all-gather.5
  576.1 54.7 all-gather.7
  632.6 19.3 all-gather.9

commit v8 on v7

--- a/solution.py
+++ b/solution.py
@@ -210,9 +210,7 @@
         gathered = lax.all_gather(gathered, axis, axis=0, tiled=True)
     gathered = gathered.reshape(padded, block, block)
     results = precondition_blocks(gathered, nb, total_rows)[None]
-    results = lax.all_gather(results, OWNER_AXES[0], axis=0, tiled=True)
-    results = lax.all_gather(results, OWNER_AXES[1], axis=1, tiled=False)
-    return results.reshape((n_owners,) + results.shape[2:])
+    return lax.all_gather(results, OWNER_AXES, axis=0, tiled=True)
 
 
 DP_AXES = ("dp_x", "dp_z", "dp_y")

time: 671 us -> 653 us (0.973)
  waiting for transfers between devices: 311 us -> 295 us
    all_gather x2 -> x1, waiting for transfers between devices: 75.9 us -> 60 us  [body(): return lax.all_gather(results, OWNER_AXES, axis=0, tiled=True)]
  transfers between devices with their start and end apart: 8 -> 7, of which waited for: 7 -> 6; matrix products, arithmetic and copies ran while one was open for 2% -> 2% of each run, Pallas kernels for 0% -> 0%
where the time goes in v8:
time: 653 us; the launch traced here: 647 us
  waiting for transfers between devices  295 us (45%)
  Pallas kernels  157 us (24%)
  matrix products  89.9 us (14%)
  local copies, waits for them, and re-layouts  33 us (5%)
  blocking collectives  26.5 us (4%)
  other arithmetic  20.8 us (3%)
  between operations  14.1 us (2%)
  starting transfers between devices  11.2 us (2%)
    pallas_call x10, Pallas kernels, _chol_inverse(): pl.pallas_call(_leaf_kernel, out_shape=jax.ShapeDtypeStruct((n, n), jnp.f...  157 us
    reduce_scatter x3, waiting for transfers between devices, body(): mine = lax.psum_scatter(mine, axis, scatter_dimension=0, tiled=True)  98.6 us
    all_to_all x1, waiting for transfers between devices, body(): lax.all_to_all(ordered, OWNER_AXES, split_axis=0, concat_axis=1, tiled=True)  93.7 us
    all_gather x1, waiting for transfers between devices, body(): return lax.all_gather(results, OWNER_AXES, axis=0, tiled=True)  60 us
    dot_general x18, matrix products, _mm_nt(): lax.dot_general(a, b, (((1,), (1,)), ((), ())), precision=HIGH, preferred...  47.5 us
    all_gather x1, waiting for transfers between devices, body(): gathered = lax.all_gather(gathered, axis, axis=0, tiled=True)  43 us
    all_gather x2, blocking collectives, body(): gathered = lax.all_gather(gathered, axis, axis=0, tiled=True)  26.5 us
    dot_general x10, matrix products, body(): lax.dot_general(columns[:, j * block:], columns[:, j * block:(j + 1) * bl...  24.7 us
  transfers between devices with their start and end apart: 7, of which 6 were waited for; matrix products, arithmetic and copies ran while one was open for 2% of the time, Pallas kernels for 0%

profile of v8, /device:TPU:2, one launch (start us, length us, event | category | flops | bytes accessed | tf_op | source)
XLA Modules:
  0.0 647.5 jit_solution(13250207482063701550)
XLA Ops:
  7.8 5.9 all-to-all-start
  15.0 5.0 gather_fusion
  20.0 4.7 broadcast_select_fusion
  24.7 5.1 all-to-all-start.1
  30.2 93.7 %all-to-all-done.1 = bf16[8,512,512]{2,1,0:T(8,128)(2,1)} async-done(((bf16[8,512,512]{2,1,0:T(8,128)(2,1)}), bf16[8,512,512]{2,1,0:T(8,128)(2,1)}, u32[]{:S(2)}, u32[]{:S(2)}) %all-to-all-start.1) | async-done | bytes 4194336 | tf_op jit(solution)/shard_map/all_to_all | solution.py:189
  125.2 2.3 slice.732
  127.5 3.9 fusion.109
  131.3 2.2 pad_select_fusion
  133.5 4.7 maximum_select_fusion
  138.3 3.8 convolution_dynamic-update-slice_fusion
  142.0 3.5 fusion.14
  145.5 3.2 fusion.21
  148.7 2.9 fusion.24
  151.5 2.6 fusion.27
  154.1 2.7 fusion.30
  156.8 2.0 fusion.34
  163.7 45.5 %reduce-scatter.4.cloned.1.call-done = f32[1792,128]{1,0:T(8,128)} async-done(((f32[7168,128]{1,0:T(8,128)}), f32[1792,128]{1,0:T(8,128)}) %reduce-scatter.4.cloned.1.call-update) | async-done | bytes 917520 | tf_op jit(solution)/shard_map/reduce_scatter | solution.py:207
  209.2 25.5 %reduce-scatter.6.cloned.1.call-done = f32[448,128]{1,0:T(8,128)} async-done(((f32[1792,128]{1,0:T(8,128)}), f32[448,128]{1,0:T(8,128)}) %reduce-scatter.6.cloned.1.call-update) | async-done | bytes 229392 | tf_op jit(solution)/shard_map/reduce_scatter | solution.py:207
  234.8 27.7 %reduce-scatter.8.cloned.1.call-done = f32[224,128]{1,0:T(8,128)} async-done(((f32[448,128]{1,0:T(8,128)}), f32[224,128]{1,0:T(8,128)}) %reduce-scatter.8.cloned.1.call-update) | async-done | bytes 114704 | tf_op jit(solution)/shard_map/reduce_scatter | solution.py:207
  262.4 12.1 %all_gather.12 = f32[448,128]{1,0:T(8,128)S(1)} all-gather(f32[224,128]{1,0:T(8,128)} %reduce-scatter.8.cloned.1.call-done), channel_id=1, replica_groups=mesh['dp_x'=4,'dp_z'=2,'dp_y'=4,'owner_z'=4,'owner_c'=2] {'dp_z'}, dimensions={0}, use_global_device_ids=true | all-gather | bytes 344064 | tf_op jit(solution)/shard_map/all_gather | solution.py:210
  274.6 14.3 %all_gather.13 = f32[1792,128]{1,0:T(8,128)} all-gather(f32[448,128]{1,0:T(8,128)S(1)} %all_gather.12), channel_id=1, replica_groups=mesh['dp_x'=4,'dp_z'=2,'dp_y'=4,'owner_z'=4,'owner_c'=2] {'dp_x'}, dimensions={0}, use_global_device_ids=true | all-gather | bytes 1146880 | tf_op jit(solution)/shard_map/all_gather | solution.py:210
  289.0 43.0 %all-gather.4.cloned.1.call-done = f32[7168,128]{1,0:T(8,128)} async-done(((f32[1792,128]{1,0:T(8,128)}), f32[7168,128]{1,0:T(8,128)}) %all-gather.4.cloned.1.call-update) | async-done | bytes 3670032 | tf_op jit(solution)/shard_map/all_gather | solution.py:210
  336.4 2.5 copy-done
  339.6 15.7 %shard_map.37 = f32[128,128]{1,0:T(8,128)} custom-call(f32[128,128]{1,0:T(8,128)} %select_add_fusion.9.a_ref), custom_call_target="tpu_custom_call" | custom-call | flops 12582912 | bytes 131072 | tf_op jit(solution)/shard_map/pallas_call | solution.py:124
  357.9 7.3 %constant_dynamic-update-slice_fusion.46 = (f32[1280,1152]{1,0:T(8,128)}, f32[1152,1024]{1,0:T(8,128)S(1)}) fusion(f32[1280,1152]{1,0:T(8,128)} %constant_dynamic-update-slice_fusion.47, f32[1152,128]{1,0:T(8,128)S(1)} %fusion.54), kind=kOutput, calls=%fused_computation.198 | convolution fusion | flops 1814298624 | bytes 15269888 | tf_op jit(solution)/shard_map/dot_general | solution.py:85
  365.2 2.2 copy-done.1
  368.0 15.7 %shard_map.38 = f32[128,128]{1,0:T(8,128)} custom-call(f32[128,128]{1,0:T(8,128)} %select_add_fusion.8.a_ref), custom_call_target="tpu_custom_call" | custom-call | flops 12582912 | bytes 131072 | tf_op jit(solution)/shard_map/pallas_call | solution.py:124
  383.7 2.5 constant_dynamic-update-slice_fusion.45
  386.2 6.0 constant_dynamic-update-slice_fusion.44
  394.7 15.7 %shard_map.39 = f32[128,128]{1,0:T(8,128)} custom-call(f32[128,128]{1,0:T(8,128)} %select_add_fusion.7.a_ref), custom_call_target="tpu_custom_call" | custom-call | flops 12582912 | bytes 131072 | tf_op jit(solution)/shard_map/pallas_call | solution.py:124
  410.3 2.4 constant_dynamic-update-slice_fusion.43
  412.7 5.7 constant_dynamic-update-slice_fusion.42
  419.1 15.7 %shard_map.40 = f32[128,128]{1,0:T(8,128)} custom-call(f32[128,128]{1,0:T(8,128)} %select_add_fusion.6.a_ref), custom_call_target="tpu_custom_call" | custom-call | flops 12582912 | bytes 131072 | tf_op jit(solution)/shard_map/pallas_call | solution.py:124
  434.8 2.1 constant_dynamic-update-slice_fusion.41
  436.9 4.7 constant_dynamic-update-slice_fusion.40
  442.2 15.7 %shard_map.41 = f32[128,128]{1,0:T(8,128)} custom-call(f32[128,128]{1,0:T(8,128)} %select_add_fusion.5.a_ref), custom_call_target="tpu_custom_call" | custom-call | flops 12582912 | bytes 131072 | tf_op jit(solution)/shard_map/pallas_call | solution.py:124
  457.9 2.0 constant_dynamic-update-slice_fusion.39
  459.9 2.5 fusion.19
  464.3 15.7 %shard_map.42 = f32[128,128]{1,0:T(8,128)} custom-call(f32[128,128]{1,0:T(8,128)} %select_add_fusion.4.a_ref), custom_call_target="tpu_custom_call" | custom-call | flops 12582912 | bytes 131072 | tf_op jit(solution)/shard_map/pallas_call | solution.py:124
  480.0 2.0 constant_dynamic-update-slice_fusion.37
  487.1 15.6 %shard_map.46 = f32[128,128]{1,0:T(8,128)} custom-call(f32[128,128]{1,0:T(8,128)} %select_add_fusion.a_ref), custom_call_target="tpu_custom_call" | custom-call | flops 12582912 | bytes 131072 | tf_op jit(solution)/shard_map/pallas_call | solution.py:124
  502.7 15.7 %shard_map.43 = f32[128,128]{1,0:T(8,128)} custom-call(f32[128,128]{1,0:T(8,128)} %select_add_fusion.3.a_ref), custom_call_target="tpu_custom_call" | custom-call | flops 12582912 | bytes 131072 | tf_op jit(solution)/shard_map/pallas_call | solution.py:124
  522.4 15.7 %shard_map.44 = f32[128,128]{1,0:T(8,128)} custom-call(f32[128,128]{1,0:T(8,128)} %select_add_fusion.2.a_ref), custom_call_target="tpu_custom_call" | custom-call | flops 12582912 | bytes 131072 | tf_op jit(solution)/shard_map/pallas_call | solution.py:124
  540.1 15.7 %shard_map.45 = f32[128,128]{1,0:T(8,128)} custom-call(f32[128,128]{1,0:T(8,128)} %select_add_fusion.1.a_ref), custom_call_target="tpu_custom_call" | custom-call | flops 12582912 | bytes 131072 | tf_op jit(solution)/shard_map/pallas_call | solution.py:124
  568.9 1.9 convolution_subtract_fusion.1
  571.2 2.1 convolution_subtract_fusion
  575.8 60.0 %all-gather.6.cloned.1.call-done = f32[9216,128]{1,0:T(8,128)} async-done(((f32[1152,128]{1,0:T(8,128)}), f32[9216,128]{1,0:T(8,128)}) %all-gather.6.cloned.1.call-update) | async-done | bytes 4718608 | tf_op jit(solution)/shard_map/all_gather | solution.py:213
  635.9 4.9 copy.91
  (138 shorter events, 49.8 us)
Async XLA Ops:
  7.8 16.9 %all-to-all-start = ((s32[8,1,4]{2,1,0:T(1,128)}), s32[8,1,4]{2,1,0:T(1,128)S(1)}, u32[]{:S(2)}, u32[]{:S(2)}) async-start(s32[8,1,4]{2,1,0:T(1,128)} %broadcast_in_dim.59), calls=%async_computation | async-start | bytes 8192 | tf_op jit(solution)/shard_map/all_to_all | solution.py:190
  24.7 99.2 %all-to-all-start.1 = ((bf16[8,512,512]{2,1,0:T(8,128)(2,1)}), bf16[8,512,512]{2,1,0:T(8,128)(2,1)}, u32[]{:S(2)}, u32[]{:S(2)}) async-start(bf16[8,512,512]{2,1,0:T(8,128)(2,1)} %broadcast_select_fusion), calls=%async_computation.1 | async-start | bytes 8388608 | tf_op jit(solution)/shard_map/all_to_all | solution.py:189
  29.8 179.4 %reduce-scatter.4.cloned.1.call-start = ((), (), s32[]{:S(2)}) async-start(), calls=%async_computation.5 | async-start | bytes 4587520 | tf_op jit(solution)/shard_map/reduce_scatter | solution.py:207
  163.6 71.0 %reduce-scatter.6.cloned.1.call-start = ((), (), s32[]{:S(2)}) async-start(), calls=%async_computation.6 | async-start | bytes 1146880 | tf_op jit(solution)/shard_map/reduce_scatter | solution.py:207
  209.2 53.2 %reduce-scatter.8.cloned.1.call-start = ((), (), s32[]{:S(2)}) async-start(), calls=%async_computation.7 | async-start | bytes 344064 | tf_op jit(solution)/shard_map/reduce_scatter | solution.py:207
  234.7 97.3 %all-gather.4.cloned.1.call-start = ((), (), s32[]{:S(2)}) async-start(), calls=%async_computation.8 | async-start | bytes 4587520 | tf_op jit(solution)/shard_map/all_gather | solution.py:210
  288.9 347.0 %all-gather.6.cloned.1.call-start = ((), (), s32[]{:S(2)}) async-start(), calls=%async_computation.9 | async-start | bytes 5308416 | tf_op jit(solution)/shard_map/all_gather | solution.py:213
  332.0 3.6 slice-start
  332.0 3.7 slice-start.1
  332.0 3.7 slice-start.2
  332.0 3.8 slice-start.3
  333.2 2.6 slice-start.4
  334.4 1.5 slice-start.5
  336.4 2.5 copy-start
  365.2 2.2 copy-start.1
  392.2 1.8 copy-start.2
  463.7 100.6 %copy-start.8 = (f32[128,128]{1,0:T(8,128)S(1)}, f32[128,128]{1,0:T(8,128)}, u32[]{:S(2)}) copy-start(f32[128,128]{1,0:T(8,128)} %shard_map.41) | copy-start | bytes 196612
  480.0 82.4 %copy-start.9 = (f32[128,128]{1,0:T(8,128)S(1)}, f32[128,128]{1,0:T(8,128)}, u32[]{:S(2)}) copy-start(f32[128,128]{1,0:T(8,128)} %shard_map.42) | copy-start | bytes 196612
  480.0 86.3 %copy-start.7 = (f32[128,128]{1,0:T(8,128)S(1)}, f32[128,128]{1,0:T(8,128)}, u32[]{:S(2)}) copy-start(f32[128,128]{1,0:T(8,128)} %shard_map.40) | copy-start | bytes 196612
  483.9 84.5 %copy-start.6 = (f32[128,128]{1,0:T(8,128)S(1)}, f32[128,128]{1,0:T(8,128)}, u32[]{:S(2)}) copy-start(f32[128,128]{1,0:T(8,128)} %shard_map.39) | copy-start | bytes 196612
  485.0 85.8 %copy-start.5 = (f32[128,128]{1,0:T(8,128)S(1)}, f32[128,128]{1,0:T(8,128)}, u32[]{:S(2)}) copy-start(f32[128,128]{1,0:T(8,128)} %shard_map.38) | copy-start | bytes 196612
  521.7 51.6 %copy-start.3 = (f32[128,128]{1,0:T(8,128)S(1)}, f32[128,128]{1,0:T(8,128)}, u32[]{:S(2)}) copy-start(f32[128,128]{1,0:T(8,128)} %shard_map.37) | copy-start | bytes 196612
  539.5 34.3 %copy-start.4 = (f32[128,128]{1,0:T(8,128)S(1)}, f32[128,128]{1,0:T(8,128)}, u32[]{:S(2)}) copy-start(f32[128,128]{1,0:T(8,128)} %shard_map.46) | copy-start | bytes 196612
Sparse Core Ops, SparseCore 0:
  163.8 45.3 reduce-scatter.3
  211.7 22.9 reduce-scatter.5
  237.2 25.1 reduce-scatter.7
  289.0 42.9 all-gather.3
  576.0 59.8 all-gather.5

commit v9 on v8

--- a/solution.py
+++ b/solution.py
@@ -100,24 +100,27 @@
     lane = lax.broadcasted_iota(jnp.int32, (n, n), 1)
     w_ref[...] = jnp.where(sub == lane, 1.0, 0.0).astype(jnp.float32)
     lane_row = lax.broadcasted_iota(jnp.int32, (1, n), 1)
-    sub_col = lax.broadcasted_iota(jnp.int32, (n, 1), 0)
-
-    def step(j, carry):
-        a = s_ref[...]
-        row = s_ref[pl.ds(j, 1), :]
-        pivot = jnp.sum(jnp.where(lane_row == j, row, 0.0), axis=1, keepdims=True)
-        inv_root = 1.0 / jnp.sqrt(pivot)
-        col = jnp.sum(jnp.where(lane == j, a, 0.0), axis=1, keepdims=True)
-        lcol = jnp.where(sub_col > j, col * inv_root, 0.0)
-        lrow = jnp.where(lane_row >= j, row * inv_root, 0.0)
-        s_ref[...] = a - lcol * lrow
-        wrow = w_ref[pl.ds(j, 1), :] * inv_root
-        w_ref[...] = w_ref[...] - lcol * wrow
-        w_ref[pl.ds(j, 1), :] = wrow
-        return carry
-
-    lax.fori_loop(0, n, step, 0)
-
+    seg = 16
+    for start in range(0, n, seg):
+        rows = n - start
+        lane_t = lax.broadcasted_iota(jnp.int32, (rows, n), 1)
+        sub_col = lax.broadcasted_iota(jnp.int32, (rows, 1), 0) + start
+
+        def step(j, carry, start=start, lane_t=lane_t, sub_col=sub_col):
+            a = s_ref[start:, :]
+            row = s_ref[pl.ds(j, 1), :]
+            pivot = jnp.sum(jnp.where(lane_row == j, row, 0.0), axis=1, keepdims=True)
+            inv_root = 1.0 / jnp.sqrt(pivot)
+            col = jnp.sum(jnp.where(lane_t == j, a, 0.0), axis=1, keepdims=True)
+            lcol = jnp.where(sub_col > j, col * inv_root, 0.0)
+            lrow = jnp.where(lane_row >= j, row * inv_root, 0.0)
+            s_ref[start:, :] = a - lcol * lrow
+            wrow = w_ref[pl.ds(j, 1), :] * inv_root
+            w_ref[start:, :] = w_ref[start:, :] - lcol * wrow
+            w_ref[pl.ds(j, 1), :] = wrow
+            return carry
+
+        lax.fori_loop(start, start + seg, step, 0)
 
 def _chol_inverse(block):
     n = block.shape[0]
@@ -183,7 +186,7 @@
     n_owners = lax.axis_size(OWNER_AXES[0]) * lax.axis_size(OWNER_AXES[1])
     per_owner = layer_count // n_owners
     total_rows = n_replicas * n_owners * positions
-    ordered = jnp.take(line_columns, layer_owner, axis=0)
+    ordered = jnp.take(line_columns, layer_owner, axis=0, mode="clip")
     width_copies = jnp.broadcast_to(line_widths[None, :, :], (n_owners, 1, line_widths.shape[1]))
     received, source_widths = (
         lax.all_to_all(ordered, OWNER_AXES, split_axis=0, concat_axis=1, tiled=True),

time: 653 us -> 640 us (0.980)
  Pallas kernels: 157 us -> 150 us
    pallas_call x10, Pallas kernels: 157 us -> 150 us  [_chol_inverse(): pl.pallas_call(_leaf_kernel, out_shape=jax.ShapeDtypeStruct((n, n), jnp.f...]
  transfers between devices with their start and end apart: 7 -> 7, of which waited for: 6 -> 6; matrix products, arithmetic and copies ran while one was open for 2% -> 1% of each run, Pallas kernels for 0% -> 0%
where the time goes in v9:
time: 640 us; the launch traced here: 635 us
  waiting for transfers between devices  295 us (46%)
  Pallas kernels  150 us (23%)
  matrix products  89.9 us (14%)
  local copies, waits for them, and re-layouts  33 us (5%)
  blocking collectives  26.5 us (4%)
  other arithmetic  15.5 us (2%)
  between operations  14.1 us (2%)
  starting transfers between devices  11.2 us (2%)
    pallas_call x10, Pallas kernels, _chol_inverse(): pl.pallas_call(_leaf_kernel, out_shape=jax.ShapeDtypeStruct((n, n), jnp.f...  150 us
    reduce_scatter x3, waiting for transfers between devices, body(): mine = lax.psum_scatter(mine, axis, scatter_dimension=0, tiled=True)  98.6 us
    all_to_all x1, waiting for transfers between devices, body(): lax.all_to_all(ordered, OWNER_AXES, split_axis=0, concat_axis=1, tiled=True)  93.7 us
    all_gather x1, waiting for transfers between devices, body(): return lax.all_gather(results, OWNER_AXES, axis=0, tiled=True)  60 us
    dot_general x18, matrix products, _mm_nt(): lax.dot_general(a, b, (((1,), (1,)), ((), ())), precision=HIGH, preferred...  47.5 us
    all_gather x1, waiting for transfers between devices, body(): gathered = lax.all_gather(gathered, axis, axis=0, tiled=True)  43 us
    all_gather x2, blocking collectives, body(): gathered = lax.all_gather(gathered, axis, axis=0, tiled=True)  26.5 us
    dot_general x10, matrix products, body(): lax.dot_general(columns[:, j * block:], columns[:, j * block:(j + 1) * bl...  24.7 us
  transfers between devices with their start and end apart: 7, of which 6 were waited for; matrix products, arithmetic and copies ran while one was open for 1% of the time, Pallas kernels for 0%

profile of v9, /device:TPU:2, one launch (start us, length us, event | category | flops | bytes accessed | tf_op | source)
XLA Modules:
  0.0 635.3 jit_solution(8373763203921148273)
XLA Ops:
  7.8 5.9 all-to-all-start
  14.3 5.0 gather_fusion
  19.3 5.1 all-to-all-start.1
  24.9 93.7 %all-to-all-done.1 = bf16[8,512,512]{2,1,0:T(8,128)(2,1)} async-done(((bf16[8,512,512]{2,1,0:T(8,128)(2,1)}), bf16[8,512,512]{2,1,0:T(8,128)(2,1)}, u32[]{:S(2)}, u32[]{:S(2)}) %all-to-all-start.1) | async-done | bytes 4194336 | tf_op jit(solution)/shard_map/all_to_all | solution.py:192
  119.9 2.3 slice.732
  122.1 3.9 fusion.109
  126.0 2.2 pad_select_fusion
  128.2 4.7 maximum_select_fusion
  132.9 3.8 convolution_dynamic-update-slice_fusion
  136.7 3.5 fusion.14
  140.2 3.2 fusion.21
  143.3 2.9 fusion.24
  146.2 2.6 fusion.27
  148.8 2.7 fusion.30
  151.5 2.0 fusion.34
  158.4 45.5 %reduce-scatter.4.cloned.1.call-done = f32[1792,128]{1,0:T(8,128)} async-done(((f32[7168,128]{1,0:T(8,128)}), f32[1792,128]{1,0:T(8,128)}) %reduce-scatter.4.cloned.1.call-update) | async-done | bytes 917520 | tf_op jit(solution)/shard_map/reduce_scatter | solution.py:210
  203.9 25.5 %reduce-scatter.6.cloned.1.call-done = f32[448,128]{1,0:T(8,128)} async-done(((f32[1792,128]{1,0:T(8,128)}), f32[448,128]{1,0:T(8,128)}) %reduce-scatter.6.cloned.1.call-update) | async-done | bytes 229392 | tf_op jit(solution)/shard_map/reduce_scatter | solution.py:210
  229.4 27.7 %reduce-scatter.8.cloned.1.call-done = f32[224,128]{1,0:T(8,128)} async-done(((f32[448,128]{1,0:T(8,128)}), f32[224,128]{1,0:T(8,128)}) %reduce-scatter.8.cloned.1.call-update) | async-done | bytes 114704 | tf_op jit(solution)/shard_map/reduce_scatter | solution.py:210
  257.1 12.1 %all_gather.12 = f32[448,128]{1,0:T(8,128)S(1)} all-gather(f32[224,128]{1,0:T(8,128)} %reduce-scatter.8.cloned.1.call-done), channel_id=1, replica_groups=mesh['dp_x'=4,'dp_z'=2,'dp_y'=4,'owner_z'=4,'owner_c'=2] {'dp_z'}, dimensions={0}, use_global_device_ids=true | all-gather | bytes 344064 | tf_op jit(solution)/shard_map/all_gather | solution.py:213
  269.2 14.3 %all_gather.13 = f32[1792,128]{1,0:T(8,128)} all-gather(f32[448,128]{1,0:T(8,128)S(1)} %all_gather.12), channel_id=1, replica_groups=mesh['dp_x'=4,'dp_z'=2,'dp_y'=4,'owner_z'=4,'owner_c'=2] {'dp_x'}, dimensions={0}, use_global_device_ids=true | all-gather | bytes 1146880 | tf_op jit(solution)/shard_map/all_gather | solution.py:213
  283.6 43.0 %all-gather.4.cloned.1.call-done = f32[7168,128]{1,0:T(8,128)} async-done(((f32[1792,128]{1,0:T(8,128)}), f32[7168,128]{1,0:T(8,128)}) %all-gather.4.cloned.1.call-update) | async-done | bytes 3670032 | tf_op jit(solution)/shard_map/all_gather | solution.py:213
  331.1 2.5 copy-done
  334.2 15.0 %shard_map.37 = f32[128,128]{1,0:T(8,128)} custom-call(f32[128,128]{1,0:T(8,128)} %select_add_fusion.9.a_ref), custom_call_target="tpu_custom_call" | custom-call | flops 12582912 | bytes 131072 | tf_op jit(solution)/shard_map/pallas_call | solution.py:127
  351.8 7.3 %constant_dynamic-update-slice_fusion.46 = (f32[1280,1152]{1,0:T(8,128)}, f32[1152,1024]{1,0:T(8,128)S(1)}) fusion(f32[1280,1152]{1,0:T(8,128)} %constant_dynamic-update-slice_fusion.47, f32[1152,128]{1,0:T(8,128)S(1)} %fusion.54), kind=kOutput, calls=%fused_computation.195 | convolution fusion | flops 1814298624 | bytes 15269888 | tf_op jit(solution)/shard_map/dot_general | solution.py:85
  359.2 2.2 copy-done.1
  362.0 15.0 %shard_map.38 = f32[128,128]{1,0:T(8,128)} custom-call(f32[128,128]{1,0:T(8,128)} %select_add_fusion.8.a_ref), custom_call_target="tpu_custom_call" | custom-call | flops 12582912 | bytes 131072 | tf_op jit(solution)/shard_map/pallas_call | solution.py:127
  376.9 2.5 constant_dynamic-update-slice_fusion.45
  379.5 6.0 constant_dynamic-update-slice_fusion.44
  388.0 15.0 %shard_map.39 = f32[128,128]{1,0:T(8,128)} custom-call(f32[128,128]{1,0:T(8,128)} %select_add_fusion.7.a_ref), custom_call_target="tpu_custom_call" | custom-call | flops 12582912 | bytes 131072 | tf_op jit(solution)/shard_map/pallas_call | solution.py:127
  402.9 2.4 constant_dynamic-update-slice_fusion.43
  405.3 5.7 constant_dynamic-update-slice_fusion.42
  411.7 15.0 %shard_map.40 = f32[128,128]{1,0:T(8,128)} custom-call(f32[128,128]{1,0:T(8,128)} %select_add_fusion.6.a_ref), custom_call_target="tpu_custom_call" | custom-call | flops 12582912 | bytes 131072 | tf_op jit(solution)/shard_map/pallas_call | solution.py:127
  426.7 2.1 constant_dynamic-update-slice_fusion.41
  428.8 4.7 constant_dynamic-update-slice_fusion.40
  434.1 15.1 %shard_map.41 = f32[128,128]{1,0:T(8,128)} custom-call(f32[128,128]{1,0:T(8,128)} %select_add_fusion.5.a_ref), custom_call_target="tpu_custom_call" | custom-call | flops 12582912 | bytes 131072 | tf_op jit(solution)/shard_map/pallas_call | solution.py:127
  449.2 2.0 constant_dynamic-update-slice_fusion.39
  451.3 2.5 fusion.19
  455.7 15.0 %shard_map.42 = f32[128,128]{1,0:T(8,128)} custom-call(f32[128,128]{1,0:T(8,128)} %select_add_fusion.4.a_ref), custom_call_target="tpu_custom_call" | custom-call | flops 12582912 | bytes 131072 | tf_op jit(solution)/shard_map/pallas_call | solution.py:127
  470.6 2.0 constant_dynamic-update-slice_fusion.37
  472.7 1.9 fusion.20
  477.8 15.0 %shard_map.46 = f32[128,128]{1,0:T(8,128)} custom-call(f32[128,128]{1,0:T(8,128)} %select_add_fusion.a_ref), custom_call_target="tpu_custom_call" | custom-call | flops 12582912 | bytes 131072 | tf_op jit(solution)/shard_map/pallas_call | solution.py:127
  492.7 15.0 %shard_map.43 = f32[128,128]{1,0:T(8,128)} custom-call(f32[128,128]{1,0:T(8,128)} %select_add_fusion.3.a_ref), custom_call_target="tpu_custom_call" | custom-call | flops 12582912 | bytes 131072 | tf_op jit(solution)/shard_map/pallas_call | solution.py:127
  511.7 15.0 %shard_map.44 = f32[128,128]{1,0:T(8,128)} custom-call(f32[128,128]{1,0:T(8,128)} %select_add_fusion.2.a_ref), custom_call_target="tpu_custom_call" | custom-call | flops 12582912 | bytes 131072 | tf_op jit(solution)/shard_map/pallas_call | solution.py:127
  528.7 15.0 %shard_map.45 = f32[128,128]{1,0:T(8,128)} custom-call(f32[128,128]{1,0:T(8,128)} %select_add_fusion.1.a_ref), custom_call_target="tpu_custom_call" | custom-call | flops 12582912 | bytes 131072 | tf_op jit(solution)/shard_map/pallas_call | solution.py:127
  556.8 1.9 convolution_subtract_fusion.1
  559.1 2.1 convolution_subtract_fusion
  563.7 60.0 %all-gather.6.cloned.1.call-done = f32[9216,128]{1,0:T(8,128)} async-done(((f32[1152,128]{1,0:T(8,128)}), f32[9216,128]{1,0:T(8,128)}) %all-gather.6.cloned.1.call-update) | async-done | bytes 4718608 | tf_op jit(solution)/shard_map/all_gather | solution.py:216
  623.8 4.9 copy.91
  (135 shorter events, 47.2 us)
Async XLA Ops:
  7.8 11.6 %all-to-all-start = ((s32[8,1,4]{2,1,0:T(1,128)}), s32[8,1,4]{2,1,0:T(1,128)S(1)}, u32[]{:S(2)}, u32[]{:S(2)}) async-start(s32[8,1,4]{2,1,0:T(1,128)} %broadcast_in_dim.51), calls=%async_computation | async-start | bytes 8192 | tf_op jit(solution)/shard_map/all_to_all | solution.py:193
  19.3 99.2 %all-to-all-start.1 = ((bf16[8,512,512]{2,1,0:T(8,128)(2,1)}), bf16[8,512,512]{2,1,0:T(8,128)(2,1)}, u32[]{:S(2)}, u32[]{:S(2)}) async-start(bf16[8,512,512]{2,1,0:T(8,128)(2,1)} %gather_fusion), calls=%async_computation.1 | async-start | bytes 8388608 | tf_op jit(solution)/shard_map/all_to_all | solution.py:192
  24.4 179.4 %reduce-scatter.4.cloned.1.call-start = ((), (), s32[]{:S(2)}) async-start(), calls=%async_computation.5 | async-start | bytes 4587520 | tf_op jit(solution)/shard_map/reduce_scatter | solution.py:210
  158.3 71.0 %reduce-scatter.6.cloned.1.call-start = ((), (), s32[]{:S(2)}) async-start(), calls=%async_computation.6 | async-start | bytes 1146880 | tf_op jit(solution)/shard_map/reduce_scatter | solution.py:210
  203.8 53.2 %reduce-scatter.8.cloned.1.call-start = ((), (), s32[]{:S(2)}) async-start(), calls=%async_computation.7 | async-start | bytes 344064 | tf_op jit(solution)/shard_map/reduce_scatter | solution.py:210
  229.4 97.3 %all-gather.4.cloned.1.call-start = ((), (), s32[]{:S(2)}) async-start(), calls=%async_computation.8 | async-start | bytes 4587520 | tf_op jit(solution)/shard_map/all_gather | solution.py:213
  283.6 340.2 %all-gather.6.cloned.1.call-start = ((), (), s32[]{:S(2)}) async-start(), calls=%async_computation.9 | async-start | bytes 5308416 | tf_op jit(solution)/shard_map/all_gather | solution.py:216
  326.7 3.6 slice-start
  326.7 3.7 slice-start.1
  326.7 3.7 slice-start.2
  326.7 3.8 slice-start.3
  327.9 2.6 slice-start.4
  329.1 1.5 slice-start.5
  331.1 2.5 copy-start
  359.2 2.2 copy-start.1
  385.5 1.8 copy-start.2
  455.0 97.1 %copy-start.8 = (f32[128,128]{1,0:T(8,128)S(1)}, f32[128,128]{1,0:T(8,128)}, u32[]{:S(2)}) copy-start(f32[128,128]{1,0:T(8,128)} %shard_map.41) | copy-start | bytes 196612
  470.6 79.7 %copy-start.9 = (f32[128,128]{1,0:T(8,128)S(1)}, f32[128,128]{1,0:T(8,128)}, u32[]{:S(2)}) copy-start(f32[128,128]{1,0:T(8,128)} %shard_map.42) | copy-start | bytes 196612
  470.6 83.6 %copy-start.7 = (f32[128,128]{1,0:T(8,128)S(1)}, f32[128,128]{1,0:T(8,128)}, u32[]{:S(2)}) copy-start(f32[128,128]{1,0:T(8,128)} %shard_map.40) | copy-start | bytes 196612
  474.6 81.8 %copy-start.6 = (f32[128,128]{1,0:T(8,128)S(1)}, f32[128,128]{1,0:T(8,128)}, u32[]{:S(2)}) copy-start(f32[128,128]{1,0:T(8,128)} %shard_map.39) | copy-start | bytes 196612
  475.6 83.1 %copy-start.5 = (f32[128,128]{1,0:T(8,128)S(1)}, f32[128,128]{1,0:T(8,128)}, u32[]{:S(2)}) copy-start(f32[128,128]{1,0:T(8,128)} %shard_map.38) | copy-start | bytes 196612
  511.0 50.2 %copy-start.3 = (f32[128,128]{1,0:T(8,128)S(1)}, f32[128,128]{1,0:T(8,128)}, u32[]{:S(2)}) copy-start(f32[128,128]{1,0:T(8,128)} %shard_map.37) | copy-start | bytes 196612
  528.0 33.6 %copy-start.4 = (f32[128,128]{1,0:T(8,128)S(1)}, f32[128,128]{1,0:T(8,128)}, u32[]{:S(2)}) copy-start(f32[128,128]{1,0:T(8,128)} %shard_map.46) | copy-start | bytes 196612
Sparse Core Ops, SparseCore 0:
  158.4 45.3 reduce-scatter.3
  206.4 22.9 reduce-scatter.5
  231.8 25.1 reduce-scatter.7
  283.7 42.9 all-gather.3
  563.8 59.8 all-gather.5

commit v10 on v9

--- a/solution.py
+++ b/solution.py
@@ -188,12 +188,19 @@
     total_rows = n_replicas * n_owners * positions
     ordered = jnp.take(line_columns, layer_owner, axis=0, mode="clip")
     width_copies = jnp.broadcast_to(line_widths[None, :, :], (n_owners, 1, line_widths.shape[1]))
-    received, source_widths = (
-        lax.all_to_all(ordered, OWNER_AXES, split_axis=0, concat_axis=1, tiled=True),
-        lax.all_to_all(width_copies, OWNER_AXES, split_axis=0, concat_axis=1, tiled=True),
-    )
-    blocks = received.reshape(per_owner, n_owners, positions, packed_width)
-    columns = patch_columns(blocks, source_widths.reshape(n_owners, line_widths.shape[1]))
+    source_widths = lax.all_to_all(width_copies, OWNER_AXES, split_axis=0, concat_axis=1, tiled=True)
+    source_widths = source_widths.reshape(n_owners, line_widths.shape[1])
+    me = lax.axis_index(OWNER_AXES)
+    pieces = [lax.dynamic_index_in_dim(ordered, me, 0, keepdims=False)]
+    piece_widths = [lax.dynamic_index_in_dim(source_widths, me, 0, keepdims=False)]
+    for k in range(1, n_owners):
+        outgoing = lax.dynamic_index_in_dim(ordered, (me + k) % n_owners, 0, keepdims=False)
+        perm = [(o, (o + k) % n_owners) for o in range(n_owners)]
+        pieces.append(lax.ppermute(outgoing, OWNER_AXES, perm))
+        piece_widths.append(
+            lax.dynamic_index_in_dim(source_widths, (me - k) % n_owners, 0, keepdims=False))
+    blocks = jnp.stack(pieces)[None]
+    columns = patch_columns(blocks, jnp.stack(piece_widths))
     columns = columns.reshape(n_owners * positions, full_width)
     block = 128
     nb = full_width // block

time: 640 us -> 658 us (1.028)
  waiting for transfers between devices: 295 us -> 266 us
  starting transfers between devices: 11.2 us -> 34 us
  matrix products: 89.9 us -> 102 us
  local copies, waits for them, and re-layouts: 33 us -> 40.9 us
    all_to_all x1 -> x0, waiting for transfers between devices: 93.7 us -> none  [body(): lax.all_to_all(ordered, OWNER_AXES, split_axis=0, concat_axis=1, tiled=True)]
    ppermute x0 -> x7, waiting for transfers between devices: none -> 60 us  [body(): pieces.append(lax.ppermute(outgoing, OWNER_AXES, perm))]
    ppermute x0 -> x7, starting transfers between devices: none -> 27.9 us  [body(): pieces.append(lax.ppermute(outgoing, OWNER_AXES, perm))]
    dot_general x10, matrix products: 24.7 us -> 36.8 us  [body(): lax.dot_general(columns[:, j * block:], columns[:, j * block:(j + 1) * bl...]
    unnamed x55 -> x63, local copies, waits for them, and re-layouts: 13.1 us -> 18.2 us
  transfers between devices with their start and end apart: 7 -> 13, of which waited for: 6 -> 7; matrix products, arithmetic and copies ran while one was open for 1% -> 2% of each run, Pallas kernels for 0% -> 0%
where the time goes in v10:
time: 658 us; the launch traced here: 649 us
  waiting for transfers between devices  266 us (40%)
  Pallas kernels  150 us (23%)
  matrix products  102 us (16%)
  local copies, waits for them, and re-layouts  40.9 us (6%)
  starting transfers between devices  34 us (5%)
  blocking collectives  26.5 us (4%)
  other arithmetic  15.7 us (2%)
  between operations  14.4 us (2%)
    pallas_call x10, Pallas kernels, _chol_inverse(): pl.pallas_call(_leaf_kernel, out_shape=jax.ShapeDtypeStruct((n, n), jnp.f...  150 us
    reduce_scatter x3, waiting for transfers between devices, body(): mine = lax.psum_scatter(mine, axis, scatter_dimension=0, tiled=True)  103 us
    all_gather x1, waiting for transfers between devices, body(): return lax.all_gather(results, OWNER_AXES, axis=0, tiled=True)  60 us
    ppermute x7, waiting for transfers between devices, body(): pieces.append(lax.ppermute(outgoing, OWNER_AXES, perm))  60 us
    dot_general x18, matrix products, _mm_nt(): lax.dot_general(a, b, (((1,), (1,)), ((), ())), precision=HIGH, preferred...  47.5 us
    all_gather x1, waiting for transfers between devices, body(): gathered = lax.all_gather(gathered, axis, axis=0, tiled=True)  43.1 us
    dot_general x10, matrix products, body(): lax.dot_general(columns[:, j * block:], columns[:, j * block:(j + 1) * bl...  36.8 us
    ppermute x7, starting transfers between devices, body(): pieces.append(lax.ppermute(outgoing, OWNER_AXES, perm))  27.9 us
  transfers between devices with their start and end apart: 13, of which 7 were waited for; matrix products, arithmetic and copies ran while one was open for 2% of the time, Pallas kernels for 0%

profile of v10, /device:TPU:2, one launch (start us, length us, event | category | flops | bytes accessed | tf_op | source)
XLA Modules:
  0.0 649.3 jit_solution(11989464043703169254)
XLA Ops:
  7.8 5.9 all-to-all-start
  14.5 5.0 gather_fusion
  19.5 4.0 dynamic-slice_bitcast_fusion
  23.5 3.4 collective-permute-start.6
  29.8 44.3 %collective-permute-done = bf16[512,512]{1,0:T(8,128)(2,1)S(1)} collective-permute-done((bf16[512,512]{1,0:T(8,128)(2,1)}, bf16[512,512]{1,0:T(8,128)(2,1)S(1)}, u32[]{:S(2)}, u32[]{:S(2)}) %collective-permute-start) | collective-permute-done | bytes 524320 | tf_op jit(solution)/shard_map/ppermute | solution.py:199
  74.1 22.4 %collective-permute-start.3 = (bf16[512,512]{1,0:T(8,128)(2,1)}, bf16[512,512]{1,0:T(8,128)(2,1)S(1)}, u32[]{:S(2)}, u32[]{:S(2)}) collective-permute-start(bf16[512,512]{1,0:T(8,128)(2,1)} %get-tuple-element.214), channel_id=1, source_target_pairs={{0,4},{1,5},{2,6},{3,7},{4,0},{5,1},{6,2},{7,3},{8,12},{9,13},{10,... | collective-permute-start | bytes 1572872 | tf_op jit(solution)/shard_map/ppermute | solution.py:199
  99.0 15.7 %collective-permute-done.3 = bf16[512,512]{1,0:T(8,128)(2,1)S(1)} collective-permute-done((bf16[512,512]{1,0:T(8,128)(2,1)}, bf16[512,512]{1,0:T(8,128)(2,1)S(1)}, u32[]{:S(2)}, u32[]{:S(2)}) %collective-permute-start.3) | collective-permute-done | bytes 524320 | tf_op jit(solution)/shard_map/ppermute | solution.py:199
  119.6 2.4 slice.732
  123.2 2.2 pad_select_fusion
  125.4 4.8 maximum_select_fusion
  130.2 3.8 convolution_dynamic-update-slice_fusion
  134.0 3.5 fusion.14
  137.5 3.2 fusion.21
  140.6 2.9 fusion.24
  143.5 2.6 fusion.27
  146.1 14.8 %fusion.30 = f32[7168,128]{1,0:T(8,128)} fusion(f32[7168,128]{1,0:T(8,128)} %fusion.27, bf16[4096,1280]{1,0:T(8,128)(2,1)S(1)} %maximum_select_fusion), kind=kOutput, calls=%fused_computation.34 | convolution fusion | flops 671088640 | bytes 6619136 | tf_op jit(solution)/shard_map/dot_general | solution.py:210
  160.9 2.0 fusion.34
  167.8 49.7 %reduce-scatter.4.cloned.1.call-done = f32[1792,128]{1,0:T(8,128)} async-done(((f32[7168,128]{1,0:T(8,128)}), f32[1792,128]{1,0:T(8,128)}) %reduce-scatter.4.cloned.1.call-update) | async-done | bytes 917520 | tf_op jit(solution)/shard_map/reduce_scatter | solution.py:217
  217.6 25.4 %reduce-scatter.6.cloned.1.call-done = f32[448,128]{1,0:T(8,128)} async-done(((f32[1792,128]{1,0:T(8,128)}), f32[448,128]{1,0:T(8,128)}) %reduce-scatter.6.cloned.1.call-update) | async-done | bytes 229392 | tf_op jit(solution)/shard_map/reduce_scatter | solution.py:217
  243.1 27.7 %reduce-scatter.8.cloned.1.call-done = f32[224,128]{1,0:T(8,128)} async-done(((f32[448,128]{1,0:T(8,128)}), f32[224,128]{1,0:T(8,128)}) %reduce-scatter.8.cloned.1.call-update) | async-done | bytes 114704 | tf_op jit(solution)/shard_map/reduce_scatter | solution.py:217
  270.8 12.1 %all_gather.12 = f32[448,128]{1,0:T(8,128)S(1)} all-gather(f32[224,128]{1,0:T(8,128)} %reduce-scatter.8.cloned.1.call-done), channel_id=1, replica_groups=mesh['dp_x'=4,'dp_z'=2,'dp_y'=4,'owner_z'=4,'owner_c'=2] {'dp_z'}, dimensions={0}, use_global_device_ids=true | all-gather | bytes 344064 | tf_op jit(solution)/shard_map/all_gather | solution.py:220
  282.9 14.3 %all_gather.13 = f32[1792,128]{1,0:T(8,128)} all-gather(f32[448,128]{1,0:T(8,128)S(1)} %all_gather.12), channel_id=1, replica_groups=mesh['dp_x'=4,'dp_z'=2,'dp_y'=4,'owner_z'=4,'owner_c'=2] {'dp_x'}, dimensions={0}, use_global_device_ids=true | all-gather | bytes 1146880 | tf_op jit(solution)/shard_map/all_gather | solution.py:220
  297.3 43.1 %all-gather.4.cloned.1.call-done = f32[7168,128]{1,0:T(8,128)} async-done(((f32[1792,128]{1,0:T(8,128)}), f32[7168,128]{1,0:T(8,128)}) %all-gather.4.cloned.1.call-update) | async-done | bytes 3670032 | tf_op jit(solution)/shard_map/all_gather | solution.py:220
  344.7 2.5 copy-done
  347.9 15.0 %shard_map.37 = f32[128,128]{1,0:T(8,128)} custom-call(f32[128,128]{1,0:T(8,128)} %select_add_fusion.9.a_ref), custom_call_target="tpu_custom_call" | custom-call | flops 12582912 | bytes 131072 | tf_op jit(solution)/shard_map/pallas_call | solution.py:127
  365.5 7.4 %constant_dynamic-update-slice_fusion.47 = (f32[1280,1152]{1,0:T(8,128)}, f32[1152,1024]{1,0:T(8,128)S(1)}) fusion(f32[1280,1152]{1,0:T(8,128)} %constant_dynamic-update-slice_fusion.35, f32[1152,128]{1,0:T(8,128)S(1)} %fusion.54), kind=kOutput, calls=%fused_computation.218 | convolution fusion | flops 1814298624 | bytes 15269888 | tf_op jit(solution)/shard_map/dot_general | solution.py:85
  372.9 2.2 copy-done.2
  375.7 15.0 %shard_map.38 = f32[128,128]{1,0:T(8,128)} custom-call(f32[128,128]{1,0:T(8,128)} %select_add_fusion.8.a_ref), custom_call_target="tpu_custom_call" | custom-call | flops 12582912 | bytes 131072 | tf_op jit(solution)/shard_map/pallas_call | solution.py:127
  390.7 2.5 constant_dynamic-update-slice_fusion.46
  393.1 6.0 constant_dynamic-update-slice_fusion.45
  401.6 15.0 %shard_map.39 = f32[128,128]{1,0:T(8,128)} custom-call(f32[128,128]{1,0:T(8,128)} %select_add_fusion.7.a_ref), custom_call_target="tpu_custom_call" | custom-call | flops 12582912 | bytes 131072 | tf_op jit(solution)/shard_map/pallas_call | solution.py:127
  416.6 2.4 constant_dynamic-update-slice_fusion.44
  419.0 5.8 constant_dynamic-update-slice_fusion.43
  425.4 15.0 %shard_map.40 = f32[128,128]{1,0:T(8,128)} custom-call(f32[128,128]{1,0:T(8,128)} %select_add_fusion.6.a_ref), custom_call_target="tpu_custom_call" | custom-call | flops 12582912 | bytes 131072 | tf_op jit(solution)/shard_map/pallas_call | solution.py:127
  440.3 2.1 constant_dynamic-update-slice_fusion.42
  442.5 4.7 constant_dynamic-update-slice_fusion.41
  447.8 15.1 %shard_map.41 = f32[128,128]{1,0:T(8,128)} custom-call(f32[128,128]{1,0:T(8,128)} %select_add_fusion.5.a_ref), custom_call_target="tpu_custom_call" | custom-call | flops 12582912 | bytes 131072 | tf_op jit(solution)/shard_map/pallas_call | solution.py:127
  462.9 2.0 constant_dynamic-update-slice_fusion.40
  465.0 2.5 fusion.19
  469.3 15.0 %shard_map.42 = f32[128,128]{1,0:T(8,128)} custom-call(f32[128,128]{1,0:T(8,128)} %select_add_fusion.4.a_ref), custom_call_target="tpu_custom_call" | custom-call | flops 12582912 | bytes 131072 | tf_op jit(solution)/shard_map/pallas_call | solution.py:127
  484.3 2.0 constant_dynamic-update-slice_fusion.38
  491.4 15.0 %shard_map.46 = f32[128,128]{1,0:T(8,128)} custom-call(f32[128,128]{1,0:T(8,128)} %select_add_fusion.a_ref), custom_call_target="tpu_custom_call" | custom-call | flops 12582912 | bytes 131072 | tf_op jit(solution)/shard_map/pallas_call | solution.py:127
  506.4 15.0 %shard_map.43 = f32[128,128]{1,0:T(8,128)} custom-call(f32[128,128]{1,0:T(8,128)} %select_add_fusion.3.a_ref), custom_call_target="tpu_custom_call" | custom-call | flops 12582912 | bytes 131072 | tf_op jit(solution)/shard_map/pallas_call | solution.py:127
  525.4 15.0 %shard_map.44 = f32[128,128]{1,0:T(8,128)} custom-call(f32[128,128]{1,0:T(8,128)} %select_add_fusion.2.a_ref), custom_call_target="tpu_custom_call" | custom-call | flops 12582912 | bytes 131072 | tf_op jit(solution)/shard_map/pallas_call | solution.py:127
  542.4 15.0 %shard_map.45 = f32[128,128]{1,0:T(8,128)} custom-call(f32[128,128]{1,0:T(8,128)} %select_add_fusion.1.a_ref), custom_call_target="tpu_custom_call" | custom-call | flops 12582912 | bytes 131072 | tf_op jit(solution)/shard_map/pallas_call | solution.py:127
  572.8 2.1 convolution_subtract_fusion
  577.5 60.0 %all-gather.6.cloned.1.call-done = f32[9216,128]{1,0:T(8,128)} async-done(((f32[1152,128]{1,0:T(8,128)}), f32[9216,128]{1,0:T(8,128)}) %all-gather.6.cloned.1.call-update) | async-done | bytes 4718608 | tf_op jit(solution)/shard_map/all_gather | solution.py:223
  637.5 4.9 copy.92
  (160 shorter events, 60.8 us)
Async XLA Ops:
  7.8 21.2 %all-to-all-start = ((s32[8,1,4]{2,1,0:T(1,128)}), s32[8,1,4]{2,1,0:T(1,128)S(1)}, u32[]{:S(2)}, u32[]{:S(2)}) async-start(s32[8,1,4]{2,1,0:T(1,128)} %broadcast_in_dim.54), calls=%async_computation | async-start | bytes 8192 | tf_op jit(solution)/shard_map/all_to_all | solution.py:191
  13.7 203.8 %reduce-scatter.4.cloned.1.call-start = ((), (), s32[]{:S(2)}) async-start(), calls=%async_computation.4 | async-start | bytes 4587520 | tf_op jit(solution)/shard_map/reduce_scatter | solution.py:217
  23.5 93.8 %collective-permute-start.6 = (bf16[512,512]{1,0:T(8,128)(2,1)S(1)}, bf16[512,512]{1,0:T(8,128)(2,1)S(1)}, u32[]{:S(2)}, u32[]{:S(2)}) collective-permute-start(bf16[512,512]{1,0:T(8,128)(2,1)S(1)} %get-tuple-element.211), channel_id=1, source_target_pairs={{0,7},{1,0},{2,1},{3,2},{4,3},{5,4},{6,5},{7,6},{8,15},{9,8},{10,9... | collective-permute-start | bytes 1572872 | tf_op jit(solution)/shard_map/ppermute | solution.py:199
  26.9 89.5 %collective-permute-start.5 = (bf16[512,512]{1,0:T(8,128)(2,1)}, bf16[512,512]{1,0:T(8,128)(2,1)S(1)}, u32[]{:S(2)}, u32[]{:S(2)}) collective-permute-start(bf16[512,512]{1,0:T(8,128)(2,1)} %get-tuple-element.212), channel_id=1, source_target_pairs={{0,6},{1,7},{2,0},{3,1},{4,2},{5,3},{6,4},{7,5},{8,14},{9,15},{10,... | collective-permute-start | bytes 1572872 | tf_op jit(solution)/shard_map/ppermute | solution.py:199
  27.5 70.7 %collective-permute-start.2 = (bf16[512,512]{1,0:T(8,128)(2,1)}, bf16[512,512]{1,0:T(8,128)(2,1)S(1)}, u32[]{:S(2)}, u32[]{:S(2)}) collective-permute-start(bf16[512,512]{1,0:T(8,128)(2,1)} %get-tuple-element.215), channel_id=1, source_target_pairs={{0,3},{1,4},{2,5},{3,6},{4,7},{5,0},{6,1},{7,2},{8,11},{9,12},{10,... | collective-permute-start | bytes 1572872 | tf_op jit(solution)/shard_map/ppermute | solution.py:199
  27.5 69.8 %collective-permute-start.1 = (bf16[512,512]{1,0:T(8,128)(2,1)}, bf16[512,512]{1,0:T(8,128)(2,1)S(1)}, u32[]{:S(2)}, u32[]{:S(2)}) collective-permute-start(bf16[512,512]{1,0:T(8,128)(2,1)} %get-tuple-element.216), channel_id=1, source_target_pairs={{0,2},{1,3},{2,4},{3,5},{4,6},{5,7},{6,0},{7,1},{8,10},{9,11},{10,... | collective-permute-start | bytes 1572872 | tf_op jit(solution)/shard_map/ppermute | solution.py:199
  29.0 45.1 %collective-permute-start = (bf16[512,512]{1,0:T(8,128)(2,1)}, bf16[512,512]{1,0:T(8,128)(2,1)S(1)}, u32[]{:S(2)}, u32[]{:S(2)}) collective-permute-start(bf16[512,512]{1,0:T(8,128)(2,1)} %get-tuple-element.217), channel_id=1, source_target_pairs={{0,1},{1,2},{2,3},{3,4},{4,5},{5,6},{6,7},{7,0},{8,9},{9,10},{10,1... | collective-permute-start | bytes 1572872 | tf_op jit(solution)/shard_map/ppermute | solution.py:199
  74.1 40.7 %collective-permute-start.3 = (bf16[512,512]{1,0:T(8,128)(2,1)}, bf16[512,512]{1,0:T(8,128)(2,1)S(1)}, u32[]{:S(2)}, u32[]{:S(2)}) collective-permute-start(bf16[512,512]{1,0:T(8,128)(2,1)} %get-tuple-element.214), channel_id=1, source_target_pairs={{0,4},{1,5},{2,6},{3,7},{4,0},{5,1},{6,2},{7,3},{8,12},{9,13},{10,... | collective-permute-start | bytes 1572872 | tf_op jit(solution)/shard_map/ppermute | solution.py:199
  97.3 18.3 %collective-permute-start.4 = (bf16[512,512]{1,0:T(8,128)(2,1)}, bf16[512,512]{1,0:T(8,128)(2,1)S(1)}, u32[]{:S(2)}, u32[]{:S(2)}) collective-permute-start(bf16[512,512]{1,0:T(8,128)(2,1)} %get-tuple-element.213), channel_id=1, source_target_pairs={{0,5},{1,6},{2,7},{3,0},{4,1},{5,2},{6,3},{7,4},{8,13},{9,14},{10,... | collective-permute-start | bytes 1572872 | tf_op jit(solution)/shard_map/ppermute | solution.py:199
  118.1 3.9 copy-start.1
  167.7 75.3 %reduce-scatter.6.cloned.1.call-start = ((), (), s32[]{:S(2)}) async-start(), calls=%async_computation.5 | async-start | bytes 1146880 | tf_op jit(solution)/shard_map/reduce_scatter | solution.py:217
  217.6 53.2 %reduce-scatter.8.cloned.1.call-start = ((), (), s32[]{:S(2)}) async-start(), calls=%async_computation.6 | async-start | bytes 344064 | tf_op jit(solution)/shard_map/reduce_scatter | solution.py:217
  243.0 97.3 %all-gather.4.cloned.1.call-start = ((), (), s32[]{:S(2)}) async-start(), calls=%async_computation.7 | async-start | bytes 4587520 | tf_op jit(solution)/shard_map/all_gather | solution.py:220
  297.3 340.2 %all-gather.6.cloned.1.call-start = ((), (), s32[]{:S(2)}) async-start(), calls=%async_computation.8 | async-start | bytes 5308416 | tf_op jit(solution)/shard_map/all_gather | solution.py:223
  340.4 3.6 slice-start
  340.4 3.7 slice-start.1
  340.4 3.7 slice-start.2
  340.4 3.8 slice-start.3
  341.6 2.6 slice-start.4
  342.8 1.5 slice-start.5
  344.7 2.5 copy-start
  372.9 2.2 copy-start.2
  399.2 1.8 copy-start.3
  468.7 97.2 %copy-start.9 = (f32[128,128]{1,0:T(8,128)S(1)}, f32[128,128]{1,0:T(8,128)}, u32[]{:S(2)}) copy-start(f32[128,128]{1,0:T(8,128)} %shard_map.41) | copy-start | bytes 196612
  484.3 79.7 %copy-start.10 = (f32[128,128]{1,0:T(8,128)S(1)}, f32[128,128]{1,0:T(8,128)}, u32[]{:S(2)}) copy-start(f32[128,128]{1,0:T(8,128)} %shard_map.42) | copy-start | bytes 196612
  484.3 83.6 %copy-start.8 = (f32[128,128]{1,0:T(8,128)S(1)}, f32[128,128]{1,0:T(8,128)}, u32[]{:S(2)}) copy-start(f32[128,128]{1,0:T(8,128)} %shard_map.40) | copy-start | bytes 196612
  488.2 81.9 %copy-start.7 = (f32[128,128]{1,0:T(8,128)S(1)}, f32[128,128]{1,0:T(8,128)}, u32[]{:S(2)}) copy-start(f32[128,128]{1,0:T(8,128)} %shard_map.39) | copy-start | bytes 196612
  489.3 83.1 %copy-start.6 = (f32[128,128]{1,0:T(8,128)S(1)}, f32[128,128]{1,0:T(8,128)}, u32[]{:S(2)}) copy-start(f32[128,128]{1,0:T(8,128)} %shard_map.38) | copy-start | bytes 196612
  524.7 50.2 %copy-start.4 = (f32[128,128]{1,0:T(8,128)S(1)}, f32[128,128]{1,0:T(8,128)}, u32[]{:S(2)}) copy-start(f32[128,128]{1,0:T(8,128)} %shard_map.37) | copy-start | bytes 196612
  541.8 33.6 %copy-start.5 = (f32[128,128]{1,0:T(8,128)S(1)}, f32[128,128]{1,0:T(8,128)}, u32[]{:S(2)}) copy-start(f32[128,128]{1,0:T(8,128)} %shard_map.46) | copy-start | bytes 196612
Sparse Core Ops, SparseCore 0:
  167.9 49.6 reduce-scatter.3
  220.1 22.8 reduce-scatter.5
  245.5 25.1 reduce-scatter.7
  297.4 42.9 all-gather.3
  577.6 59.8 all-gather.5

commit v11 on v9

--- a/solution.py
+++ b/solution.py
@@ -94,11 +94,13 @@
 
 
 def _leaf_kernel(a_ref, w_ref, s_ref):
-    n = a_ref.shape[0]
+    count, n, _ = a_ref.shape
     s_ref[...] = a_ref[...]
     sub = lax.broadcasted_iota(jnp.int32, (n, n), 0)
     lane = lax.broadcasted_iota(jnp.int32, (n, n), 1)
-    w_ref[...] = jnp.where(sub == lane, 1.0, 0.0).astype(jnp.float32)
+    eye = jnp.where(sub == lane, 1.0, 0.0).astype(jnp.float32)
+    for m in range(count):
+        w_ref[m] = eye
     lane_row = lax.broadcasted_iota(jnp.int32, (1, n), 1)
     seg = 16
     for start in range(0, n, seg):
@@ -107,33 +109,36 @@
         sub_col = lax.broadcasted_iota(jnp.int32, (rows, 1), 0) + start
 
         def step(j, carry, start=start, lane_t=lane_t, sub_col=sub_col):
-            a = s_ref[start:, :]
-            row = s_ref[pl.ds(j, 1), :]
-            pivot = jnp.sum(jnp.where(lane_row == j, row, 0.0), axis=1, keepdims=True)
-            inv_root = 1.0 / jnp.sqrt(pivot)
-            col = jnp.sum(jnp.where(lane_t == j, a, 0.0), axis=1, keepdims=True)
-            lcol = jnp.where(sub_col > j, col * inv_root, 0.0)
-            lrow = jnp.where(lane_row >= j, row * inv_root, 0.0)
-            s_ref[start:, :] = a - lcol * lrow
-            wrow = w_ref[pl.ds(j, 1), :] * inv_root
-            w_ref[start:, :] = w_ref[start:, :] - lcol * wrow
-            w_ref[pl.ds(j, 1), :] = wrow
+            for m in range(count):
+                a = s_ref[m, start:, :]
+                row = s_ref[m, pl.ds(j, 1), :]
+                pivot = jnp.sum(jnp.where(lane_row == j, row, 0.0), axis=1, keepdims=True)
+                inv_root = 1.0 / jnp.sqrt(pivot)
+                col = jnp.sum(jnp.where(lane_t == j, a, 0.0), axis=1, keepdims=True)
+                lcol = jnp.where(sub_col > j, col * inv_root, 0.0)
+                lrow = jnp.where(lane_row >= j, row * inv_root, 0.0)
+                s_ref[m, start:, :] = a - lcol * lrow
+                wrow = w_ref[m, pl.ds(j, 1), :] * inv_root
+                w_ref[m, start:, :] = w_ref[m, start:, :] - lcol * wrow
+                w_ref[m, pl.ds(j, 1), :] = wrow
             return carry
 
         lax.fori_loop(start, start + seg, step, 0)
 
-def _chol_inverse(block):
-    n = block.shape[0]
-    return pl.pallas_call(
+
+def _chol_inverse(*blocks):
+    stacked = jnp.stack(blocks)
+    count, n, _ = stacked.shape
+    out = pl.pallas_call(
         _leaf_kernel,
-        out_shape=jax.ShapeDtypeStruct((n, n), jnp.float32),
+        out_shape=jax.ShapeDtypeStruct((count, n, n), jnp.float32),
         in_specs=[pl.BlockSpec(memory_space=pltpu.VMEM)],
         out_specs=pl.BlockSpec(memory_space=pltpu.VMEM),
-        scratch_shapes=[pltpu.VMEM((n, n), jnp.float32)],
-        cost_estimate=pl.CostEstimate(flops=6 * n * n * n, bytes_accessed=8 * n * n,
-                                      transcendentals=n),
-    )(block)
-
+        scratch_shapes=[pltpu.VMEM((count, n, n), jnp.float32)],
+        cost_estimate=pl.CostEstimate(flops=6 * count * n * n * n, bytes_accessed=8 * count * n * n,
+                                      transcendentals=count * n),
+    )(stacked)
+    return [out[m] for m in range(count)]
 
 def precondition_blocks(blocks, nb, total_rows):
     block = blocks.shape[-1]
@@ -154,7 +159,10 @@
         lo = k * block
         hi = lo + block
         diag = work[lo:hi, lo:hi] + damping * eye
-        inverse = _chol_inverse(diag)
+        if k == 0:
+            inverse, grad_inverse = _chol_inverse(diag, grad_factor)
+        else:
+            (inverse,) = _chol_inverse(diag)
         inverses.append(inverse)
         panel = _mm_nt(work[hi:, lo:hi], inverse)
         work = work.at[hi:, lo:hi].set(panel)
@@ -172,7 +180,6 @@
             rhs = rhs - _mm_t(work[hi:na * block, lo:hi], below)
         pieces[k] = _mm_t(inverses[k], rhs)
     left_solved = jnp.concatenate(pieces, axis=0)
-    grad_inverse = _chol_inverse(grad_factor)
     return _mm(_mm_nt(left_solved, grad_inverse), grad_inverse)
 
 

time: 640 us -> 644 us (level)
    pallas_call x10 -> x9, Pallas kernels: 150 us -> 148 us  [_chol_inverse(): pl.pallas_call(_leaf_kernel, out_shape=jax.ShapeDtypeStruct((count, n, n)...]
where the time goes in v11:
time: 644 us; the launch traced here: 633 us
  waiting for transfers between devices  295 us (46%)
  Pallas kernels  148 us (23%)
  matrix products  89.9 us (14%)
  local copies, waits for them, and re-layouts  33.8 us (5%)
  blocking collectives  26.5 us (4%)
  other arithmetic  14.1 us (2%)
  between operations  14.1 us (2%)
  starting transfers between devices  11.2 us (2%)
    pallas_call x9, Pallas kernels, _chol_inverse(): pl.pallas_call(_leaf_kernel, out_shape=jax.ShapeDtypeStruct((count, n, n)...  148 us
    reduce_scatter x3, waiting for transfers between devices, body(): mine = lax.psum_scatter(mine, axis, scatter_dimension=0, tiled=True)  98.6 us
    all_to_all x1, waiting for transfers between devices, body(): lax.all_to_all(ordered, OWNER_AXES, split_axis=0, concat_axis=1, tiled=True)  93.7 us
    all_gather x1, waiting for transfers between devices, body(): return lax.all_gather(results, OWNER_AXES, axis=0, tiled=True)  60 us
    dot_general x18, matrix products, _mm_nt(): lax.dot_general(a, b, (((1,), (1,)), ((), ())), precision=HIGH, preferred...  47.6 us
    all_gather x1, waiting for transfers between devices, body(): gathered = lax.all_gather(gathered, axis, axis=0, tiled=True)  43 us
    all_gather x2, blocking collectives, body(): gathered = lax.all_gather(gathered, axis, axis=0, tiled=True)  26.5 us
    dot_general x10, matrix products, body(): lax.dot_general(columns[:, j * block:], columns[:, j * block:(j + 1) * bl...  24.7 us
  transfers between devices with their start and end apart: 7, of which 6 were waited for; matrix products, arithmetic and copies ran while one was open for 1% of the time, Pallas kernels for 0%

profile of v11, /device:TPU:2, one launch (start us, length us, event | category | flops | bytes accessed | tf_op | source)
XLA Modules:
  0.0 633.0 jit_solution(11435108045317809664)
XLA Ops:
  7.8 5.9 all-to-all-start
  14.3 5.0 gather_fusion
  19.3 5.1 all-to-all-start.1
  24.9 93.7 %all-to-all-done.1 = bf16[8,512,512]{2,1,0:T(8,128)(2,1)} async-done(((bf16[8,512,512]{2,1,0:T(8,128)(2,1)}), bf16[8,512,512]{2,1,0:T(8,128)(2,1)}, u32[]{:S(2)}, u32[]{:S(2)}) %all-to-all-start.1) | async-done | bytes 4194336 | tf_op jit(solution)/shard_map/all_to_all | solution.py:199
  119.9 2.3 slice.740
  122.1 3.9 fusion.145
  126.0 2.2 pad_select_fusion
  128.2 4.7 maximum_select_fusion
  132.9 3.8 convolution_dynamic-update-slice_fusion
  136.7 3.5 fusion.14
  140.2 3.2 fusion.21
  143.3 2.9 fusion.24
  146.2 2.6 fusion.27
  148.8 2.7 fusion.30
  151.5 2.0 fusion.34
  158.4 45.5 %reduce-scatter.4.cloned.1.call-done = f32[1792,128]{1,0:T(8,128)} async-done(((f32[7168,128]{1,0:T(8,128)}), f32[1792,128]{1,0:T(8,128)}) %reduce-scatter.4.cloned.1.call-update) | async-done | bytes 917520 | tf_op jit(solution)/shard_map/reduce_scatter | solution.py:217
  203.9 25.5 %reduce-scatter.6.cloned.1.call-done = f32[448,128]{1,0:T(8,128)} async-done(((f32[1792,128]{1,0:T(8,128)}), f32[448,128]{1,0:T(8,128)}) %reduce-scatter.6.cloned.1.call-update) | async-done | bytes 229392 | tf_op jit(solution)/shard_map/reduce_scatter | solution.py:217
  229.4 27.7 %reduce-scatter.8.cloned.1.call-done = f32[224,128]{1,0:T(8,128)} async-done(((f32[448,128]{1,0:T(8,128)}), f32[224,128]{1,0:T(8,128)}) %reduce-scatter.8.cloned.1.call-update) | async-done | bytes 114704 | tf_op jit(solution)/shard_map/reduce_scatter | solution.py:217
  257.1 12.1 %all_gather.12 = f32[448,128]{1,0:T(8,128)S(1)} all-gather(f32[224,128]{1,0:T(8,128)} %reduce-scatter.8.cloned.1.call-done), channel_id=1, replica_groups=mesh['dp_x'=4,'dp_z'=2,'dp_y'=4,'owner_z'=4,'owner_c'=2] {'dp_z'}, dimensions={0}, use_global_device_ids=true | all-gather | bytes 344064 | tf_op jit(solution)/shard_map/all_gather | solution.py:220
  269.2 14.3 %all_gather.13 = f32[1792,128]{1,0:T(8,128)} all-gather(f32[448,128]{1,0:T(8,128)S(1)} %all_gather.12), channel_id=1, replica_groups=mesh['dp_x'=4,'dp_z'=2,'dp_y'=4,'owner_z'=4,'owner_c'=2] {'dp_x'}, dimensions={0}, use_global_device_ids=true | all-gather | bytes 1146880 | tf_op jit(solution)/shard_map/all_gather | solution.py:220
  283.6 43.0 %all-gather.4.cloned.1.call-done = f32[7168,128]{1,0:T(8,128)} async-done(((f32[1792,128]{1,0:T(8,128)}), f32[7168,128]{1,0:T(8,128)}) %all-gather.4.cloned.1.call-update) | async-done | bytes 3670032 | tf_op jit(solution)/shard_map/all_gather | solution.py:220
  331.1 2.8 copy-done
  335.1 28.2 %shard_map.37 = f32[2,128,128]{2,1,0:T(8,128)} custom-call(f32[2,128,128]{2,1,0:T(8,128)} %pad_maximum_fusion.a_ref), custom_call_target="tpu_custom_call" | custom-call | flops 25165824 | bytes 262144 | tf_op jit(solution)/shard_map/pallas_call | solution.py:132
  365.9 7.3 %constant_dynamic-update-slice_fusion.46 = (f32[1280,1152]{1,0:T(8,128)}, f32[1152,1024]{1,0:T(8,128)S(1)}) fusion(f32[1280,1152]{1,0:T(8,128)} %constant_dynamic-update-slice_fusion.47, f32[1152,128]{1,0:T(8,128)S(1)} %fusion.54), kind=kOutput, calls=%fused_computation.234 | convolution fusion | flops 1814298624 | bytes 15269888 | tf_op jit(solution)/shard_map/dot_general | solution.py:85
  373.2 2.2 copy-done.1
  376.1 15.0 %shard_map.38 = f32[1,128,128]{2,1,0:T(8,128)} custom-call(f32[1,128,128]{2,1,0:T(8,128)} %fusion.101.a_ref), custom_call_target="tpu_custom_call" | custom-call | flops 12582912 | bytes 131072 | tf_op jit(solution)/shard_map/pallas_call | solution.py:132
  391.0 2.5 constant_dynamic-update-slice_fusion.45
  393.6 6.0 constant_dynamic-update-slice_fusion.44
  402.0 15.0 %shard_map.39 = f32[1,128,128]{2,1,0:T(8,128)} custom-call(f32[1,128,128]{2,1,0:T(8,128)} %fusion.102.a_ref), custom_call_target="tpu_custom_call" | custom-call | flops 12582912 | bytes 131072 | tf_op jit(solution)/shard_map/pallas_call | solution.py:132
  417.0 2.4 constant_dynamic-update-slice_fusion.43
  419.4 5.8 constant_dynamic-update-slice_fusion.42
  425.8 15.0 %shard_map.40 = f32[1,128,128]{2,1,0:T(8,128)} custom-call(f32[1,128,128]{2,1,0:T(8,128)} %fusion.103.a_ref), custom_call_target="tpu_custom_call" | custom-call | flops 12582912 | bytes 131072 | tf_op jit(solution)/shard_map/pallas_call | solution.py:132
  440.7 2.2 constant_dynamic-update-slice_fusion.41
  442.9 4.7 constant_dynamic-update-slice_fusion.40
  448.2 15.1 %shard_map.41 = f32[1,128,128]{2,1,0:T(8,128)} custom-call(f32[1,128,128]{2,1,0:T(8,128)} %fusion.104.a_ref), custom_call_target="tpu_custom_call" | custom-call | flops 12582912 | bytes 131072 | tf_op jit(solution)/shard_map/pallas_call | solution.py:132
  463.3 2.0 constant_dynamic-update-slice_fusion.39
  465.4 2.5 fusion.19
  469.7 15.0 %shard_map.42 = f32[1,128,128]{2,1,0:T(8,128)} custom-call(f32[1,128,128]{2,1,0:T(8,128)} %fusion.105.a_ref), custom_call_target="tpu_custom_call" | custom-call | flops 12582912 | bytes 131072 | tf_op jit(solution)/shard_map/pallas_call | solution.py:132
  484.7 2.0 constant_dynamic-update-slice_fusion.37
  486.8 2.0 fusion.20
  490.4 15.0 %shard_map.43 = f32[1,128,128]{2,1,0:T(8,128)} custom-call(f32[1,128,128]{2,1,0:T(8,128)} %fusion.106.a_ref), custom_call_target="tpu_custom_call" | custom-call | flops 12582912 | bytes 131072 | tf_op jit(solution)/shard_map/pallas_call | solution.py:132
  505.3 1.9 constant_dynamic-update-slice_fusion.35
  509.3 15.0 %shard_map.44 = f32[1,128,128]{2,1,0:T(8,128)} custom-call(f32[1,128,128]{2,1,0:T(8,128)} %fusion.107.a_ref), custom_call_target="tpu_custom_call" | custom-call | flops 12582912 | bytes 131072 | tf_op jit(solution)/shard_map/pallas_call | solution.py:132
  526.3 15.0 %shard_map.45 = f32[1,128,128]{2,1,0:T(8,128)} custom-call(f32[1,128,128]{2,1,0:T(8,128)} %fusion.108.a_ref), custom_call_target="tpu_custom_call" | custom-call | flops 12582912 | bytes 131072 | tf_op jit(solution)/shard_map/pallas_call | solution.py:132
  554.4 1.9 convolution_subtract_fusion.1
  556.8 2.1 convolution_subtract_fusion
  561.4 60.0 %all-gather.6.cloned.1.call-done = f32[9216,128]{1,0:T(8,128)} async-done(((f32[1152,128]{1,0:T(8,128)}), f32[9216,128]{1,0:T(8,128)}) %all-gather.6.cloned.1.call-update) | async-done | bytes 4718608 | tf_op jit(solution)/shard_map/all_gather | solution.py:223
  621.4 4.9 copy.91
  (135 shorter events, 44.4 us)
Async XLA Ops:
  7.8 11.6 %all-to-all-start = ((s32[8,1,4]{2,1,0:T(1,128)}), s32[8,1,4]{2,1,0:T(1,128)S(1)}, u32[]{:S(2)}, u32[]{:S(2)}) async-start(s32[8,1,4]{2,1,0:T(1,128)} %broadcast_in_dim.51), calls=%async_computation | async-start | bytes 8192 | tf_op jit(solution)/shard_map/all_to_all | solution.py:200
  19.3 99.2 %all-to-all-start.1 = ((bf16[8,512,512]{2,1,0:T(8,128)(2,1)}), bf16[8,512,512]{2,1,0:T(8,128)(2,1)}, u32[]{:S(2)}, u32[]{:S(2)}) async-start(bf16[8,512,512]{2,1,0:T(8,128)(2,1)} %gather_fusion), calls=%async_computation.1 | async-start | bytes 8388608 | tf_op jit(solution)/shard_map/all_to_all | solution.py:199
  24.4 179.4 %reduce-scatter.4.cloned.1.call-start = ((), (), s32[]{:S(2)}) async-start(), calls=%async_computation.5 | async-start | bytes 4587520 | tf_op jit(solution)/shard_map/reduce_scatter | solution.py:217
  158.3 71.0 %reduce-scatter.6.cloned.1.call-start = ((), (), s32[]{:S(2)}) async-start(), calls=%async_computation.6 | async-start | bytes 1146880 | tf_op jit(solution)/shard_map/reduce_scatter | solution.py:217
  203.8 53.2 %reduce-scatter.8.cloned.1.call-start = ((), (), s32[]{:S(2)}) async-start(), calls=%async_computation.7 | async-start | bytes 344064 | tf_op jit(solution)/shard_map/reduce_scatter | solution.py:217
  229.4 97.3 %all-gather.4.cloned.1.call-start = ((), (), s32[]{:S(2)}) async-start(), calls=%async_computation.8 | async-start | bytes 4587520 | tf_op jit(solution)/shard_map/all_gather | solution.py:220
  283.6 337.8 %all-gather.6.cloned.1.call-start = ((), (), s32[]{:S(2)}) async-start(), calls=%async_computation.9 | async-start | bytes 5308416 | tf_op jit(solution)/shard_map/all_gather | solution.py:223
  326.7 3.6 slice-start
  326.7 3.7 slice-start.1
  326.7 3.7 slice-start.2
  326.7 3.8 slice-start.3
  327.9 2.6 slice-start.4
  329.1 1.5 slice-start.5
  330.7 3.7 copy-start.3
  331.1 2.8 copy-start
  373.2 2.2 copy-start.1
  399.6 1.8 copy-start.2
  469.1 80.7 %copy-start.8 = (f32[1,128,128]{2,1,0:T(8,128)S(1)}, f32[1,128,128]{2,1,0:T(8,128)}, u32[]{:S(2)}) copy-start(f32[1,128,128]{2,1,0:T(8,128)} %shard_map.41) | copy-start | bytes 196612
  484.7 63.2 %copy-start.9 = (f32[1,128,128]{2,1,0:T(8,128)S(1)}, f32[1,128,128]{2,1,0:T(8,128)}, u32[]{:S(2)}) copy-start(f32[1,128,128]{2,1,0:T(8,128)} %shard_map.42) | copy-start | bytes 196612
  484.7 67.1 %copy-start.7 = (f32[1,128,128]{2,1,0:T(8,128)S(1)}, f32[1,128,128]{2,1,0:T(8,128)}, u32[]{:S(2)}) copy-start(f32[1,128,128]{2,1,0:T(8,128)} %shard_map.40) | copy-start | bytes 196612
  486.8 67.3 %copy-start.6 = (f32[1,128,128]{2,1,0:T(8,128)S(1)}, f32[1,128,128]{2,1,0:T(8,128)}, u32[]{:S(2)}) copy-start(f32[1,128,128]{2,1,0:T(8,128)} %shard_map.39) | copy-start | bytes 196612
  489.7 66.6 %copy-start.5 = (f32[1,128,128]{2,1,0:T(8,128)S(1)}, f32[1,128,128]{2,1,0:T(8,128)}, u32[]{:S(2)}) copy-start(f32[1,128,128]{2,1,0:T(8,128)} %shard_map.38) | copy-start | bytes 196612
  508.7 50.1 %copy-start.4 = (f32[2,128,128]{2,1,0:T(8,128)S(1)}, f32[2,128,128]{2,1,0:T(8,128)}, u32[]{:S(2)}) copy-start(f32[2,128,128]{2,1,0:T(8,128)} %shard_map.37) | copy-start | bytes 393220
Sparse Core Ops, SparseCore 0:
  158.4 45.3 reduce-scatter.3
  206.4 22.9 reduce-scatter.5
  231.8 25.1 reduce-scatter.7
  283.7 42.9 all-gather.3
  561.5 59.8 all-gather.5

commit v12 on v9

--- a/solution.py
+++ b/solution.py
@@ -162,16 +162,14 @@
             update = _mm_nt(panel, panel[: (na - k - 1) * block])
             work = work.at[hi:, hi:].add(-update)
     solved_t = work[na * block:, :]
-    pieces = [None] * na
+    left_solved = jnp.zeros((na * block, block), jnp.float32)
     for k in reversed(range(na)):
         lo = k * block
         hi = lo + block
         rhs = solved_t[:, lo:hi].T
         if k + 1 < na:
-            below = jnp.concatenate(pieces[k + 1:], axis=0)
-            rhs = rhs - _mm_t(work[hi:na * block, lo:hi], below)
-        pieces[k] = _mm_t(inverses[k], rhs)
-    left_solved = jnp.concatenate(pieces, axis=0)
+            rhs = rhs - _mm_t(work[hi:na * block, lo:hi], left_solved[hi:])
+        left_solved = left_solved.at[lo:hi].set(_mm_t(inverses[k], rhs))
     grad_inverse = _chol_inverse(grad_factor)
     return _mm(_mm_nt(left_solved, grad_inverse), grad_inverse)
 

time: 640 us -> 646 us (level)
    unnamed x55 -> x30, local copies, waits for them, and re-layouts: 13.1 us -> 12.9 us
where the time goes in v12:
time: 646 us; the launch traced here: 635 us
  waiting for transfers between devices  295 us (46%)
  Pallas kernels  150 us (23%)
  matrix products  89.8 us (14%)
  local copies, waits for them, and re-layouts  33 us (5%)
  blocking collectives  26.5 us (4%)
  other arithmetic  15.5 us (2%)
  between operations  13.8 us (2%)
  starting transfers between devices  11.2 us (2%)
    pallas_call x10, Pallas kernels, _chol_inverse(): pl.pallas_call(_leaf_kernel, out_shape=jax.ShapeDtypeStruct((n, n), jnp.f...  150 us
    reduce_scatter x3, waiting for transfers between devices, body(): mine = lax.psum_scatter(mine, axis, scatter_dimension=0, tiled=True)  98.6 us
    all_to_all x1, waiting for transfers between devices, body(): lax.all_to_all(ordered, OWNER_AXES, split_axis=0, concat_axis=1, tiled=True)  93.7 us
    all_gather x1, waiting for transfers between devices, body(): return lax.all_gather(results, OWNER_AXES, axis=0, tiled=True)  60 us
    dot_general x18, matrix products, _mm_nt(): lax.dot_general(a, b, (((1,), (1,)), ((), ())), precision=HIGH, preferred...  47.4 us
    all_gather x1, waiting for transfers between devices, body(): gathered = lax.all_gather(gathered, axis, axis=0, tiled=True)  43 us
    all_gather x2, blocking collectives, body(): gathered = lax.all_gather(gathered, axis, axis=0, tiled=True)  26.5 us
    dot_general x10, matrix products, body(): lax.dot_general(columns[:, j * block:], columns[:, j * block:(j + 1) * bl...  24.7 us
  transfers between devices with their start and end apart: 7, of which 6 were waited for; matrix products, arithmetic and copies ran while one was open for 1% of the time, Pallas kernels for 0%

profile of v12, /device:TPU:2, one launch (start us, length us, event | category | flops | bytes accessed | tf_op | source)
XLA Modules:
  0.0 635.0 jit_solution(11890193875451314579)
XLA Ops:
  7.8 5.9 all-to-all-start
  14.3 5.0 gather_fusion
  19.4 5.1 all-to-all-start.1
  24.9 93.7 %all-to-all-done.1 = bf16[8,512,512]{2,1,0:T(8,128)(2,1)} async-done(((bf16[8,512,512]{2,1,0:T(8,128)(2,1)}), bf16[8,512,512]{2,1,0:T(8,128)(2,1)}, u32[]{:S(2)}, u32[]{:S(2)}) %all-to-all-start.1) | async-done | bytes 4194336 | tf_op jit(solution)/shard_map/all_to_all | solution.py:190
  119.9 2.3 slice.913
  122.1 3.9 fusion.98
  126.0 2.2 pad_select_fusion
  128.2 4.7 maximum_select_fusion
  133.0 3.8 convolution_dynamic-update-slice_fusion
  136.7 3.5 fusion.14
  140.2 3.2 fusion.21
  143.3 2.9 fusion.24
  146.2 2.6 fusion.27
  148.8 2.7 fusion.30
  151.5 2.0 fusion.34
  158.4 45.5 %reduce-scatter.4.cloned.1.call-done = f32[1792,128]{1,0:T(8,128)} async-done(((f32[7168,128]{1,0:T(8,128)}), f32[1792,128]{1,0:T(8,128)}) %reduce-scatter.4.cloned.1.call-update) | async-done | bytes 917520 | tf_op jit(solution)/shard_map/reduce_scatter | solution.py:208
  203.9 25.5 %reduce-scatter.6.cloned.1.call-done = f32[448,128]{1,0:T(8,128)} async-done(((f32[1792,128]{1,0:T(8,128)}), f32[448,128]{1,0:T(8,128)}) %reduce-scatter.6.cloned.1.call-update) | async-done | bytes 229392 | tf_op jit(solution)/shard_map/reduce_scatter | solution.py:208
  229.4 27.7 %reduce-scatter.8.cloned.1.call-done = f32[224,128]{1,0:T(8,128)} async-done(((f32[448,128]{1,0:T(8,128)}), f32[224,128]{1,0:T(8,128)}) %reduce-scatter.8.cloned.1.call-update) | async-done | bytes 114704 | tf_op jit(solution)/shard_map/reduce_scatter | solution.py:208
  257.1 12.1 %all_gather.12 = f32[448,128]{1,0:T(8,128)S(1)} all-gather(f32[224,128]{1,0:T(8,128)} %reduce-scatter.8.cloned.1.call-done), channel_id=1, replica_groups=mesh['dp_x'=4,'dp_z'=2,'dp_y'=4,'owner_z'=4,'owner_c'=2] {'dp_z'}, dimensions={0}, use_global_device_ids=true | all-gather | bytes 344064 | tf_op jit(solution)/shard_map/all_gather | solution.py:211
  269.3 14.3 %all_gather.13 = f32[1792,128]{1,0:T(8,128)} all-gather(f32[448,128]{1,0:T(8,128)S(1)} %all_gather.12), channel_id=1, replica_groups=mesh['dp_x'=4,'dp_z'=2,'dp_y'=4,'owner_z'=4,'owner_c'=2] {'dp_x'}, dimensions={0}, use_global_device_ids=true | all-gather | bytes 1146880 | tf_op jit(solution)/shard_map/all_gather | solution.py:211
  283.7 43.0 %all-gather.4.cloned.1.call-done = f32[7168,128]{1,0:T(8,128)} async-done(((f32[1792,128]{1,0:T(8,128)}), f32[7168,128]{1,0:T(8,128)}) %all-gather.4.cloned.1.call-update) | async-done | bytes 3670032 | tf_op jit(solution)/shard_map/all_gather | solution.py:211
  331.1 2.5 copy-done
  334.3 15.0 %shard_map.37 = f32[128,128]{1,0:T(8,128)} custom-call(f32[128,128]{1,0:T(8,128)} %select_add_fusion.9.a_ref), custom_call_target="tpu_custom_call" | custom-call | flops 12582912 | bytes 131072 | tf_op jit(solution)/shard_map/pallas_call | solution.py:127
  351.8 7.3 %constant_dynamic-update-slice_fusion.13 = (f32[1280,1152]{1,0:T(8,128)}, f32[1152,1024]{1,0:T(8,128)S(1)}) fusion(f32[1280,1152]{1,0:T(8,128)} %constant_dynamic-update-slice_fusion.1, f32[1152,128]{1,0:T(8,128)S(1)} %fusion.54), kind=kOutput, calls=%fused_computation.161 | convolution fusion | flops 1814298624 | bytes 15269888 | tf_op jit(solution)/shard_map/dot_general | solution.py:85
  359.2 2.2 copy-done.1
  362.0 15.0 %shard_map.38 = f32[128,128]{1,0:T(8,128)} custom-call(f32[128,128]{1,0:T(8,128)} %select_add_fusion.8.a_ref), custom_call_target="tpu_custom_call" | custom-call | flops 12582912 | bytes 131072 | tf_op jit(solution)/shard_map/pallas_call | solution.py:127
  377.0 2.5 constant_dynamic-update-slice_fusion.12
  379.4 6.0 constant_dynamic-update-slice_fusion.11
  387.9 15.0 %shard_map.39 = f32[128,128]{1,0:T(8,128)} custom-call(f32[128,128]{1,0:T(8,128)} %select_add_fusion.7.a_ref), custom_call_target="tpu_custom_call" | custom-call | flops 12582912 | bytes 131072 | tf_op jit(solution)/shard_map/pallas_call | solution.py:127
  402.9 2.4 constant_dynamic-update-slice_fusion.10
  405.3 5.8 constant_dynamic-update-slice_fusion.9
  411.7 15.0 %shard_map.40 = f32[128,128]{1,0:T(8,128)} custom-call(f32[128,128]{1,0:T(8,128)} %select_add_fusion.6.a_ref), custom_call_target="tpu_custom_call" | custom-call | flops 12582912 | bytes 131072 | tf_op jit(solution)/shard_map/pallas_call | solution.py:127
  426.6 2.1 constant_dynamic-update-slice_fusion.8
  428.7 4.7 constant_dynamic-update-slice_fusion.7
  434.1 15.1 %shard_map.41 = f32[128,128]{1,0:T(8,128)} custom-call(f32[128,128]{1,0:T(8,128)} %select_add_fusion.5.a_ref), custom_call_target="tpu_custom_call" | custom-call | flops 12582912 | bytes 131072 | tf_op jit(solution)/shard_map/pallas_call | solution.py:127
  449.2 2.0 constant_dynamic-update-slice_fusion.6
  451.2 2.5 fusion.19
  455.6 15.0 %shard_map.42 = f32[128,128]{1,0:T(8,128)} custom-call(f32[128,128]{1,0:T(8,128)} %select_add_fusion.4.a_ref), custom_call_target="tpu_custom_call" | custom-call | flops 12582912 | bytes 131072 | tf_op jit(solution)/shard_map/pallas_call | solution.py:127
  470.6 2.0 constant_dynamic-update-slice_fusion.4
  472.6 2.0 fusion.20
  477.7 15.0 %shard_map.46 = f32[128,128]{1,0:T(8,128)} custom-call(f32[128,128]{1,0:T(8,128)} %select_add_fusion.a_ref), custom_call_target="tpu_custom_call" | custom-call | flops 12582912 | bytes 131072 | tf_op jit(solution)/shard_map/pallas_call | solution.py:127
  492.7 15.0 %shard_map.43 = f32[128,128]{1,0:T(8,128)} custom-call(f32[128,128]{1,0:T(8,128)} %select_add_fusion.3.a_ref), custom_call_target="tpu_custom_call" | custom-call | flops 12582912 | bytes 131072 | tf_op jit(solution)/shard_map/pallas_call | solution.py:127
  511.7 15.0 %shard_map.44 = f32[128,128]{1,0:T(8,128)} custom-call(f32[128,128]{1,0:T(8,128)} %select_add_fusion.2.a_ref), custom_call_target="tpu_custom_call" | custom-call | flops 12582912 | bytes 131072 | tf_op jit(solution)/shard_map/pallas_call | solution.py:127
  528.7 15.0 %shard_map.45 = f32[128,128]{1,0:T(8,128)} custom-call(f32[128,128]{1,0:T(8,128)} %select_add_fusion.1.a_ref), custom_call_target="tpu_custom_call" | custom-call | flops 12582912 | bytes 131072 | tf_op jit(solution)/shard_map/pallas_call | solution.py:127
  556.6 1.9 convolution_subtract_fusion.1
  558.8 2.1 convolution_subtract_fusion
  563.3 60.0 %all-gather.6.cloned.1.call-done = f32[9216,128]{1,0:T(8,128)} async-done(((f32[1152,128]{1,0:T(8,128)}), f32[9216,128]{1,0:T(8,128)}) %all-gather.6.cloned.1.call-update) | async-done | bytes 4718608 | tf_op jit(solution)/shard_map/all_gather | solution.py:214
  623.4 4.9 copy.69
  (106 shorter events, 47.1 us)
Async XLA Ops:
  7.8 11.6 %all-to-all-start = ((s32[8,1,4]{2,1,0:T(1,128)}), s32[8,1,4]{2,1,0:T(1,128)S(1)}, u32[]{:S(2)}, u32[]{:S(2)}) async-start(s32[8,1,4]{2,1,0:T(1,128)} %broadcast_in_dim.52), calls=%async_computation | async-start | bytes 8192 | tf_op jit(solution)/shard_map/all_to_all | solution.py:191
  19.4 99.2 %all-to-all-start.1 = ((bf16[8,512,512]{2,1,0:T(8,128)(2,1)}), bf16[8,512,512]{2,1,0:T(8,128)(2,1)}, u32[]{:S(2)}, u32[]{:S(2)}) async-start(bf16[8,512,512]{2,1,0:T(8,128)(2,1)} %gather_fusion), calls=%async_computation.1 | async-start | bytes 8388608 | tf_op jit(solution)/shard_map/all_to_all | solution.py:190
  24.5 179.4 %reduce-scatter.4.cloned.1.call-start = ((), (), s32[]{:S(2)}) async-start(), calls=%async_computation.5 | async-start | bytes 4587520 | tf_op jit(solution)/shard_map/reduce_scatter | solution.py:208
  158.3 71.0 %reduce-scatter.6.cloned.1.call-start = ((), (), s32[]{:S(2)}) async-start(), calls=%async_computation.6 | async-start | bytes 1146880 | tf_op jit(solution)/shard_map/reduce_scatter | solution.py:208
  203.9 53.2 %reduce-scatter.8.cloned.1.call-start = ((), (), s32[]{:S(2)}) async-start(), calls=%async_computation.7 | async-start | bytes 344064 | tf_op jit(solution)/shard_map/reduce_scatter | solution.py:208
  229.4 97.3 %all-gather.4.cloned.1.call-start = ((), (), s32[]{:S(2)}) async-start(), calls=%async_computation.8 | async-start | bytes 4587520 | tf_op jit(solution)/shard_map/all_gather | solution.py:211
  283.6 339.8 %all-gather.6.cloned.1.call-start = ((), (), s32[]{:S(2)}) async-start(), calls=%async_computation.9 | async-start | bytes 5308416 | tf_op jit(solution)/shard_map/all_gather | solution.py:214
  326.7 3.6 slice-start
  326.7 3.7 slice-start.1
  326.7 3.7 slice-start.2
  326.7 3.8 slice-start.3
  327.9 2.6 slice-start.4
  329.1 1.5 slice-start.5
  331.1 2.5 copy-start
  359.2 2.2 copy-start.1
  385.5 1.8 copy-start.2
  455.0 97.2 %copy-start.7 = (f32[128,128]{1,0:T(8,128)S(1)}, f32[128,128]{1,0:T(8,128)}, u32[]{:S(2)}) copy-start(f32[128,128]{1,0:T(8,128)} %shard_map.41) | copy-start | bytes 196612
  470.6 79.8 %copy-start.9 = (f32[128,128]{1,0:T(8,128)S(1)}, f32[128,128]{1,0:T(8,128)}, u32[]{:S(2)}) copy-start(f32[128,128]{1,0:T(8,128)} %shard_map.42) | copy-start | bytes 196612
  470.6 83.6 %copy-start.6 = (f32[128,128]{1,0:T(8,128)S(1)}, f32[128,128]{1,0:T(8,128)}, u32[]{:S(2)}) copy-start(f32[128,128]{1,0:T(8,128)} %shard_map.40) | copy-start | bytes 196612
  472.6 83.7 %copy-start.5 = (f32[128,128]{1,0:T(8,128)S(1)}, f32[128,128]{1,0:T(8,128)}, u32[]{:S(2)}) copy-start(f32[128,128]{1,0:T(8,128)} %shard_map.39) | copy-start | bytes 196612
  474.5 84.0 %copy-start.4 = (f32[128,128]{1,0:T(8,128)S(1)}, f32[128,128]{1,0:T(8,128)}, u32[]{:S(2)}) copy-start(f32[128,128]{1,0:T(8,128)} %shard_map.38) | copy-start | bytes 196612
  475.6 85.3 %copy-start.3 = (f32[128,128]{1,0:T(8,128)S(1)}, f32[128,128]{1,0:T(8,128)}, u32[]{:S(2)}) copy-start(f32[128,128]{1,0:T(8,128)} %shard_map.37) | copy-start | bytes 196612
  492.7 68.6 %copy-start.8 = (f32[128,128]{1,0:T(8,128)S(1)}, f32[128,128]{1,0:T(8,128)}, u32[]{:S(2)}) copy-start(f32[128,128]{1,0:T(8,128)} %shard_map.46) | copy-start | bytes 196612
Sparse Core Ops, SparseCore 0:
  158.5 45.3 reduce-scatter.3
  206.4 22.9 reduce-scatter.5
  231.9 25.1 reduce-scatter.7
  283.7 42.9 all-gather.3
  563.5 59.8 all-gather.5
